TPU v7x, 512 devices: a whole 4x8x8 slice. The times are simulated.
512 devices in a mesh: row: 32 (over z_hi, x, core), col: 16 (over z_lo, y).
Axes of the slice: x: 4, y: 8, z: 8 (z_hi: 4, z_lo: 2; z = z_hi * 2 + z_lo), core: 2. Of those that a mesh axis runs over, the one named last changes fastest.
Arguments:
- embeddings: float32 [16384, 768], P(('row', 'col')), may hold values from -0.21650635 to 0.21650635
- sharpness: float32 [16384], P(('row', 'col')), may hold values from 0.5 to 4
- soft_labels: float32 [16384, 256], P(('row', 'col')), may hold values from 0 to 1
- seed_mask: int32 [16384], P(('row', 'col')), may hold values 0 or 1
- tile_mask: int32 [512, 512], P('row'), may hold values from 0 to 1, as said below
Outputs:
- spread_labels: float32 [16384, 256], P(('row', 'col'))
Inputs may be any that keep to these rules, and one draw needn't show every extreme that they name: Every diagonal entry tile_mask[p, p] is 1.
All inputs are finite; a program needn't handle non-finite values. No bound on the sum of `seed_mask` on one device may be relied on, other than what follows from the above.
Results may differ from a plain program's by a relative error of at most 0.0003.
Values sent between devices are 32-bit elements; how exact they have to be, the bound alone decides.
No kernel may reach another device: no remote copies, remote signals or barrier semaphores. Data moves between devices by JAX's collectives and lax.ppermute only.
A program may use at most 64 MiB of HBM per device.

v0:
```python
import jax
import jax.numpy as jnp
from jax import lax
from jax.sharding import PartitionSpec as P

ITERS = 3


def kernel_tile(row_emb, row_squares, row_width, col_emb, col_width, col_mask):
    cross = jnp.dot(
        row_emb, col_emb.T, precision=lax.Precision.HIGHEST, preferred_element_type=jnp.float32
    )
    col_squares = jnp.sum(col_emb * col_emb, axis=1)
    distance = row_squares[:, None] + col_squares[None, :] - 2.0 * cross
    return jnp.exp(-(distance * row_width[:, None] * col_width[None, :])) * col_mask


def local(embeddings, sharpness, soft_labels, seed_mask, tile_mask):
    n_row = lax.axis_size("row")
    n_col = lax.axis_size("col")
    col_index = lax.axis_index("col")
    piece = embeddings.shape[0]
    seeded = seed_mask.astype(jnp.float32)[:, None] * soft_labels
    row_emb, row_width = (
        lax.all_gather(embeddings, "col", axis=0, tiled=True),
        lax.all_gather(sharpness, "col", axis=0, tiled=True),
    )
    row_squares = jnp.sum(row_emb * row_emb, axis=1)
    block_rows = row_emb.shape[0]
    col_rows = piece * n_row
    grouped = tile_mask.reshape(n_col, n_row, n_col)
    chosen = lax.dynamic_index_in_dim(grouped, col_index, axis=2, keepdims=False)
    col_mask = jnp.broadcast_to(chosen[:, None, :, None], (n_col, piece, n_row, piece))
    col_mask = col_mask.reshape(block_rows, col_rows).astype(jnp.float32)
    col_emb, col_width = (
        lax.all_gather(embeddings, "row", axis=0, tiled=True),
        lax.all_gather(sharpness, "row", axis=0, tiled=True),
    )
    labels = seeded
    for iteration in range(ITERS):
        col_labels = lax.all_gather(labels, "row", axis=0, tiled=True)
        weights = kernel_tile(row_emb, row_squares, row_width, col_emb, col_width, col_mask)
        partial_value = jnp.dot(
            weights, col_labels, precision=lax.Precision.HIGHEST, preferred_element_type=jnp.float32
        )
        degree = jnp.sum(weights, axis=1)
        total_part, total_degree = lax.psum((partial_value, degree), "col")
        own_part = lax.dynamic_slice_in_dim(total_part, col_index * piece, piece, 0)
        own_degree = lax.dynamic_slice_in_dim(total_degree, col_index * piece, piece, 0)
        labels = 0.9 * own_part / own_degree[:, None] + 0.1 * seeded
    return labels


def solution(mesh):
    return jax.shard_map(
        local,
        mesh=mesh,
        in_specs=(
            P(("row", "col"), None),
            P(("row", "col")),
            P(("row", "col"), None),
            P(("row", "col")),
            P("row", None),
        ),
        out_specs=P(("row", "col"), None),
        check_vma=False,
    )
```

profile of v0, /device:TPU:4, one launch (start us, length us, event | category | flops | bytes accessed | tf_op | source)
XLA Modules:
  0.0 762.3 jit_solution(18345925877665009551)
XLA Ops:
  6.5 0.0 all-gather.6.cloned.1.call-start
  6.5 0.7 all-gather.6.cloned.1.call-update
  7.3 0.0 all-gather.8.cloned.1.call-start
  7.3 0.7 all-gather.8.cloned.1.call-update
  8.0 0.0 all-gather.10.cloned.1.call-start
  8.1 0.7 convert_element_type.16
  8.7 1.4 broadcast_multiply_fusion
  10.2 0.0 all-gather.10.cloned.1.call-update
  10.2 0.0 all-reduce.6.cloned.1.call-start
  10.2 0.9 reshape.14
  11.1 0.3 convert_reduce_fusion
  11.4 4.4 broadcast_in_dim.2
  15.8 7.7 %convert_element_type.15 = f32[512,1024]{1,0:T(8,128)} reshape(f32[16,32,32,32]{3,2,1,0:T(8,128)} %broadcast_in_dim.2) | data formatting | bytes 4194304 | tf_op jit(solution)/shard_map/convert_element_type | solution.py:34
  23.5 1.3 dynamic-slice.1
  24.7 1.3 dynamic-slice
  27.4 0.2 dynamic-update-slice.1
  27.6 0.2 dynamic-update-slice
  27.8 35.9 %all-reduce = f32[512]{0:T(512)S(1)} all-reduce(f32[512]{0:T(512)S(1)} %dynamic-update-slice), channel_id=1, replica_groups=mesh['row'=32,'col'=16] {'col'}, use_global_device_ids=true, to_apply=%add | all-reduce | flops 512 | bytes 4096
  63.8 62.1 %all-reduce.1 = f32[1024]{0:T(1024)S(1)} all-reduce(f32[1024]{0:T(1024)S(1)} %dynamic-update-slice.1), channel_id=1, replica_groups=mesh['row'=32,'col'=16] {'row'}, use_global_device_ids=true, to_apply=%add.1 | all-reduce | flops 1024 | bytes 8192
  125.8 0.0 all-gather.6.cloned.1.call-done
  125.9 1.6 multiply_reduce_fusion.1
  127.4 22.1 %all-gather.8.cloned.1.call-done = f32[1024,768]{1,0:T(8,128)} async-done(((f32[32,768]{1,0:T(8,128)}), f32[1024,768]{1,0:T(8,128)}) %all-gather.8.cloned.1.call-update) | async-done | bytes 3145744 | tf_op jit(solution)/shard_map/all_gather | solution.py:36
  149.6 2.3 multiply_reduce_fusion
  151.9 0.5 copy-done
  152.4 7.7 %fusion = (f32[512]{0:T(512)S(1)}, f32[512,1024]{1,0:T(8,128)S(1)}) fusion(f32[512,1024]{1,0:T(8,128)} %convert_element_type.15, f32[1024]{0:T(1024)S(1)} %all-reduce.1, f32[512]{0:T(512)S(1)} %all-reduce, f32[512,768]{1,0:T(8,128)} %all-gather.6.cloned.1.call-done, f32[1024,768]{1,0:T(8,128)S(1)} %copy-done, f32[1024]{0:T(1024)S(1)} %multiply_reduce_fusion, ...), kind=kOutput, calls=%fused_computation.8 | convolution fusion | flops 4836032000 | bytes 8927232 | tf_op jit(solution)/shard_map/dot_general | solution.py:10
  160.1 47.0 %all-gather.10.cloned.1.call-done = f32[1024,256]{1,0:T(8,128)} async-done(((f32[32,256]{1,0:T(8,128)}), f32[1024,256]{1,0:T(8,128)}) %all-gather.10.cloned.1.call-update) | async-done | bytes 1048592 | tf_op jit(solution)/shard_map/all_gather | solution.py:41
  207.1 3.8 fusion.1
  211.0 0.0 all-reduce.6.cloned.1.call-update
  211.0 0.0 all-gather.12.cloned.1.call-start
  211.0 33.9 %psum.29 = f32[512]{0:T(512)S(1)} all-reduce(f32[512]{0:T(512)S(1)} %get-tuple-element.5), channel_id=1, replica_groups=mesh['row'=32,'col'=16] {'col'}, use_global_device_ids=true, to_apply=%region_4.5 | all-reduce | flops 512 | bytes 4096 | tf_op jit(solution)/shard_map/psum | solution.py:47
  245.0 0.1 dynamic_slice.20
  245.0 106.3 %all-reduce.6.cloned.1.call-done = f32[512,256]{1,0:T(8,128)} async-done(((f32[512,256]{1,0:T(8,128)}), f32[512,256]{1,0:T(8,128)}) %all-reduce.6.cloned.1.call-update) | async-done | bytes 524304 | tf_op jit(solution)/shard_map/psum | solution.py:47
  351.3 1.5 divide_add_fusion.2
  352.8 0.0 all-gather.12.cloned.1.call-update
  352.8 0.2 all-reduce.8.cloned.1.call-start
  353.0 55.4 %all-gather.12.cloned.1.call-done = f32[1024,256]{1,0:T(8,128)} async-done(((f32[32,256]{1,0:T(8,128)}), f32[1024,256]{1,0:T(8,128)}) %all-gather.12.cloned.1.call-update) | async-done | bytes 1048592 | tf_op jit(solution)/shard_map/all_gather | solution.py:41
  408.4 3.8 fusion.2
  412.3 0.0 all-reduce.8.cloned.1.call-update
  412.3 0.0 all-gather.14.cloned.1.call-start
  412.3 140.2 %all-reduce.8.cloned.1.call-done = f32[512,256]{1,0:T(8,128)} async-done(((f32[512,256]{1,0:T(8,128)}), f32[512,256]{1,0:T(8,128)}) %all-reduce.8.cloned.1.call-update) | async-done | bytes 524304 | tf_op jit(solution)/shard_map/psum | solution.py:47
  552.6 1.5 divide_add_fusion.1
  554.0 0.0 all-gather.14.cloned.1.call-update
  554.1 0.0 all-reduce.10.cloned.1.call-start
  554.1 55.7 %all-gather.14.cloned.1.call-done = f32[1024,256]{1,0:T(8,128)} async-done(((f32[32,256]{1,0:T(8,128)}), f32[1024,256]{1,0:T(8,128)}) %all-gather.14.cloned.1.call-update) | async-done | bytes 1048592 | tf_op jit(solution)/shard_map/all_gather | solution.py:41
  609.8 3.9 fusion.3
  613.7 0.0 all-reduce.10.cloned.1.call-update
  613.7 140.3 %all-reduce.10.cloned.1.call-done = f32[512,256]{1,0:T(8,128)} async-done(((f32[512,256]{1,0:T(8,128)}), f32[512,256]{1,0:T(8,128)}) %all-reduce.10.cloned.1.call-update) | async-done | bytes 524304 | tf_op jit(solution)/shard_map/psum | solution.py:47
  754.0 1.5 divide_add_fusion
  (7 shorter events, 0.0 us)
Async XLA Ops:
  6.5 119.3 %all-gather.6.cloned.1.call-start = ((), (), s32[]{:S(2)}) async-start(), calls=%async_computation | async-start | bytes 1671168 | tf_op jit(solution)/shard_map/all_gather | solution.py:25
  7.3 142.3 %all-gather.8.cloned.1.call-start = ((), (), s32[]{:S(2)}) async-start(), calls=%async_computation.1 | async-start | bytes 3244032 | tf_op jit(solution)/shard_map/all_gather | solution.py:36
  8.0 199.1 %all-gather.10.cloned.1.call-start = ((), (), s32[]{:S(2)}) async-start(), calls=%async_computation.2 | async-start | bytes 1081344 | tf_op jit(solution)/shard_map/all_gather | solution.py:41
  10.2 341.1 %all-reduce.6.cloned.1.call-start = ((), (), s32[]{:S(2)}) async-start(), calls=%async_computation.3 | async-start | bytes 1048576 | tf_op jit(solution)/shard_map/psum | solution.py:47
  15.8 11.6 %copy-start.2 = (f32[32]{0:T(128)S(1)}, f32[32]{0:T(128)}, u32[]{:S(2)}) copy-start(f32[32]{0:T(128)} %param.6) | copy-start | bytes 388
  149.6 2.8 copy-start
  207.1 144.2 %copy-start.1 = (f32[32,256]{1,0:T(8,128)S(1)}, f32[32,256]{1,0:T(8,128)}, u32[]{:S(2)}) copy-start(f32[32,256]{1,0:T(8,128)} %param.7) | copy-start | bytes 98308
  211.0 197.4 %all-gather.12.cloned.1.call-start = ((), (), s32[]{:S(2)}) async-start(), calls=%async_computation.4 | async-start | bytes 1081344 | tf_op jit(solution)/shard_map/all_gather | solution.py:41
  352.8 199.8 %all-reduce.8.cloned.1.call-start = ((), (), s32[]{:S(2)}) async-start(), calls=%async_computation.5 | async-start | bytes 1048576 | tf_op jit(solution)/shard_map/psum | solution.py:47
  412.3 197.5 %all-gather.14.cloned.1.call-start = ((), (), s32[]{:S(2)}) async-start(), calls=%async_computation.6 | async-start | bytes 1081344 | tf_op jit(solution)/shard_map/all_gather | solution.py:41
  554.1 199.9 %all-reduce.10.cloned.1.call-start = ((), (), s32[]{:S(2)}) async-start(), calls=%async_computation.7 | async-start | bytes 1048576 | tf_op jit(solution)/shard_map/psum | solution.py:47
Sparse Core Ops, SparseCore 0:
  9.4 77.2 all-gather.5
  89.8 59.7 all-gather.7
  152.7 54.3 all-gather.9
  211.1 140.1 all-reduce.5
  354.3 54.0 all-gather.11
  412.4 140.1 all-reduce.7
  555.7 54.0 all-gather.13
  613.8 140.1 all-reduce.9
where the time goes:
time: 763 us; the launch traced here: 762 us
  waiting for transfers between devices  569 us (75%)
  blocking collectives  132 us (17%)
  matrix products  19.2 us (3%)
  local copies, waits for them, and re-layouts  16.6 us (2%)
  between operations  14.8 us (2%)
  other arithmetic  10.6 us (1%)
    psum x3, waiting for transfers between devices, local(): total_part, total_degree = lax.psum((partial_value, degree), 'col')  387 us
    all_gather x3, waiting for transfers between devices, local(): col_labels = lax.all_gather(labels, 'row', axis=0, tiled=True)  158 us
    unnamed x2, blocking collectives  98 us
    psum x1, blocking collectives, local(): total_part, total_degree = lax.psum((partial_value, degree), 'col')  33.9 us
    all_gather x1, waiting for transfers between devices, local(): lax.all_gather(embeddings, 'row', axis=0, tiled=True)  22.1 us
  transfers between devices with their start and end apart: 8, of which 7 were waited for; matrix products, arithmetic and copies ran while one was open for 4% of the time, Pallas kernels for 0%

commit v1 on v0

v1 whole, which is shorter than its diff:
```python
import jax
import jax.numpy as jnp
from jax import lax
from jax.sharding import PartitionSpec as P

ITERS = 3


def gather_rows(x, axis, n):
    copies = jnp.broadcast_to(x[None], (n,) + x.shape)
    got = lax.all_to_all(copies, axis, 0, 0, tiled=False)
    return got.reshape((n * x.shape[0],) + x.shape[1:])


def scatter_sum(p, axis, n):
    chunk = p.shape[0] // n
    got = lax.all_to_all(p.reshape((n, chunk) + p.shape[1:]), axis, 0, 0, tiled=False)
    return jnp.sum(got, axis=0)


def local(embeddings, sharpness, soft_labels, seed_mask, tile_mask):
    n_row = lax.axis_size("row")
    n_col = lax.axis_size("col")
    col_index = lax.axis_index("col")
    piece, width = embeddings.shape
    n_labels = soft_labels.shape[1]
    seeded = seed_mask.astype(jnp.float32)[:, None] * soft_labels
    squares = jnp.sum(embeddings * embeddings, axis=1)
    packed = jnp.concatenate([embeddings, sharpness[:, None], squares[:, None]], axis=1)
    row_pack = gather_rows(packed, "col", n_col)
    col_pack = gather_rows(jnp.concatenate([packed, seeded], axis=1), "row", n_row)
    row_emb, row_width, row_squares = row_pack[:, :width], row_pack[:, width], row_pack[:, width + 1]
    col_emb, col_width, col_squares = col_pack[:, :width], col_pack[:, width], col_pack[:, width + 1]
    col_labels = col_pack[:, width + 2:]
    block_rows = row_emb.shape[0]
    col_rows = piece * n_row
    grouped = tile_mask.reshape(n_col, n_row, n_col)
    chosen = lax.dynamic_index_in_dim(grouped, col_index, axis=2, keepdims=False)
    col_mask = jnp.broadcast_to(chosen[:, None, :, None], (n_col, piece, n_row, piece))
    col_mask = col_mask.reshape(block_rows, col_rows).astype(jnp.float32)
    cross = jnp.dot(row_emb, col_emb.T, precision=lax.Precision.HIGHEST, preferred_element_type=jnp.float32)
    distance = row_squares[:, None] + col_squares[None, :] - 2.0 * cross
    weights = jnp.exp(-(distance * row_width[:, None] * col_width[None, :])) * col_mask
    degree = None
    labels = seeded
    for iteration in range(ITERS):
        if iteration > 0:
            col_labels = gather_rows(labels, "row", n_row)
        partial_value = jnp.dot(
            weights, col_labels, precision=lax.Precision.HIGHEST, preferred_element_type=jnp.float32
        )
        if degree is None:
            both = jnp.concatenate([partial_value, jnp.sum(weights, axis=1)[:, None]], axis=1)
            both = scatter_sum(both, "col", n_col)
            own_part, degree = both[:, :n_labels], both[:, n_labels]
        else:
            own_part = scatter_sum(partial_value, "col", n_col)
        labels = 0.9 * own_part / degree[:, None] + 0.1 * seeded
    return labels


def solution(mesh):
    return jax.shard_map(
        local,
        mesh=mesh,
        in_specs=(
            P(("row", "col"), None),
            P(("row", "col")),
            P(("row", "col"), None),
            P(("row", "col")),
            P("row", None),
        ),
        out_specs=P(("row", "col"), None),
        check_vma=False,
    )
```

time: 763 us -> 337 us (0.44)
  the two profiles are of different devices: /device:TPU:4 before, /device:TPU:8 now
where the time goes in v1:
time: 337 us; the launch traced here: 336 us
  waiting for transfers between devices  138 us (41%)
  blocking collectives  136 us (40%)
  starting transfers between devices  22 us (7%)
  local copies, waits for them, and re-layouts  19.9 us (6%)
  matrix products  17 us (5%)
    all_to_all x2, waiting for transfers between devices, gather_rows(): got = lax.all_to_all(copies, axis, 0, 0, tiled=False)  138 us
    all_to_all x3, blocking collectives, scatter_sum(): lax.all_to_all(p.reshape((n, chunk) + p.shape[1:]), axis, 0, 0, tiled=False)  73.8 us
    all_to_all x2, blocking collectives, gather_rows(): got = lax.all_to_all(copies, axis, 0, 0, tiled=False)  62 us
    all_to_all x2, starting transfers between devices, gather_rows(): got = lax.all_to_all(copies, axis, 0, 0, tiled=False)  22 us
    dot_general x1, matrix products, local(): jnp.dot(row_emb, col_emb.T, precision=lax.Precision.HIGHEST, preferred_el...  10.1 us
    convert_element_type x1, local copies, waits for them, and re-layouts, local(): col_mask = col_mask.reshape(block_rows, col_rows).astype(jnp.float32)  7.7 us
    dot_general x3, matrix products, local(): jnp.dot(weights, col_labels, precision=lax.Precision.HIGHEST, preferred_e...  6.95 us
  transfers between devices with their start and end apart: 2, of which 2 were waited for; matrix products, arithmetic and copies ran while one was open for 4% of the time, Pallas kernels for 0%

profile of v1, /device:TPU:8, one launch (start us, length us, event | category | flops | bytes accessed | tf_op | source)
XLA Modules:
  0.0 336.0 jit_solution(13849672691605903603)
XLA Ops:
  0.0 0.7 copy.17
  0.7 1.0 multiply_reduce_fusion
  1.7 0.1 copy.18
  1.8 1.0 pad_maximum_fusion.1
  2.8 1.4 broadcast_in_dim.16
  4.3 0.0 copy-start.4
  4.3 0.0 copy-start.2
  4.3 0.0 copy-start.1
  4.3 9.5 %all-to-all-start = ((f32[16,32,770]{2,1,0:T(8,128)}), f32[16,32,770]{2,1,0:T(8,128)S(1)}, u32[]{:S(2)}, u32[]{:S(2)}) async-start(f32[16,32,770]{2,1,0:T(8,128)} %broadcast_in_dim.16), calls=%async_computation | async-start | bytes 3670016 | tf_op jit(solution)/shard_map/all_to_all | solution.py:11
  13.8 0.0 copy-done.4
  13.8 0.0 copy-done.2
  13.8 0.1 broadcast_multiply_fusion
  13.9 0.0 copy-done.1
  13.9 0.1 concatenate.16
  14.0 43.0 %all-to-all-done = f32[16,32,770]{2,1,0:T(8,128)S(1)} async-done(((f32[16,32,770]{2,1,0:T(8,128)}), f32[16,32,770]{2,1,0:T(8,128)S(1)}, u32[]{:S(2)}, u32[]{:S(2)}) %all-to-all-start) | async-done | bytes 1576992 | tf_op jit(solution)/shard_map/all_to_all | solution.py:11
  57.0 0.0 copy-start
  57.0 2.6 broadcast_in_dim.17
  59.6 0.0 copy-start.3
  59.6 12.5 %all-to-all-start.1 = ((f32[32,32,1026]{2,1,0:T(8,128)}), f32[32,32,1026]{2,1,0:T(8,128)}, u32[]{:S(2)}, u32[]{:S(2)}) async-start(f32[32,32,1026]{2,1,0:T(8,128)} %broadcast_in_dim.17), calls=%async_computation.1 | async-start | bytes 9437184 | tf_op jit(solution)/shard_map/all_to_all | solution.py:11
  72.1 0.0 copy-done.3
  72.1 0.1 reshape.37
  72.3 0.3 convert_reduce_fusion
  72.5 4.4 %broadcast_in_dim.18 = f32[16,32,32,32]{3,2,1,0:T(8,128)} broadcast(f32[16,32]{1,0:T(8,128)S(1)} %convert_reduce_fusion), dimensions={0,2} | broadcast | bytes 2099200 | tf_op jit(solution)/shard_map/broadcast_in_dim | solution.py:39
  76.9 7.7 %convert_element_type.16 = f32[512,1024]{1,0:T(8,128)} reshape(f32[16,32,32,32]{3,2,1,0:T(8,128)} %broadcast_in_dim.18) | data formatting | bytes 4194304 | tf_op jit(solution)/shard_map/convert_element_type | solution.py:40
  84.6 0.0 copy-done
  84.6 0.3 slice_reduce_fusion.3
  84.9 94.8 %all-to-all-done.1 = f32[32,32,1026]{2,1,0:T(8,128)} async-done(((f32[32,32,1026]{2,1,0:T(8,128)}), f32[32,32,1026]{2,1,0:T(8,128)}, u32[]{:S(2)}, u32[]{:S(2)}) %all-to-all-start.1) | async-done | bytes 4202528 | tf_op jit(solution)/shard_map/all_to_all | solution.py:11
  179.7 1.8 slice_reduce_fusion.1
  181.6 10.1 %fusion.9 = (f32[512]{0:T(512)S(1)}, f32[512,1024]{1,0:T(8,128)S(1)}) fusion(f32[512,1024]{1,0:T(8,128)} %convert_element_type.16, f32[1024]{0:T(1024)S(1)} %get-tuple-element.6, f32[512]{0:T(512)S(1)} %get-tuple-element.8, f32[1024,1026]{1,0:T(8,128)} %bitcast.3, f32[512,770]{1,0:T(8,128)} %bitcast.22, f32[1024]{0:T(1024)S(1)} %get-tuple-element.5, ...), kind=kOutput, calls=%fused_computation.21 | convolution fusion | flops 4836032000 | bytes 8927232 | tf_op jit(solution)/shard_map/dot_general | solution.py:41
  191.7 0.2 concatenate.20
  191.9 3.3 fusion.5
  195.2 0.1 pad_maximum_fusion
  195.3 26.7 %all_to_all.35 = f32[16,32,257]{2,1,0:T(8,128)S(1)} all-to-all(f32[16,32,257]{2,1,0:T(8,128)S(1)} %pad_maximum_fusion), channel_id=1, replica_groups=mesh['row'=32,'col'=16] {'col'}, dimensions={0} | all-to-all | bytes 1052672 | tf_op jit(solution)/shard_map/all_to_all | solution.py:17
  222.1 0.1 slice_reduce_fusion.4
  222.2 0.1 fusion.8
  222.3 0.1 broadcast_in_dim.19
  222.4 32.9 %all_to_all.36 = f32[32,32,256]{2,1,0:T(8,128)S(1)} all-to-all(f32[32,32,256]{2,1,0:T(8,128)S(1)} %broadcast_in_dim.19), channel_id=1, replica_groups=mesh['row'=32,'col'=16] {'row'}, dimensions={0} | all-to-all | bytes 2097152 | tf_op jit(solution)/shard_map/all_to_all | solution.py:11
  255.3 1.8 fusion.10
  257.1 22.2 %all_to_all.37 = f32[16,32,256]{2,1,0:T(8,128)S(1)} all-to-all(f32[16,32,256]{2,1,0:T(8,128)S(1)} %fusion.10), channel_id=1, replica_groups=mesh['row'=32,'col'=16] {'col'}, dimensions={0} | all-to-all | bytes 1048576 | tf_op jit(solution)/shard_map/all_to_all | solution.py:17
  279.4 0.1 divide_add_fusion.1
  279.4 0.1 broadcast_in_dim.20
  279.6 29.1 %all_to_all.38 = f32[32,32,256]{2,1,0:T(8,128)S(1)} all-to-all(f32[32,32,256]{2,1,0:T(8,128)S(1)} %broadcast_in_dim.20), channel_id=1, replica_groups=mesh['row'=32,'col'=16] {'row'}, dimensions={0} | all-to-all | bytes 2097152 | tf_op jit(solution)/shard_map/all_to_all | solution.py:11
  308.6 1.8 fusion.11
  310.4 24.9 %all_to_all.39 = f32[16,32,256]{2,1,0:T(8,128)S(1)} all-to-all(f32[16,32,256]{2,1,0:T(8,128)S(1)} %fusion.11), channel_id=1, replica_groups=mesh['row'=32,'col'=16] {'col'}, dimensions={0} | all-to-all | bytes 1048576 | tf_op jit(solution)/shard_map/all_to_all | solution.py:17
  335.3 0.7 divide_add_fusion
  (4 shorter events, 0.1 us)
Async XLA Ops:
  4.3 9.5 %copy-start.4 = (s32[32]{0:T(128)S(1)}, s32[32]{0:T(128)}, u32[]{:S(2)}) copy-start(s32[32]{0:T(128)} %param.8) | copy-start | bytes 388
  4.3 9.5 %copy-start.2 = (f32[32,256]{1,0:T(8,128)S(1)}, f32[32,256]{1,0:T(8,128)}, u32[]{:S(2)}) copy-start(f32[32,256]{1,0:T(8,128)} %param.7) | copy-start | bytes 98308
  4.3 9.6 %copy-start.1 = (f32[32,768]{1,0:T(8,128)S(1)}, f32[32,768]{1,0:T(8,128)}, u32[]{:S(2)}) copy-start(f32[32,768]{1,0:T(8,128)} %param.5) | copy-start | bytes 294916
  4.3 52.7 %all-to-all-start = ((f32[16,32,770]{2,1,0:T(8,128)}), f32[16,32,770]{2,1,0:T(8,128)S(1)}, u32[]{:S(2)}, u32[]{:S(2)}) async-start(f32[16,32,770]{2,1,0:T(8,128)} %broadcast_in_dim.16), calls=%async_computation | async-start | bytes 3670016 | tf_op jit(solution)/shard_map/all_to_all | solution.py:11
  57.0 27.6 %copy-start = (f32[16,32,770]{2,1,0:T(8,128)}, f32[16,32,770]{2,1,0:T(8,128)S(1)}, u32[]{:S(2)}) copy-start(f32[16,32,770]{2,1,0:T(8,128)S(1)} %all-to-all-done) | copy-start | bytes 4730884
  59.6 12.5 %copy-start.3 = (s32[16,512]{1,0:T(8,128)S(1)}, s32[16,512]{1,0:T(8,128)}, u32[]{:S(2)}) copy-start(s32[16,512]{1,0:T(8,128)} %param.9) | copy-start | bytes 98308
  59.6 120.1 %all-to-all-start.1 = ((f32[32,32,1026]{2,1,0:T(8,128)}), f32[32,32,1026]{2,1,0:T(8,128)}, u32[]{:S(2)}, u32[]{:S(2)}) async-start(f32[32,32,1026]{2,1,0:T(8,128)} %broadcast_in_dim.17), calls=%async_computation.1 | async-start | bytes 9437184 | tf_op jit(solution)/shard_map/all_to_all | solution.py:11

commit v2 on v1

v2 whole, which is shorter than its diff:
```python
import jax
import jax.numpy as jnp
from jax import lax
from jax.sharding import Mesh
from jax.sharding import PartitionSpec as P

ITERS = 3
CHIPS = ("zh", "x")
DOCS = ("zh", "x", "core", "col")


def gather_rows(x, axis, n):
    copies = jnp.broadcast_to(x[None], (n,) + x.shape)
    got = lax.all_to_all(copies, axis, 0, 0, tiled=False)
    return got.reshape((n * x.shape[0],) + x.shape[1:])


def gather_row_set(x, n_chips):
    mine = gather_rows(x, CHIPS, n_chips)
    other = lax.ppermute(mine, "core", [(0, 1), (1, 0)])
    return jnp.concatenate([mine, other], axis=0)


def scatter_sum(p, axis, n):
    chunk = p.shape[0] // n
    got = lax.all_to_all(p.reshape((n, chunk) + p.shape[1:]), axis, 0, 0, tiled=False)
    return jnp.sum(got, axis=0)


def local(embeddings, sharpness, soft_labels, seed_mask, tile_mask):
    n_chips = lax.axis_size(CHIPS)
    n_col = lax.axis_size("col")
    col_index = lax.axis_index("col")
    core = lax.axis_index("core")
    piece, width = embeddings.shape
    n_labels = soft_labels.shape[1]
    seeded = seed_mask.astype(jnp.float32)[:, None] * soft_labels
    squares = jnp.sum(embeddings * embeddings, axis=1)
    packed = jnp.concatenate([embeddings, sharpness[:, None], squares[:, None]], axis=1)
    row_pack = gather_rows(packed, "col", n_col)
    col_pack = gather_row_set(jnp.concatenate([packed, seeded], axis=1), n_chips)
    row_emb, row_width, row_squares = row_pack[:, :width], row_pack[:, width], row_pack[:, width + 1]
    col_emb, col_width, col_squares = col_pack[:, :width], col_pack[:, width], col_pack[:, width + 1]
    col_labels = col_pack[:, width + 2:]
    block_rows = row_emb.shape[0]
    col_rows = col_emb.shape[0]
    grouped = tile_mask.reshape(n_col, n_chips, 2, n_col)
    chosen = lax.dynamic_index_in_dim(grouped, col_index, axis=3, keepdims=False)
    own_half = lax.dynamic_index_in_dim(chosen, core, axis=2, keepdims=False)
    other_half = lax.dynamic_index_in_dim(chosen, 1 - core, axis=2, keepdims=False)
    chosen = jnp.concatenate([own_half, other_half], axis=1)
    col_mask = jnp.broadcast_to(chosen[:, None, :, None], (n_col, piece, 2 * n_chips, piece))
    col_mask = col_mask.reshape(block_rows, col_rows).astype(jnp.float32)
    cross = jnp.dot(row_emb, col_emb.T, precision=lax.Precision.HIGHEST, preferred_element_type=jnp.float32)
    distance = row_squares[:, None] + col_squares[None, :] - 2.0 * cross
    weights = jnp.exp(-(distance * row_width[:, None] * col_width[None, :])) * col_mask
    degree = None
    labels = seeded
    for iteration in range(ITERS):
        if iteration > 0:
            col_labels = gather_row_set(labels, n_chips)
        partial_value = jnp.dot(
            weights, col_labels, precision=lax.Precision.HIGHEST, preferred_element_type=jnp.float32
        )
        if degree is None:
            both = jnp.concatenate([partial_value, jnp.sum(weights, axis=1)[:, None]], axis=1)
            both = scatter_sum(both, "col", n_col)
            own_part, degree = both[:, :n_labels], both[:, n_labels]
        else:
            own_part = scatter_sum(partial_value, "col", n_col)
        labels = 0.9 * own_part / degree[:, None] + 0.1 * seeded
    return labels


def solution(mesh):
    n_row, n_col = mesh.devices.shape
    fine = Mesh(mesh.devices.reshape(n_row // 8, 4, 2, n_col), DOCS)
    return jax.shard_map(
        local,
        mesh=fine,
        in_specs=(
            P(DOCS, None),
            P(DOCS),
            P(DOCS, None),
            P(DOCS),
            P(("zh", "x", "core"), None),
        ),
        out_specs=P(DOCS, None),
        check_vma=False,
    )
```

time: 337 us -> 274 us (0.81)
  waiting for transfers between devices: 138 us -> 65.4 us
  blocking collectives: 136 us -> 111 us
  starting transfers between devices: 22 us -> 43.4 us
  local copies, waits for them, and re-layouts: 19.9 us -> 34.9 us
  matrix products: 17 us -> 12.7 us
    all_to_all x2, waiting for transfers between devices: 138 us -> 61.8 us  [gather_rows(): got = lax.all_to_all(copies, axis, 0, 0, tiled=False)]
    all_to_all x2, blocking collectives: 62 us -> 35.6 us  [gather_rows(): got = lax.all_to_all(copies, axis, 0, 0, tiled=False)]
    all_to_all x2, starting transfers between devices: 22 us -> 37.5 us  [gather_rows(): got = lax.all_to_all(copies, axis, 0, 0, tiled=False)]
    dynamic_slice x0 -> x1, local copies, waits for them, and re-layouts: none -> 10.1 us  [local(): own_half = lax.dynamic_index_in_dim(chosen, core, axis=2, keepdims=False)]
    ppermute x0 -> x3, starting transfers between devices: none -> 5.95 us  [gather_row_set(): other = lax.ppermute(mine, 'core', [(0, 1), (1, 0)])]
    ppermute x0 -> x3, waiting for transfers between devices: none -> 3.53 us  [gather_row_set(): other = lax.ppermute(mine, 'core', [(0, 1), (1, 0)])]
  transfers between devices with their start and end apart: 2 -> 5, of which waited for: 2 -> 4; matrix products, arithmetic and copies ran while one was open for 4% -> 10% of each run, Pallas kernels for 0% -> 0%
where the time goes in v2:
time: 274 us; the launch traced here: 273 us
  blocking collectives  111 us (41%)
  waiting for transfers between devices  65.4 us (24%)
  starting transfers between devices  43.4 us (16%)
  local copies, waits for them, and re-layouts  34.9 us (13%)
  matrix products  12.7 us (5%)
  other arithmetic  5.36 us (2%)
    all_to_all x3, blocking collectives, scatter_sum(): lax.all_to_all(p.reshape((n, chunk) + p.shape[1:]), axis, 0, 0, tiled=False)  75.3 us
    all_to_all x2, waiting for transfers between devices, gather_rows(): got = lax.all_to_all(copies, axis, 0, 0, tiled=False)  61.8 us
    all_to_all x2, starting transfers between devices, gather_rows(): got = lax.all_to_all(copies, axis, 0, 0, tiled=False)  37.5 us
    all_to_all x2, blocking collectives, gather_rows(): got = lax.all_to_all(copies, axis, 0, 0, tiled=False)  35.6 us
    dynamic_slice x1, local copies, waits for them, and re-layouts, local(): own_half = lax.dynamic_index_in_dim(chosen, core, axis=2, keepdims=False)  10.1 us
    convert_element_type x1, local copies, waits for them, and re-layouts, local(): col_mask = col_mask.reshape(block_rows, col_rows).astype(jnp.float32)  7.7 us
    dot_general x1, matrix products, local(): jnp.dot(row_emb, col_emb.T, precision=lax.Precision.HIGHEST, preferred_el...  7.14 us
    ppermute x3, starting transfers between devices, gather_row_set(): other = lax.ppermute(mine, 'core', [(0, 1), (1, 0)])  5.95 us
  transfers between devices with their start and end apart: 5, of which 4 were waited for; matrix products, arithmetic and copies ran while one was open for 10% of the time, Pallas kernels for 0%

profile of v2, /device:TPU:8, one launch (start us, length us, event | category | flops | bytes accessed | tf_op | source)
XLA Modules:
  0.0 272.9 jit_solution(16627055772259063951)
XLA Ops:
  0.0 0.7 convert_element_type.10
  0.7 1.0 multiply_reduce_fusion
  1.7 0.1 copy.23
  1.8 0.7 copy.22
  2.5 0.8 broadcast_multiply_fusion
  3.3 1.0 concatenate.28
  4.3 1.6 broadcast_in_dim.17
  6.0 13.0 %all-to-all-start.1 = ((f32[16,32,1026]{2,1,0:T(8,128)}), f32[16,32,1026]{2,1,0:T(8,128)S(1)}, u32[]{:S(2)}, u32[]{:S(2)}) async-start(f32[16,32,1026]{2,1,0:T(8,128)} %broadcast_in_dim.17), calls=%async_computation.1 | async-start | bytes 4718592 | tf_op jit(solution)/shard_map/all_to_all | solution.py:14
  19.0 0.1 pad_maximum_fusion.3
  19.1 45.3 %all-to-all-done.1 = f32[16,32,1026]{2,1,0:T(8,128)S(1)} async-done(((f32[16,32,1026]{2,1,0:T(8,128)}), f32[16,32,1026]{2,1,0:T(8,128)S(1)}, u32[]{:S(2)}, u32[]{:S(2)}) %all-to-all-start.1) | async-done | bytes 2101280 | tf_op jit(solution)/shard_map/all_to_all | solution.py:14
  64.4 1.4 broadcast_in_dim.16
  65.8 24.5 %all-to-all-start = ((f32[16,32,770]{2,1,0:T(8,128)}), f32[16,32,770]{2,1,0:T(8,128)}, u32[]{:S(2)}, u32[]{:S(2)}) async-start(f32[16,32,770]{2,1,0:T(8,128)} %broadcast_in_dim.16), calls=%async_computation | async-start | bytes 3670016 | tf_op jit(solution)/shard_map/all_to_all | solution.py:14
  90.3 1.9 copy.26
  92.1 1.9 collective-permute-start
  94.1 0.4 reshape.41
  94.5 10.1 %dynamic-slice_reduce_fusion.1 = (s32[16,16]{1,0:T(8,128)S(1)}, s32[16,16]{1,0:T(8,128)S(1)}) fusion(s32[16,16,2,16]{3,2,1,0:T(2,128)S(1)} %reshape.41, s32[]{:T(128)S(6)} %select_n.18, s32[]{:T(128)S(6)} %select_n.20, s32[]{:T(128)S(6)} %select_n.22), kind=kLoop, calls=%fused_computation.26 | loop fusion | bytes 4108 | tf_op jit(solution)/shard_map/jit(dynamic_index_in_dim)/dynamic_slice | solution.py:49
  104.6 0.1 add_convert_fusion
  104.7 4.4 %broadcast_in_dim.18 = f32[16,32,32,32]{3,2,1,0:T(8,128)} broadcast(f32[16,32]{1,0:T(8,128)S(1)} %add_convert_fusion), dimensions={0,2} | broadcast | bytes 2099200 | tf_op jit(solution)/shard_map/broadcast_in_dim | solution.py:52
  109.0 7.7 %convert_element_type.12 = f32[512,1024]{1,0:T(8,128)} reshape(f32[16,32,32,32]{3,2,1,0:T(8,128)} %broadcast_in_dim.18) | data formatting | bytes 4194304 | tf_op jit(solution)/shard_map/convert_element_type | solution.py:53
  116.7 16.5 %all-to-all-done = f32[16,32,770]{2,1,0:T(8,128)} async-done(((f32[16,32,770]{2,1,0:T(8,128)}), f32[16,32,770]{2,1,0:T(8,128)}, u32[]{:S(2)}, u32[]{:S(2)}) %all-to-all-start) | async-done | bytes 1576992 | tf_op jit(solution)/shard_map/all_to_all | solution.py:14
  133.2 1.4 slice_reduce_fusion.1
  134.6 0.0 collective-permute-done
  134.6 3.0 %copy.27 = f32[512,1026]{1,0:T(8,128)} copy(f32[512,1026]{0,1:T(8,128)} %collective-permute-done) | data formatting | bytes 4202496 | tf_op jit(solution)/shard_map/ppermute | solution.py:20
  137.7 1.7 maximum_reduce_fusion
  139.4 0.1 copy-done
  139.5 0.6 copy-done.3
  140.1 7.1 %fusion.26 = (f32[512]{0:T(512)S(1)}, f32[512,1024]{1,0:T(8,128)S(1)}) fusion(f32[512,1024]{1,0:T(8,128)S(1)} %copy-done.3, f32[1024]{0:T(1024)S(1)} %get-tuple-element.6, f32[512]{0:T(512)S(1)} %get-tuple-element.8, f32[512,1026]{1,0:T(8,128)S(1)} %bitcast.16, f32[512,1026]{1,0:T(8,128)S(1)} %copy-done, f32[512,770]{1,0:T(8,128)} %bitcast.2, ...), kind=kOutput, calls=%fused_computation.41 | convolution fusion | flops 4836818432 | bytes 9984000 | tf_op jit(solution)/shard_map/dot_general | solution.py:54
  147.3 1.9 fusion.4
  149.2 0.0 copy-start.5
  149.3 0.2 concatenate.36
  149.5 0.1 pad_maximum_fusion.2
  149.5 0.0 copy-start.2
  149.5 27.4 %all_to_all.35 = f32[16,32,257]{2,1,0:T(8,128)S(1)} all-to-all(f32[16,32,257]{2,1,0:T(8,128)S(1)} %pad_maximum_fusion.2), channel_id=1, replica_groups=mesh['zh'=4,'x'=4,'core'=2,'col'=16] {'col'}, dimensions={0} | all-to-all | bytes 1052672 | tf_op jit(solution)/shard_map/all_to_all | solution.py:26
  177.0 0.1 slice_reduce_fusion.2
  177.1 0.0 copy-done.5
  177.1 0.1 fusion.17
  177.3 17.7 %all_to_all.36 = f32[16,32,256]{2,1,0:T(8,128)S(1)} all-to-all(f32[16,32,256]{2,1,0:T(8,128)S(1)} %broadcast_in_dim.19), channel_id=1, replica_groups=mesh['zh'=4,'x'=4,'core'=2,'col'=16] {'zh','x'}, dimensions={0} | all-to-all | bytes 1048576 | tf_op jit(solution)/shard_map/all_to_all | solution.py:14
  195.0 2.1 collective-permute-start.1
  197.1 1.7 collective-permute-done.1
  198.8 1.8 fusion.6
  200.6 23.5 %all_to_all.37 = f32[16,32,256]{2,1,0:T(8,128)S(1)} all-to-all(f32[16,32,256]{2,1,0:T(8,128)S(1)} %bitcast.24), channel_id=1, replica_groups=mesh['zh'=4,'x'=4,'core'=2,'col'=16] {'col'}, dimensions={0} | all-to-all | bytes 1048576 | tf_op jit(solution)/shard_map/all_to_all | solution.py:26
  224.2 0.1 divide_add_fusion.1
  224.3 17.9 %all_to_all.38 = f32[16,32,256]{2,1,0:T(8,128)S(1)} all-to-all(f32[16,32,256]{2,1,0:T(8,128)S(1)} %broadcast_in_dim.20), channel_id=1, replica_groups=mesh['zh'=4,'x'=4,'core'=2,'col'=16] {'zh','x'}, dimensions={0} | all-to-all | bytes 1048576 | tf_op jit(solution)/shard_map/all_to_all | solution.py:14
  242.2 1.9 collective-permute-start.2
  244.1 1.9 collective-permute-done.2
  246.0 1.8 fusion.10
  247.8 24.3 %all_to_all.39 = f32[16,32,256]{2,1,0:T(8,128)S(1)} all-to-all(f32[16,32,256]{2,1,0:T(8,128)S(1)} %bitcast.23), channel_id=1, replica_groups=mesh['zh'=4,'x'=4,'core'=2,'col'=16] {'col'}, dimensions={0} | all-to-all | bytes 1048576 | tf_op jit(solution)/shard_map/all_to_all | solution.py:26
  272.2 0.7 divide_add_fusion
  (14 shorter events, 0.2 us)
Async XLA Ops:
  6.0 13.0 %copy-start.4 = (f32[32,768]{1,0:T(8,128)S(1)}, f32[32,768]{1,0:T(8,128)}, u32[]{:S(2)}) copy-start(f32[32,768]{1,0:T(8,128)} %param.5) | copy-start | bytes 294916
  6.0 58.4 %all-to-all-start.1 = ((f32[16,32,1026]{2,1,0:T(8,128)}), f32[16,32,1026]{2,1,0:T(8,128)S(1)}, u32[]{:S(2)}, u32[]{:S(2)}) async-start(f32[16,32,1026]{2,1,0:T(8,128)} %broadcast_in_dim.17), calls=%async_computation.1 | async-start | bytes 4718592 | tf_op jit(solution)/shard_map/all_to_all | solution.py:14
  65.8 67.4 %all-to-all-start = ((f32[16,32,770]{2,1,0:T(8,128)}), f32[16,32,770]{2,1,0:T(8,128)}, u32[]{:S(2)}, u32[]{:S(2)}) async-start(f32[16,32,770]{2,1,0:T(8,128)} %broadcast_in_dim.16), calls=%async_computation | async-start | bytes 3670016 | tf_op jit(solution)/shard_map/all_to_all | solution.py:14
  90.3 3.8 %copy-start.6 = (s32[16,512]{1,0:T(8,128)S(1)}, s32[16,512]{1,0:T(8,128)}, u32[]{:S(2)}) copy-start(s32[16,512]{1,0:T(8,128)} %param.9) | copy-start | bytes 98308
  92.1 42.5 %collective-permute-start = (f32[512,1026]{0,1:T(8,128)}, f32[512,1026]{0,1:T(8,128)}, u32[]{:S(2)}, u32[]{:S(2)}) collective-permute-start(f32[512,1026]{0,1:T(8,128)} %copy.26), channel_id=1, source_target_pairs={{0,16},{16,0},{1,17},{17,1},{2,18},{18,2},{3,19},{19,3},{4,20},{20... | collective-permute-start | bytes 6303752 | tf_op jit(solution)/shard_map/ppermute | solution.py:20
  137.7 1.8 copy-start
  137.7 2.5 copy-start.3
  147.3 2.0 copy-start.1
  149.2 27.9 %copy-start.5 = (f32[32,256]{1,0:T(8,128)S(1)}, f32[32,256]{1,0:T(8,128)}, u32[]{:S(2)}) copy-start(f32[32,256]{1,0:T(8,128)} %param.7) | copy-start | bytes 98308
  149.5 49.2 %copy-start.2 = (f32[512,1024]{1,0:T(8,128)S(1)}, f32[512,1024]{1,0:T(8,128)}, u32[]{:S(2)}) copy-start(f32[512,1024]{1,0:T(8,128)} %copy-done.1) | copy-start | bytes 6291460
  195.0 3.8 %collective-permute-start.1 = (f32[512,256]{1,0:T(8,128)S(1)}, f32[512,256]{1,0:T(8,128)S(1)}, u32[]{:S(2)}, u32[]{:S(2)}) collective-permute-start(f32[512,256]{1,0:T(8,128)S(1)} %bitcast.21), channel_id=1, source_target_pairs={{0,16},{16,0},{1,17},{17,1},{2,18},{18,2},{3,19},{19,3},{4,20},{20... | collective-permute-start | bytes 1572872 | tf_op jit(solution)/shard_map/ppermute | solution.py:20
  242.2 3.8 %collective-permute-start.2 = (f32[512,256]{1,0:T(8,128)S(1)}, f32[512,256]{1,0:T(8,128)S(1)}, u32[]{:S(2)}, u32[]{:S(2)}) collective-permute-start(f32[512,256]{1,0:T(8,128)S(1)} %bitcast.19), channel_id=1, source_target_pairs={{0,16},{16,0},{1,17},{17,1},{2,18},{18,2},{3,19},{19,3},{4,20},{20... | collective-permute-start | bytes 1572872 | tf_op jit(solution)/shard_map/ppermute | solution.py:20

commit v3 on v2

--- a/solution.py
+++ b/solution.py
@@ -37,7 +37,7 @@
     seeded = seed_mask.astype(jnp.float32)[:, None] * soft_labels
     squares = jnp.sum(embeddings * embeddings, axis=1)
     packed = jnp.concatenate([embeddings, sharpness[:, None], squares[:, None]], axis=1)
-    row_pack = gather_rows(packed, "col", n_col)
+    row_pack = lax.all_gather(packed, "col", axis=0, tiled=True)
     col_pack = gather_row_set(jnp.concatenate([packed, seeded], axis=1), n_chips)
     row_emb, row_width, row_squares = row_pack[:, :width], row_pack[:, width], row_pack[:, width + 1]
     col_emb, col_width, col_squares = col_pack[:, :width], col_pack[:, width], col_pack[:, width + 1]

time: 274 us -> 274 us (level)
  starting transfers between devices: 43.4 us -> 19 us
  blocking collectives: 111 us -> 133 us
  between operations: 0.22 us -> 13.6 us
  waiting for transfers between devices: 65.4 us -> 55.7 us
    all_to_all x2 -> x1, starting transfers between devices: 37.5 us -> 13 us  [gather_rows(): got = lax.all_to_all(copies, axis, 0, 0, tiled=False)]
    all_to_all x3, blocking collectives: 75.3 us -> 96.5 us  [scatter_sum(): lax.all_to_all(p.reshape((n, chunk) + p.shape[1:]), axis, 0, 0, tiled=False)]
    all_to_all x2 -> x1, waiting for transfers between devices: 61.8 us -> 44.6 us  [gather_rows(): got = lax.all_to_all(copies, axis, 0, 0, tiled=False)]
    all_gather x0 -> x1, waiting for transfers between devices: none -> 7.55 us  [local(): row_pack = lax.all_gather(packed, 'col', axis=0, tiled=True)]
where the time goes in v3:
time: 274 us
  blocking collectives  133 us (49%)
  waiting for transfers between devices  55.7 us (20%)
  local copies, waits for them, and re-layouts  33.5 us (12%)
  starting transfers between devices  19 us (7%)
  between operations  13.6 us (5%)
  matrix products  12.7 us (5%)
  other arithmetic  6 us (2%)
    all_to_all x3, blocking collectives, scatter_sum(): lax.all_to_all(p.reshape((n, chunk) + p.shape[1:]), axis, 0, 0, tiled=False)  96.5 us
    all_to_all x1, waiting for transfers between devices, gather_rows(): got = lax.all_to_all(copies, axis, 0, 0, tiled=False)  44.6 us
    all_to_all x2, blocking collectives, gather_rows(): got = lax.all_to_all(copies, axis, 0, 0, tiled=False)  36.7 us
    all_to_all x1, starting transfers between devices, gather_rows(): got = lax.all_to_all(copies, axis, 0, 0, tiled=False)  13 us
    dynamic_slice x1, local copies, waits for them, and re-layouts, local(): own_half = lax.dynamic_index_in_dim(chosen, core, axis=2, keepdims=False)  10.1 us
    convert_element_type x1, local copies, waits for them, and re-layouts, local(): col_mask = col_mask.reshape(block_rows, col_rows).astype(jnp.float32)  7.71 us
    all_gather x1, waiting for transfers between devices, local(): row_pack = lax.all_gather(packed, 'col', axis=0, tiled=True)  7.55 us
    dot_general x1, matrix products, local(): jnp.dot(row_emb, col_emb.T, precision=lax.Precision.HIGHEST, preferred_el...  7.14 us
  transfers between devices with their start and end apart: 5, of which 4 were waited for; matrix products, arithmetic and copies ran while one was open for 10% of the time, Pallas kernels for 0%

profile of v3, /device:TPU:8, one launch (start us, length us, event | category | flops | bytes accessed | tf_op | source)
XLA Modules:
  0.0 273.7 jit_solution(6123440267275811822)
XLA Ops:
  6.5 0.7 convert_element_type.10
  7.2 1.0 multiply_reduce_fusion
  8.2 0.1 copy.22
  8.3 0.7 copy.21
  9.0 0.8 broadcast_multiply_fusion
  9.9 1.0 concatenate.28
  10.8 1.6 broadcast_in_dim.14
  12.5 13.0 %all-to-all-start = ((f32[16,32,1026]{2,1,0:T(8,128)}), f32[16,32,1026]{2,1,0:T(8,128)S(1)}, u32[]{:S(2)}, u32[]{:S(2)}) async-start(f32[16,32,1026]{2,1,0:T(8,128)} %broadcast_in_dim.14), calls=%async_computation | async-start | bytes 4718592 | tf_op jit(solution)/shard_map/all_to_all | solution.py:14
  25.5 0.0 all-gather.2.cloned.1.call-start
  25.5 0.0 copy-done.4
  25.6 0.7 pad_maximum_fusion.3
  26.3 0.0 all-gather.2.cloned.1.call-update
  26.3 44.6 %all-to-all-done = f32[16,32,1026]{2,1,0:T(8,128)S(1)} async-done(((f32[16,32,1026]{2,1,0:T(8,128)}), f32[16,32,1026]{2,1,0:T(8,128)S(1)}, u32[]{:S(2)}, u32[]{:S(2)}) %all-to-all-start) | async-done | bytes 2101280 | tf_op jit(solution)/shard_map/all_to_all | solution.py:14
  70.9 1.8 copy.25
  72.7 1.9 collective-permute-start
  74.7 0.4 reshape.36
  75.1 10.1 %dynamic-slice_reduce_fusion.1 = (s32[16,16]{1,0:T(8,128)S(1)}, s32[16,16]{1,0:T(8,128)S(1)}) fusion(s32[16,16,2,16]{3,2,1,0:T(2,128)S(1)} %reshape.36, s32[]{:T(128)S(6)} %select_n.18, s32[]{:T(128)S(6)} %select_n.20, s32[]{:T(128)S(6)} %select_n.22), kind=kLoop, calls=%fused_computation.26 | loop fusion | bytes 4108 | tf_op jit(solution)/shard_map/jit(dynamic_index_in_dim)/dynamic_slice | solution.py:49
  85.2 0.1 add_convert_fusion
  85.3 4.4 %broadcast_in_dim.15 = f32[16,32,32,32]{3,2,1,0:T(8,128)} broadcast(f32[16,32]{1,0:T(8,128)S(1)} %add_convert_fusion), dimensions={0,2} | broadcast | bytes 2099200 | tf_op jit(solution)/shard_map/broadcast_in_dim | solution.py:52
  89.6 7.7 %convert_element_type.12 = f32[512,1024]{1,0:T(8,128)} reshape(f32[16,32,32,32]{3,2,1,0:T(8,128)} %broadcast_in_dim.15) | data formatting | bytes 4194304 | tf_op jit(solution)/shard_map/convert_element_type | solution.py:53
  97.3 7.5 %all-gather.2.cloned.1.call-done = f32[512,770]{1,0:T(8,128)} async-done(((f32[32,770]{1,0:T(8,128)}), f32[512,770]{1,0:T(8,128)}) %all-gather.2.cloned.1.call-update) | async-done | bytes 1576976 | tf_op jit(solution)/shard_map/all_gather | solution.py:40
  104.9 1.4 slice_reduce_fusion.1
  106.3 0.0 collective-permute-done
  106.3 3.0 %copy.26 = f32[512,1026]{1,0:T(8,128)} copy(f32[512,1026]{0,1:T(8,128)} %collective-permute-done) | data formatting | bytes 4202496 | tf_op jit(solution)/shard_map/ppermute | solution.py:20
  109.3 1.7 maximum_reduce_fusion
  111.0 0.1 copy-done
  111.2 0.6 copy-done.3
  111.8 7.1 %fusion.26 = (f32[512]{0:T(512)S(1)}, f32[512,1024]{1,0:T(8,128)S(1)}) fusion(f32[512,1024]{1,0:T(8,128)S(1)} %copy-done.3, f32[1024]{0:T(1024)S(1)} %get-tuple-element.6, f32[512]{0:T(512)S(1)} %get-tuple-element.8, f32[512,1026]{1,0:T(8,128)S(1)} %bitcast.15, f32[512,1026]{1,0:T(8,128)S(1)} %copy-done, f32[512,770]{1,0:T(8,128)} %all-gather.2.cloned.1.call-done, ...), kind=kOutput, calls=%fused_computation.41 | convolution fusion | flops 4836818432 | bytes 9984000 | tf_op jit(solution)/shard_map/dot_general | solution.py:54
  119.0 1.9 fusion.4
  120.9 0.0 copy-start.5
  120.9 0.2 concatenate.36
  121.1 0.1 pad_maximum_fusion.2
  121.2 0.0 copy-start.2
  121.2 48.7 %all_to_all.30 = f32[16,32,257]{2,1,0:T(8,128)S(1)} all-to-all(f32[16,32,257]{2,1,0:T(8,128)S(1)} %pad_maximum_fusion.2), channel_id=1, replica_groups=mesh['zh'=4,'x'=4,'core'=2,'col'=16] {'col'}, dimensions={0} | all-to-all | bytes 1052672 | tf_op jit(solution)/shard_map/all_to_all | solution.py:26
  170.0 0.1 slice_reduce_fusion.2
  170.1 0.1 fusion.17
  170.2 18.7 %all_to_all.31 = f32[16,32,256]{2,1,0:T(8,128)S(1)} all-to-all(f32[16,32,256]{2,1,0:T(8,128)S(1)} %broadcast_in_dim.16), channel_id=1, replica_groups=mesh['zh'=4,'x'=4,'core'=2,'col'=16] {'zh','x'}, dimensions={0} | all-to-all | bytes 1048576 | tf_op jit(solution)/shard_map/all_to_all | solution.py:14
  189.0 2.1 collective-permute-start.1
  191.1 1.7 collective-permute-done.1
  192.8 1.8 fusion.6
  194.6 23.5 %all_to_all.32 = f32[16,32,256]{2,1,0:T(8,128)S(1)} all-to-all(f32[16,32,256]{2,1,0:T(8,128)S(1)} %bitcast.23), channel_id=1, replica_groups=mesh['zh'=4,'x'=4,'core'=2,'col'=16] {'col'}, dimensions={0} | all-to-all | bytes 1048576 | tf_op jit(solution)/shard_map/all_to_all | solution.py:26
  218.1 0.1 divide_add_fusion.1
  218.2 18.0 %all_to_all.33 = f32[16,32,256]{2,1,0:T(8,128)S(1)} all-to-all(f32[16,32,256]{2,1,0:T(8,128)S(1)} %broadcast_in_dim.17), channel_id=1, replica_groups=mesh['zh'=4,'x'=4,'core'=2,'col'=16] {'zh','x'}, dimensions={0} | all-to-all | bytes 1048576 | tf_op jit(solution)/shard_map/all_to_all | solution.py:14
  236.2 1.9 collective-permute-start.2
  238.1 1.9 collective-permute-done.2
  240.0 1.8 fusion.10
  241.8 24.3 %all_to_all.34 = f32[16,32,256]{2,1,0:T(8,128)S(1)} all-to-all(f32[16,32,256]{2,1,0:T(8,128)S(1)} %bitcast.22), channel_id=1, replica_groups=mesh['zh'=4,'x'=4,'core'=2,'col'=16] {'col'}, dimensions={0} | all-to-all | bytes 1048576 | tf_op jit(solution)/shard_map/all_to_all | solution.py:26
  266.2 0.7 divide_add_fusion
  (14 shorter events, 0.2 us)
Async XLA Ops:
  12.5 13.1 %copy-start.4 = (f32[32,768]{1,0:T(8,128)S(1)}, f32[32,768]{1,0:T(8,128)}, u32[]{:S(2)}) copy-start(f32[32,768]{1,0:T(8,128)} %param.5) | copy-start | bytes 294916
  12.5 58.4 %all-to-all-start = ((f32[16,32,1026]{2,1,0:T(8,128)}), f32[16,32,1026]{2,1,0:T(8,128)S(1)}, u32[]{:S(2)}, u32[]{:S(2)}) async-start(f32[16,32,1026]{2,1,0:T(8,128)} %broadcast_in_dim.14), calls=%async_computation | async-start | bytes 4718592 | tf_op jit(solution)/shard_map/all_to_all | solution.py:14
  25.5 79.4 %all-gather.2.cloned.1.call-start = ((), (), s32[]{:S(2)}) async-start(), calls=%async_computation.6 | async-start | bytes 1949696 | tf_op jit(solution)/shard_map/all_gather | solution.py:40
  70.9 3.8 %copy-start.6 = (s32[16,512]{1,0:T(8,128)S(1)}, s32[16,512]{1,0:T(8,128)}, u32[]{:S(2)}) copy-start(s32[16,512]{1,0:T(8,128)} %param.9) | copy-start | bytes 98308
  72.7 33.6 %collective-permute-start = (f32[512,1026]{0,1:T(8,128)}, f32[512,1026]{0,1:T(8,128)}, u32[]{:S(2)}, u32[]{:S(2)}) collective-permute-start(f32[512,1026]{0,1:T(8,128)} %copy.25), channel_id=1, source_target_pairs={{0,16},{16,0},{1,17},{17,1},{2,18},{18,2},{3,19},{19,3},{4,20},{20... | collective-permute-start | bytes 6303752 | tf_op jit(solution)/shard_map/ppermute | solution.py:20
  109.3 1.8 copy-start
  109.3 2.5 copy-start.3
  118.9 2.0 copy-start.1
  120.9 49.2 %copy-start.5 = (f32[32,256]{1,0:T(8,128)S(1)}, f32[32,256]{1,0:T(8,128)}, u32[]{:S(2)}) copy-start(f32[32,256]{1,0:T(8,128)} %param.7) | copy-start | bytes 98308
  121.2 71.6 %copy-start.2 = (f32[512,1024]{1,0:T(8,128)S(1)}, f32[512,1024]{1,0:T(8,128)}, u32[]{:S(2)}) copy-start(f32[512,1024]{1,0:T(8,128)} %copy-done.1) | copy-start | bytes 6291460
  189.0 3.8 %collective-permute-start.1 = (f32[512,256]{1,0:T(8,128)S(1)}, f32[512,256]{1,0:T(8,128)S(1)}, u32[]{:S(2)}, u32[]{:S(2)}) collective-permute-start(f32[512,256]{1,0:T(8,128)S(1)} %bitcast.20), channel_id=1, source_target_pairs={{0,16},{16,0},{1,17},{17,1},{2,18},{18,2},{3,19},{19,3},{4,20},{20... | collective-permute-start | bytes 1572872 | tf_op jit(solution)/shard_map/ppermute | solution.py:20
  236.2 3.8 %collective-permute-start.2 = (f32[512,256]{1,0:T(8,128)S(1)}, f32[512,256]{1,0:T(8,128)S(1)}, u32[]{:S(2)}, u32[]{:S(2)}) collective-permute-start(f32[512,256]{1,0:T(8,128)S(1)} %bitcast.18), channel_id=1, source_target_pairs={{0,16},{16,0},{1,17},{17,1},{2,18},{18,2},{3,19},{19,3},{4,20},{20... | collective-permute-start | bytes 1572872 | tf_op jit(solution)/shard_map/ppermute | solution.py:20
Sparse Core Ops, SparseCore 0:
  28.4 76.4 all-gather.1

commit v4 on v3

--- a/solution.py
+++ b/solution.py
@@ -16,9 +16,11 @@
 
 
 def gather_row_set(x, n_chips):
-    mine = gather_rows(x, CHIPS, n_chips)
+    copies = jnp.broadcast_to(x[None], (n_chips,) + x.shape)
+    mine = lax.all_to_all(copies, CHIPS, 0, 0, tiled=False)
     other = lax.ppermute(mine, "core", [(0, 1), (1, 0)])
-    return jnp.concatenate([mine, other], axis=0)
+    both = jnp.concatenate([mine, other], axis=0)
+    return both.reshape((2 * n_chips * x.shape[0],) + x.shape[1:])
 
 
 def scatter_sum(p, axis, n):
@@ -37,8 +39,8 @@
     seeded = seed_mask.astype(jnp.float32)[:, None] * soft_labels
     squares = jnp.sum(embeddings * embeddings, axis=1)
     packed = jnp.concatenate([embeddings, sharpness[:, None], squares[:, None]], axis=1)
-    row_pack = lax.all_gather(packed, "col", axis=0, tiled=True)
     col_pack = gather_row_set(jnp.concatenate([packed, seeded], axis=1), n_chips)
+    row_pack = gather_rows(packed, "col", n_col)
     row_emb, row_width, row_squares = row_pack[:, :width], row_pack[:, width], row_pack[:, width + 1]
     col_emb, col_width, col_squares = col_pack[:, :width], col_pack[:, width], col_pack[:, width + 1]
     col_labels = col_pack[:, width + 2:]
@@ -63,9 +65,11 @@
             weights, col_labels, precision=lax.Precision.HIGHEST, preferred_element_type=jnp.float32
         )
         if degree is None:
-            both = jnp.concatenate([partial_value, jnp.sum(weights, axis=1)[:, None]], axis=1)
-            both = scatter_sum(both, "col", n_col)
-            own_part, degree = both[:, :n_labels], both[:, n_labels]
+            row_sums = jnp.sum(weights, axis=1).reshape(n_col, 1, piece)
+            row_sums = jnp.pad(row_sums, ((0, 0), (0, 7), (0, n_labels - piece)))
+            both = jnp.concatenate([partial_value.reshape(n_col, piece, n_labels), row_sums], axis=1)
+            both = scatter_sum(both.reshape(n_col * (piece + 8), n_labels), "col", n_col)
+            own_part, degree = both[:piece], both[piece, :piece]
         else:
             own_part = scatter_sum(partial_value, "col", n_col)
         labels = 0.9 * own_part / degree[:, None] + 0.1 * seeded

time: 274 us -> 268 us (0.978)
  blocking collectives: 133 us -> 108 us
  starting transfers between devices: 19 us -> 43.5 us
  between operations: 13.6 us -> 0.22 us
  waiting for transfers between devices: 55.7 us -> 67.2 us
  local copies, waits for them, and re-layouts: 33.5 us -> 29.5 us
    all_to_all x0 -> x1, waiting for transfers between devices: none -> 45.3 us  [gather_row_set(): mine = lax.all_to_all(copies, CHIPS, 0, 0, tiled=False)]
    all_to_all x1, waiting for transfers between devices: 44.6 us -> 18.4 us  [gather_rows(): got = lax.all_to_all(copies, axis, 0, 0, tiled=False)]
    all_to_all x3, blocking collectives: 96.5 us -> 71.5 us  [scatter_sum(): lax.all_to_all(p.reshape((n, chunk) + p.shape[1:]), axis, 0, 0, tiled=False)]
    all_to_all x0 -> x1, starting transfers between devices: none -> 13 us  [gather_row_set(): mine = lax.all_to_all(copies, CHIPS, 0, 0, tiled=False)]
    all_to_all x1, starting transfers between devices: 13 us -> 24.6 us  [gather_rows(): got = lax.all_to_all(copies, axis, 0, 0, tiled=False)]
    all_gather x1 -> x0, waiting for transfers between devices: 7.55 us -> none  [local(): row_pack = lax.all_gather(packed, 'col', axis=0, tiled=True)]
    ppermute x1 -> x0, local copies, waits for them, and re-layouts: 3.04 us -> none  [gather_row_set(): other = lax.ppermute(mine, 'core', [(0, 1), (1, 0)])]
  transfers between devices with their start and end apart: 5 -> 5, of which waited for: 4 -> 4; matrix products, arithmetic and copies ran while one was open for 10% -> 9% of each run, Pallas kernels for 0% -> 0%
where the time goes in v4:
time: 268 us; the launch traced here: 267 us
  blocking collectives  108 us (40%)
  waiting for transfers between devices  67.2 us (25%)
  starting transfers between devices  43.5 us (16%)
  local copies, waits for them, and re-layouts  29.5 us (11%)
  matrix products  12.7 us (5%)
  other arithmetic  5.93 us (2%)
    all_to_all x3, blocking collectives, scatter_sum(): lax.all_to_all(p.reshape((n, chunk) + p.shape[1:]), axis, 0, 0, tiled=False)  71.5 us
    all_to_all x1, waiting for transfers between devices, gather_row_set(): mine = lax.all_to_all(copies, CHIPS, 0, 0, tiled=False)  45.3 us
    all_to_all x2, blocking collectives, gather_row_set(): mine = lax.all_to_all(copies, CHIPS, 0, 0, tiled=False)  36.4 us
    all_to_all x1, starting transfers between devices, gather_rows(): got = lax.all_to_all(copies, axis, 0, 0, tiled=False)  24.6 us
    all_to_all x1, waiting for transfers between devices, gather_rows(): got = lax.all_to_all(copies, axis, 0, 0, tiled=False)  18.4 us
    all_to_all x1, starting transfers between devices, gather_row_set(): mine = lax.all_to_all(copies, CHIPS, 0, 0, tiled=False)  13 us
    dynamic_slice x1, local copies, waits for them, and re-layouts, local(): own_half = lax.dynamic_index_in_dim(chosen, core, axis=2, keepdims=False)  10.1 us
    convert_element_type x1, local copies, waits for them, and re-layouts, local(): col_mask = col_mask.reshape(block_rows, col_rows).astype(jnp.float32)  7.7 us
  transfers between devices with their start and end apart: 5, of which 4 were waited for; matrix products, arithmetic and copies ran while one was open for 9% of the time, Pallas kernels for 0%

profile of v4, /device:TPU:8, one launch (start us, length us, event | category | flops | bytes accessed | tf_op | source)
XLA Modules:
  0.0 267.0 jit_solution(10256139649113691512)
XLA Ops:
  0.0 0.7 convert_element_type.12
  0.7 1.0 multiply_reduce_fusion
  1.7 0.1 copy.17
  1.8 0.7 copy.16
  2.5 0.8 broadcast_multiply_fusion
  3.3 1.0 concatenate.23
  4.3 1.6 broadcast_in_dim.17
  6.0 13.0 %all-to-all-start.1 = ((f32[16,32,1026]{2,1,0:T(8,128)}), f32[16,32,1026]{2,1,0:T(8,128)S(1)}, u32[]{:S(2)}, u32[]{:S(2)}) async-start(f32[16,32,1026]{2,1,0:T(8,128)} %broadcast_in_dim.17), calls=%async_computation.1 | async-start | bytes 4718592 | tf_op jit(solution)/shard_map/all_to_all | solution.py:20
  19.0 0.0 copy-done.1
  19.0 0.1 pad_maximum_fusion.3
  19.1 45.3 %all-to-all-done.1 = f32[16,32,1026]{2,1,0:T(8,128)S(1)} async-done(((f32[16,32,1026]{2,1,0:T(8,128)}), f32[16,32,1026]{2,1,0:T(8,128)S(1)}, u32[]{:S(2)}, u32[]{:S(2)}) %all-to-all-start.1) | async-done | bytes 2101280 | tf_op jit(solution)/shard_map/all_to_all | solution.py:20
  64.4 1.4 broadcast_in_dim.16
  65.8 24.6 %all-to-all-start = ((f32[16,32,770]{2,1,0:T(8,128)}), f32[16,32,770]{2,1,0:T(8,128)}, u32[]{:S(2)}, u32[]{:S(2)}) async-start(f32[16,32,770]{2,1,0:T(8,128)} %broadcast_in_dim.16), calls=%async_computation | async-start | bytes 3670016 | tf_op jit(solution)/shard_map/all_to_all | solution.py:14
  90.4 1.9 collective-permute-start
  92.3 0.0 copy-done.3
  92.3 0.4 reshape.42
  92.7 10.1 %dynamic-slice_reduce_fusion.1 = (s32[16,16]{1,0:T(8,128)S(1)}, s32[16,16]{1,0:T(8,128)S(1)}) fusion(s32[16,16,2,16]{3,2,1,0:T(2,128)S(1)} %reshape.42, s32[]{:T(128)S(6)} %select_n.18, s32[]{:T(128)S(6)} %select_n.20, s32[]{:T(128)S(6)} %select_n.22), kind=kLoop, calls=%fused_computation.16 | loop fusion | bytes 4108 | tf_op jit(solution)/shard_map/jit(dynamic_index_in_dim)/dynamic_slice | solution.py:51
  102.8 0.1 add_convert_fusion
  102.9 4.4 %broadcast_in_dim.18 = f32[16,32,32,32]{3,2,1,0:T(8,128)} broadcast(f32[16,32]{1,0:T(8,128)S(1)} %add_convert_fusion), dimensions={0,2} | broadcast | bytes 2099200 | tf_op jit(solution)/shard_map/broadcast_in_dim | solution.py:54
  107.3 7.7 %convert_element_type.14 = f32[512,1024]{1,0:T(8,128)} reshape(f32[16,32,32,32]{3,2,1,0:T(8,128)} %broadcast_in_dim.18) | data formatting | bytes 4194304 | tf_op jit(solution)/shard_map/convert_element_type | solution.py:55
  115.0 18.4 %all-to-all-done = f32[16,32,770]{2,1,0:T(8,128)} async-done(((f32[16,32,770]{2,1,0:T(8,128)}), f32[16,32,770]{2,1,0:T(8,128)}, u32[]{:S(2)}, u32[]{:S(2)}) %all-to-all-start) | async-done | bytes 1576992 | tf_op jit(solution)/shard_map/all_to_all | solution.py:14
  133.4 1.4 slice_reduce_fusion.3
  134.7 0.0 copy-start
  134.7 0.0 collective-permute-done
  134.8 2.1 pad_maximum_fusion
  136.9 0.5 slice_reduce_fusion.1
  137.4 0.0 copy-done
  137.4 7.1 %fusion.7 = (f32[512]{0:T(512)S(1)}, f32[512,1024]{1,0:T(8,128)S(1)}) fusion(f32[512,1024]{1,0:T(8,128)S(1)} %copy-done, f32[1024]{0:T(1024)S(1)} %get-tuple-element.6, f32[512]{0:T(512)S(1)} %get-tuple-element.8, f32[1024]{0:T(1024)S(1)} %get-tuple-element.5, f32[512]{0:T(512)S(1)} %get-tuple-element.7, f32[1024,1026]{1,0:T(8,128)S(1)} %bitcast.24, ...), kind=kOutput, calls=%fused_computation.27 | convolution fusion | flops 4836032000 | bytes 8927232 | tf_op jit(solution)/shard_map/dot_general | solution.py:56
  144.5 1.9 fusion.3
  146.5 0.0 copy-start.2
  146.5 0.1 reshape.44
  146.6 24.9 %all_to_all.35 = f32[16,40,256]{2,1,0:T(8,128)S(1)} all-to-all(f32[16,40,256]{2,1,0:T(8,128)S(1)} %select_maximum_fusion), channel_id=1, replica_groups=mesh['zh'=4,'x'=4,'core'=2,'col'=16] {'col'}, dimensions={0} | all-to-all | bytes 1310720 | tf_op jit(solution)/shard_map/all_to_all | solution.py:28
  171.6 0.0 copy-done.2
  171.6 0.1 fusion.6
  171.7 17.9 %all_to_all.36 = f32[16,32,256]{2,1,0:T(8,128)S(1)} all-to-all(f32[16,32,256]{2,1,0:T(8,128)S(1)} %broadcast_in_dim.19), channel_id=1, replica_groups=mesh['zh'=4,'x'=4,'core'=2,'col'=16] {'zh','x'}, dimensions={0} | all-to-all | bytes 1048576 | tf_op jit(solution)/shard_map/all_to_all | solution.py:20
  189.6 2.1 collective-permute-start.1
  191.7 1.7 collective-permute-done.1
  193.4 0.1 pad_maximum_fusion.1
  193.5 1.8 fusion.8
  195.3 22.3 %all_to_all.37 = f32[16,32,256]{2,1,0:T(8,128)S(1)} all-to-all(f32[16,32,256]{2,1,0:T(8,128)S(1)} %fusion.8), channel_id=1, replica_groups=mesh['zh'=4,'x'=4,'core'=2,'col'=16] {'col'}, dimensions={0} | all-to-all | bytes 1048576 | tf_op jit(solution)/shard_map/all_to_all | solution.py:28
  217.6 0.1 divide_add_fusion.1
  217.7 18.5 %all_to_all.38 = f32[16,32,256]{2,1,0:T(8,128)S(1)} all-to-all(f32[16,32,256]{2,1,0:T(8,128)S(1)} %broadcast_in_dim.20), channel_id=1, replica_groups=mesh['zh'=4,'x'=4,'core'=2,'col'=16] {'zh','x'}, dimensions={0} | all-to-all | bytes 1048576 | tf_op jit(solution)/shard_map/all_to_all | solution.py:20
  236.3 1.9 collective-permute-start.2
  238.2 1.9 collective-permute-done.2
  240.1 0.1 pad_maximum_fusion.2
  240.1 1.8 fusion.9
  241.9 24.3 %all_to_all.39 = f32[16,32,256]{2,1,0:T(8,128)S(1)} all-to-all(f32[16,32,256]{2,1,0:T(8,128)S(1)} %fusion.9), channel_id=1, replica_groups=mesh['zh'=4,'x'=4,'core'=2,'col'=16] {'col'}, dimensions={0} | all-to-all | bytes 1048576 | tf_op jit(solution)/shard_map/all_to_all | solution.py:28
  266.3 0.7 divide_add_fusion
  (9 shorter events, 0.3 us)
Async XLA Ops:
  6.0 13.0 %copy-start.1 = (f32[32,768]{1,0:T(8,128)S(1)}, f32[32,768]{1,0:T(8,128)}, u32[]{:S(2)}) copy-start(f32[32,768]{1,0:T(8,128)} %param.5) | copy-start | bytes 294916
  6.0 58.4 %all-to-all-start.1 = ((f32[16,32,1026]{2,1,0:T(8,128)}), f32[16,32,1026]{2,1,0:T(8,128)S(1)}, u32[]{:S(2)}, u32[]{:S(2)}) async-start(f32[16,32,1026]{2,1,0:T(8,128)} %broadcast_in_dim.17), calls=%async_computation.1 | async-start | bytes 4718592 | tf_op jit(solution)/shard_map/all_to_all | solution.py:20
  65.8 26.5 %copy-start.3 = (s32[16,512]{1,0:T(8,128)S(1)}, s32[16,512]{1,0:T(8,128)}, u32[]{:S(2)}) copy-start(s32[16,512]{1,0:T(8,128)} %param.9) | copy-start | bytes 98308
  65.8 67.6 %all-to-all-start = ((f32[16,32,770]{2,1,0:T(8,128)}), f32[16,32,770]{2,1,0:T(8,128)}, u32[]{:S(2)}, u32[]{:S(2)}) async-start(f32[16,32,770]{2,1,0:T(8,128)} %broadcast_in_dim.16), calls=%async_computation | async-start | bytes 3670016 | tf_op jit(solution)/shard_map/all_to_all | solution.py:14
  90.4 44.4 %collective-permute-start = (f32[16,32,1026]{2,1,0:T(8,128)S(1)}, f32[16,32,1026]{2,1,0:T(8,128)}, u32[]{:S(2)}, u32[]{:S(2)}) collective-permute-start(f32[16,32,1026]{2,1,0:T(8,128)S(1)} %all-to-all-done.1), channel_id=1, source_target_pairs={{0,16},{16,0},{1,17},{17,1},{2,18},{18,2},{3,19},{19,3},{4,20},{20... | collective-permute-start | bytes 6303752 | tf_op jit(solution)/shard_map/ppermute | solution.py:21
  134.7 2.7 copy-start
  146.5 25.1 %copy-start.2 = (f32[32,256]{1,0:T(8,128)S(1)}, f32[32,256]{1,0:T(8,128)}, u32[]{:S(2)}) copy-start(f32[32,256]{1,0:T(8,128)} %param.7) | copy-start | bytes 98308
  189.6 3.8 %collective-permute-start.1 = (f32[16,32,256]{2,1,0:T(8,128)S(1)}, f32[16,32,256]{2,1,0:T(8,128)S(1)}, u32[]{:S(2)}, u32[]{:S(2)}) collective-permute-start(f32[16,32,256]{2,1,0:T(8,128)S(1)} %all_to_all.36), channel_id=1, source_target_pairs={{0,16},{16,0},{1,17},{17,1},{2,18},{18,2},{3,19},{19,3},{4,20},{20... | collective-permute-start | bytes 1572872 | tf_op jit(solution)/shard_map/ppermute | solution.py:21
  236.3 3.8 %collective-permute-start.2 = (f32[16,32,256]{2,1,0:T(8,128)S(1)}, f32[16,32,256]{2,1,0:T(8,128)S(1)}, u32[]{:S(2)}, u32[]{:S(2)}) collective-permute-start(f32[16,32,256]{2,1,0:T(8,128)S(1)} %all_to_all.38), channel_id=1, source_target_pairs={{0,16},{16,0},{1,17},{17,1},{2,18},{18,2},{3,19},{19,3},{4,20},{20... | collective-permute-start | bytes 1572872 | tf_op jit(solution)/shard_map/ppermute | solution.py:21

commit v5 on v4

--- a/solution.py
+++ b/solution.py
@@ -39,30 +39,30 @@
     seeded = seed_mask.astype(jnp.float32)[:, None] * soft_labels
     squares = jnp.sum(embeddings * embeddings, axis=1)
     packed = jnp.concatenate([embeddings, sharpness[:, None], squares[:, None]], axis=1)
-    col_pack = gather_row_set(jnp.concatenate([packed, seeded], axis=1), n_chips)
+    col_pack = lax.all_gather(jnp.concatenate([packed, seeded], axis=1), ("zh", "x", "core"), axis=0, tiled=True)
     row_pack = gather_rows(packed, "col", n_col)
     row_emb, row_width, row_squares = row_pack[:, :width], row_pack[:, width], row_pack[:, width + 1]
     col_emb, col_width, col_squares = col_pack[:, :width], col_pack[:, width], col_pack[:, width + 1]
     col_labels = col_pack[:, width + 2:]
     block_rows = row_emb.shape[0]
     col_rows = col_emb.shape[0]
-    grouped = tile_mask.reshape(n_col, n_chips, 2, n_col)
-    chosen = lax.dynamic_index_in_dim(grouped, col_index, axis=3, keepdims=False)
-    own_half = lax.dynamic_index_in_dim(chosen, core, axis=2, keepdims=False)
-    other_half = lax.dynamic_index_in_dim(chosen, 1 - core, axis=2, keepdims=False)
-    chosen = jnp.concatenate([own_half, other_half], axis=1)
+    grouped = tile_mask.reshape(n_col, 2 * n_chips, n_col)
+    chosen = lax.dynamic_index_in_dim(grouped, col_index, axis=2, keepdims=False)
     col_mask = jnp.broadcast_to(chosen[:, None, :, None], (n_col, piece, 2 * n_chips, piece))
     col_mask = col_mask.reshape(block_rows, col_rows).astype(jnp.float32)
     cross = jnp.dot(row_emb, col_emb.T, precision=lax.Precision.HIGHEST, preferred_element_type=jnp.float32)
     distance = row_squares[:, None] + col_squares[None, :] - 2.0 * cross
     weights = jnp.exp(-(distance * row_width[:, None] * col_width[None, :])) * col_mask
+    split = weights.reshape(block_rows, n_chips, 2, piece)
+    split = jnp.where(core == 0, split, split[:, :, ::-1, :])
+    split = jnp.transpose(split, (0, 2, 1, 3)).reshape(block_rows, col_rows)
     degree = None
     labels = seeded
     for iteration in range(ITERS):
         if iteration > 0:
             col_labels = gather_row_set(labels, n_chips)
         partial_value = jnp.dot(
-            weights, col_labels, precision=lax.Precision.HIGHEST, preferred_element_type=jnp.float32
+            split if iteration > 0 else weights, col_labels, precision=lax.Precision.HIGHEST, preferred_element_type=jnp.float32
         )
         if degree is None:
             row_sums = jnp.sum(weights, axis=1).reshape(n_col, 1, piece)

time: 268 us -> 263 us (0.981)
  starting transfers between devices: 43.5 us -> 13.5 us
  between operations: 0.22 us -> 13.6 us
  blocking collectives: 108 us -> 114 us
  waiting for transfers between devices: 67.2 us -> 61.6 us
  local copies, waits for them, and re-layouts: 29.5 us -> 34.6 us
  matrix products: 12.7 us -> 17.1 us
    all_to_all x1 -> x0, waiting for transfers between devices: 45.3 us -> none  [gather_row_set(): mine = lax.all_to_all(copies, CHIPS, 0, 0, tiled=False)]
    all_gather x0 -> x1, waiting for transfers between devices: none -> 28.9 us  [local(): lax.all_gather(jnp.concatenate([packed, seeded], axis=1), ('zh', 'x', 'co...]
    all_to_all x1, starting transfers between devices: 24.6 us -> 9.5 us  [gather_rows(): got = lax.all_to_all(copies, axis, 0, 0, tiled=False)]
    all_to_all x1 -> x0, starting transfers between devices: 13 us -> none  [gather_row_set(): mine = lax.all_to_all(copies, CHIPS, 0, 0, tiled=False)]
    all_to_all x1, waiting for transfers between devices: 18.4 us -> 30.8 us  [gather_rows(): got = lax.all_to_all(copies, axis, 0, 0, tiled=False)]
    dynamic_slice x1 -> x0, local copies, waits for them, and re-layouts: 10.1 us -> none  [local(): own_half = lax.dynamic_index_in_dim(chosen, core, axis=2, keepdims=False)]
    transpose x0 -> x1, local copies, waits for them, and re-layouts: none -> 7.62 us  [local(): split = jnp.transpose(split, (0, 2, 1, 3)).reshape(block_rows, col_rows)]
    dot_general x0 -> x1, local copies, waits for them, and re-layouts: none -> 6.63 us  [local(): jnp.dot(split if iteration > 0 else weights, col_labels, precision=lax.Pr...]
  transfers between devices with their start and end apart: 5 -> 4, of which waited for: 4 -> 3; matrix products, arithmetic and copies ran while one was open for 9% -> 13% of each run, Pallas kernels for 0% -> 0%
where the time goes in v5:
time: 263 us; the launch traced here: 262 us
  blocking collectives  114 us (43%)
  waiting for transfers between devices  61.6 us (23%)
  local copies, waits for them, and re-layouts  34.6 us (13%)
  matrix products  17.1 us (7%)
  between operations  13.6 us (5%)
  starting transfers between devices  13.5 us (5%)
  other arithmetic  7.61 us (3%)
    all_to_all x3, blocking collectives, scatter_sum(): lax.all_to_all(p.reshape((n, chunk) + p.shape[1:]), axis, 0, 0, tiled=False)  74 us
    all_to_all x2, blocking collectives, gather_row_set(): mine = lax.all_to_all(copies, CHIPS, 0, 0, tiled=False)  39.8 us
    all_to_all x1, waiting for transfers between devices, gather_rows(): got = lax.all_to_all(copies, axis, 0, 0, tiled=False)  30.8 us
    all_gather x1, waiting for transfers between devices, local(): lax.all_gather(jnp.concatenate([packed, seeded], axis=1), ('zh', 'x', 'co...  28.9 us
    dot_general x1, matrix products, local(): jnp.dot(row_emb, col_emb.T, precision=lax.Precision.HIGHEST, preferred_el...  10.1 us
    all_to_all x1, starting transfers between devices, gather_rows(): got = lax.all_to_all(copies, axis, 0, 0, tiled=False)  9.5 us
    convert_element_type x1, local copies, waits for them, and re-layouts, local(): col_mask = col_mask.reshape(block_rows, col_rows).astype(jnp.float32)  7.75 us
    transpose x1, local copies, waits for them, and re-layouts, local(): split = jnp.transpose(split, (0, 2, 1, 3)).reshape(block_rows, col_rows)  7.62 us
  transfers between devices with their start and end apart: 4, of which 3 were waited for; matrix products, arithmetic and copies ran while one was open for 13% of the time, Pallas kernels for 0%

profile of v5, /device:TPU:8, one launch (start us, length us, event | category | flops | bytes accessed | tf_op | source)
XLA Modules:
  0.0 261.6 jit_solution(15693510990097960393)
XLA Ops:
  6.5 0.0 all-gather.2.cloned.1.call-start
  6.5 0.7 convert_element_type.15
  7.2 1.0 multiply_reduce_fusion
  8.2 0.1 copy.19
  8.3 0.7 copy.18
  9.0 0.8 broadcast_multiply_fusion
  9.9 1.6 concatenate.17
  11.5 0.0 all-gather.2.cloned.1.call-update
  11.5 1.0 pad_maximum_fusion.2
  12.5 1.4 broadcast_in_dim.14
  13.9 0.0 copy-start.2
  13.9 9.5 %all-to-all-start = ((f32[16,32,770]{2,1,0:T(8,128)}), f32[16,32,770]{2,1,0:T(8,128)S(1)}, u32[]{:S(2)}, u32[]{:S(2)}) async-start(f32[16,32,770]{2,1,0:T(8,128)} %broadcast_in_dim.14), calls=%async_computation | async-start | bytes 3670016 | tf_op jit(solution)/shard_map/all_to_all | solution.py:14
  23.4 0.0 copy-done.2
  23.4 0.1 reshape.41
  23.5 0.3 convert_reduce_fusion
  23.8 4.4 %broadcast_in_dim.15 = f32[16,32,32,32]{3,2,1,0:T(8,128)} broadcast(f32[16,32]{1,0:T(8,128)S(1)} %convert_reduce_fusion), dimensions={0,2} | broadcast | bytes 2099200 | tf_op jit(solution)/shard_map/broadcast_in_dim | solution.py:51
  28.2 7.8 %convert_element_type.18 = f32[512,1024]{1,0:T(8,128)} reshape(f32[16,32,32,32]{3,2,1,0:T(8,128)} %broadcast_in_dim.15) | data formatting | bytes 4194304 | tf_op jit(solution)/shard_map/convert_element_type | solution.py:52
  35.9 30.8 %all-to-all-done = f32[16,32,770]{2,1,0:T(8,128)S(1)} async-done(((f32[16,32,770]{2,1,0:T(8,128)}), f32[16,32,770]{2,1,0:T(8,128)S(1)}, u32[]{:S(2)}, u32[]{:S(2)}) %all-to-all-start) | async-done | bytes 1576992 | tf_op jit(solution)/shard_map/all_to_all | solution.py:14
  66.7 0.0 copy-start
  66.7 0.3 slice_reduce_fusion.3
  67.0 28.9 %all-gather.2.cloned.1.call-done = f32[1024,1026]{1,0:T(8,128)} async-done(((f32[32,1026]{1,0:T(8,128)}), f32[1024,1026]{1,0:T(8,128)}) %all-gather.2.cloned.1.call-update) | async-done | bytes 4202512 | tf_op jit(solution)/shard_map/all_gather | solution.py:42
  95.9 1.8 slice_reduce_fusion.1
  97.7 0.0 copy-done
  97.8 10.1 %fusion.10 = (f32[512]{0:T(512)S(1)}, f32[512,1024]{1,0:T(8,128)S(1)}) fusion(f32[512,1024]{1,0:T(8,128)} %convert_element_type.18, f32[1024]{0:T(1024)S(1)} %get-tuple-element.6, f32[512]{0:T(512)S(1)} %get-tuple-element.8, f32[1024,1026]{1,0:T(8,128)} %all-gather.2.cloned.1.call-done, f32[512,770]{1,0:T(8,128)} %bitcast.25, ...), kind=kOutput, calls=%fused_computation.26 | convolution fusion | flops 4836032000 | bytes 8927232 | tf_op jit(solution)/shard_map/dot_general | solution.py:53
  107.9 0.1 reshape.44
  107.9 3.3 %fusion.6 = f32[512,256]{1,0:T(8,128)S(1)} fusion(f32[512,1024]{1,0:T(8,128)S(1)} %get-tuple-element.10, f32[1024,1026]{1,0:T(8,128)} %all-gather.2.cloned.1.call-done), kind=kOutput, calls=%fused_computation.6 | convolution fusion | flops 1610612736 | bytes 3670016 | tf_op jit(solution)/shard_map/dot_general | solution.py:64
  111.3 0.0 copy-start.1
  111.4 26.8 %all_to_all.30 = f32[16,40,256]{2,1,0:T(8,128)S(1)} all-to-all(f32[16,40,256]{2,1,0:T(8,128)S(1)} %select_maximum_fusion), channel_id=1, replica_groups=mesh['zh'=4,'x'=4,'core'=2,'col'=16] {'col'}, dimensions={0} | all-to-all | bytes 1310720 | tf_op jit(solution)/shard_map/all_to_all | solution.py:28
  138.2 0.0 copy-done.1
  138.2 0.1 fusion.9
  138.3 21.1 %all_to_all.31 = f32[16,32,256]{2,1,0:T(8,128)S(1)} all-to-all(f32[16,32,256]{2,1,0:T(8,128)S(1)} %broadcast_in_dim.16), channel_id=1, replica_groups=mesh['zh'=4,'x'=4,'core'=2,'col'=16] {'zh','x'}, dimensions={0} | all-to-all | bytes 1048576 | tf_op jit(solution)/shard_map/all_to_all | solution.py:20
  159.5 2.1 collective-permute-start
  161.6 1.9 copy.22
  163.4 2.7 %fusion.2 = f32[512,2,16,32]{0,3,1,2:T(8,128)S(1)} fusion(f32[512,16,2,32]{0,3,2,1:T(8,128)} %bitcast.26, pred[]{:T(512)S(6)} %eq.3), kind=kLoop, calls=%fused_computation.3 | loop fusion | flops 524288 | bytes 4194305 | tf_op jit(solution)/shard_map/transpose | solution.py:58
  166.2 7.6 %copy.23 = f32[512,2,16,32]{3,2,1,0:T(8,128)} copy(f32[512,2,16,32]{0,3,1,2:T(8,128)S(1)} %fusion.2) | data formatting | bytes 4194304 | tf_op jit(solution)/shard_map/transpose | solution.py:58
  173.8 6.6 %dot_general.15 = f32[16,32,1024]{2,1,0:T(8,128)S(1)} reshape(f32[512,2,16,32]{3,2,1,0:T(8,128)} %copy.23) | data formatting | bytes 4194304 | tf_op jit(solution)/shard_map/dot_general | solution.py:64
  180.4 0.0 collective-permute-done
  180.4 0.1 pad_maximum_fusion
  180.5 1.8 fusion.11
  182.3 23.2 %all_to_all.32 = f32[16,32,256]{2,1,0:T(8,128)S(1)} all-to-all(f32[16,32,256]{2,1,0:T(8,128)S(1)} %fusion.11), channel_id=1, replica_groups=mesh['zh'=4,'x'=4,'core'=2,'col'=16] {'col'}, dimensions={0} | all-to-all | bytes 1048576 | tf_op jit(solution)/shard_map/all_to_all | solution.py:28
  205.5 0.1 divide_add_fusion.1
  205.7 18.7 %all_to_all.33 = f32[16,32,256]{2,1,0:T(8,128)S(1)} all-to-all(f32[16,32,256]{2,1,0:T(8,128)S(1)} %broadcast_in_dim.17), channel_id=1, replica_groups=mesh['zh'=4,'x'=4,'core'=2,'col'=16] {'zh','x'}, dimensions={0} | all-to-all | bytes 1048576 | tf_op jit(solution)/shard_map/all_to_all | solution.py:20
  224.3 1.9 collective-permute-start.1
  226.3 1.9 collective-permute-done.1
  228.1 0.1 pad_maximum_fusion.1
  228.2 1.8 fusion.12
  230.0 24.0 %all_to_all.34 = f32[16,32,256]{2,1,0:T(8,128)S(1)} all-to-all(f32[16,32,256]{2,1,0:T(8,128)S(1)} %fusion.12), channel_id=1, replica_groups=mesh['zh'=4,'x'=4,'core'=2,'col'=16] {'col'}, dimensions={0} | all-to-all | bytes 1048576 | tf_op jit(solution)/shard_map/all_to_all | solution.py:28
  254.1 0.7 divide_add_fusion
  (7 shorter events, 0.3 us)
Async XLA Ops:
  6.5 89.4 %all-gather.2.cloned.1.call-start = ((), (), s32[]{:S(2)}) async-start(), calls=%async_computation.6 | async-start | bytes 4866048 | tf_op jit(solution)/shard_map/all_gather | solution.py:42
  13.9 9.5 %copy-start.2 = (s32[16,512]{1,0:T(8,128)S(1)}, s32[16,512]{1,0:T(8,128)}, u32[]{:S(2)}) copy-start(s32[16,512]{1,0:T(8,128)} %param.9) | copy-start | bytes 98308
  13.9 52.8 %all-to-all-start = ((f32[16,32,770]{2,1,0:T(8,128)}), f32[16,32,770]{2,1,0:T(8,128)S(1)}, u32[]{:S(2)}, u32[]{:S(2)}) async-start(f32[16,32,770]{2,1,0:T(8,128)} %broadcast_in_dim.14), calls=%async_computation | async-start | bytes 3670016 | tf_op jit(solution)/shard_map/all_to_all | solution.py:14
  66.7 31.1 %copy-start = (f32[16,32,770]{2,1,0:T(8,128)}, f32[16,32,770]{2,1,0:T(8,128)S(1)}, u32[]{:S(2)}) copy-start(f32[16,32,770]{2,1,0:T(8,128)S(1)} %all-to-all-done) | copy-start | bytes 4730884
  111.3 26.9 %copy-start.1 = (f32[32,256]{1,0:T(8,128)S(1)}, f32[32,256]{1,0:T(8,128)}, u32[]{:S(2)}) copy-start(f32[32,256]{1,0:T(8,128)} %param.7) | copy-start | bytes 98308
  159.5 21.0 %collective-permute-start = (f32[16,32,256]{2,1,0:T(8,128)S(1)}, f32[16,32,256]{2,1,0:T(8,128)S(1)}, u32[]{:S(2)}, u32[]{:S(2)}) collective-permute-start(f32[16,32,256]{2,1,0:T(8,128)S(1)} %all_to_all.31), channel_id=1, source_target_pairs={{0,16},{16,0},{1,17},{17,1},{2,18},{18,2},{3,19},{19,3},{4,20},{20... | collective-permute-start | bytes 1572872 | tf_op jit(solution)/shard_map/ppermute | solution.py:21
  224.3 3.8 %collective-permute-start.1 = (f32[16,32,256]{2,1,0:T(8,128)S(1)}, f32[16,32,256]{2,1,0:T(8,128)S(1)}, u32[]{:S(2)}, u32[]{:S(2)}) collective-permute-start(f32[16,32,256]{2,1,0:T(8,128)S(1)} %all_to_all.33), channel_id=1, source_target_pairs={{0,16},{16,0},{1,17},{17,1},{2,18},{18,2},{3,19},{19,3},{4,20},{20... | collective-permute-start | bytes 1572872 | tf_op jit(solution)/shard_map/ppermute | solution.py:21
Sparse Core Ops, SparseCore 0:
  11.6 84.2 all-gather.1

commit v6 on v5

--- a/solution.py
+++ b/solution.py
@@ -19,7 +19,8 @@
     copies = jnp.broadcast_to(x[None], (n_chips,) + x.shape)
     mine = lax.all_to_all(copies, CHIPS, 0, 0, tiled=False)
     other = lax.ppermute(mine, "core", [(0, 1), (1, 0)])
-    both = jnp.concatenate([mine, other], axis=0)
+    core0 = lax.axis_index("core") == 0
+    both = jnp.stack([jnp.where(core0, mine, other), jnp.where(core0, other, mine)], axis=1)
     return both.reshape((2 * n_chips * x.shape[0],) + x.shape[1:])
 
 
@@ -33,7 +34,6 @@
     n_chips = lax.axis_size(CHIPS)
     n_col = lax.axis_size("col")
     col_index = lax.axis_index("col")
-    core = lax.axis_index("core")
     piece, width = embeddings.shape
     n_labels = soft_labels.shape[1]
     seeded = seed_mask.astype(jnp.float32)[:, None] * soft_labels
@@ -53,16 +53,13 @@
     cross = jnp.dot(row_emb, col_emb.T, precision=lax.Precision.HIGHEST, preferred_element_type=jnp.float32)
     distance = row_squares[:, None] + col_squares[None, :] - 2.0 * cross
     weights = jnp.exp(-(distance * row_width[:, None] * col_width[None, :])) * col_mask
-    split = weights.reshape(block_rows, n_chips, 2, piece)
-    split = jnp.where(core == 0, split, split[:, :, ::-1, :])
-    split = jnp.transpose(split, (0, 2, 1, 3)).reshape(block_rows, col_rows)
     degree = None
     labels = seeded
     for iteration in range(ITERS):
         if iteration > 0:
             col_labels = gather_row_set(labels, n_chips)
         partial_value = jnp.dot(
-            split if iteration > 0 else weights, col_labels, precision=lax.Precision.HIGHEST, preferred_element_type=jnp.float32
+            weights, col_labels, precision=lax.Precision.HIGHEST, preferred_element_type=jnp.float32
         )
         if degree is None:
             row_sums = jnp.sum(weights, axis=1).reshape(n_col, 1, piece)

time: 263 us -> 245 us (0.932)
  local copies, waits for them, and re-layouts: 34.6 us -> 18.5 us
    transpose x1 -> x0, local copies, waits for them, and re-layouts: 7.62 us -> none  [local(): split = jnp.transpose(split, (0, 2, 1, 3)).reshape(block_rows, col_rows)]
    dot_general x1 -> x0, local copies, waits for them, and re-layouts: 6.63 us -> none  [local(): jnp.dot(split if iteration > 0 else weights, col_labels, precision=lax.Pr...]
    transpose x1 -> x0, other arithmetic: 2.73 us -> none  [local(): split = jnp.transpose(split, (0, 2, 1, 3)).reshape(block_rows, col_rows)]
  transfers between devices with their start and end apart: 4 -> 4, of which waited for: 3 -> 4; matrix products, arithmetic and copies ran while one was open for 13% -> 6% of each run, Pallas kernels for 0% -> 0%
where the time goes in v6:
time: 245 us; the launch traced here: 244 us
  blocking collectives  113 us (46%)
  waiting for transfers between devices  63.3 us (26%)
  local copies, waits for them, and re-layouts  18.5 us (8%)
  matrix products  17.1 us (7%)
  between operations  13.6 us (6%)
  starting transfers between devices  13.5 us (6%)
  other arithmetic  5.11 us (2%)
    all_to_all x3, blocking collectives, scatter_sum(): lax.all_to_all(p.reshape((n, chunk) + p.shape[1:]), axis, 0, 0, tiled=False)  73.9 us
    all_to_all x2, blocking collectives, gather_row_set(): mine = lax.all_to_all(copies, CHIPS, 0, 0, tiled=False)  39.4 us
    all_to_all x1, waiting for transfers between devices, gather_rows(): got = lax.all_to_all(copies, axis, 0, 0, tiled=False)  30.8 us
    all_gather x1, waiting for transfers between devices, local(): lax.all_gather(jnp.concatenate([packed, seeded], axis=1), ('zh', 'x', 'co...  28.9 us
    dot_general x1, matrix products, local(): jnp.dot(row_emb, col_emb.T, precision=lax.Precision.HIGHEST, preferred_el...  10.1 us
    all_to_all x1, starting transfers between devices, gather_rows(): got = lax.all_to_all(copies, axis, 0, 0, tiled=False)  9.5 us
    convert_element_type x1, local copies, waits for them, and re-layouts, local(): col_mask = col_mask.reshape(block_rows, col_rows).astype(jnp.float32)  7.75 us
    dot_general x3, matrix products, local(): jnp.dot(weights, col_labels, precision=lax.Precision.HIGHEST, preferred_e...  6.95 us
  transfers between devices with their start and end apart: 4, of which 4 were waited for; matrix products, arithmetic and copies ran while one was open for 6% of the time, Pallas kernels for 0%

profile of v6, /device:TPU:8, one launch (start us, length us, event | category | flops | bytes accessed | tf_op | source)
XLA Modules:
  0.0 244.4 jit_solution(6137486558375386604)
XLA Ops:
  6.5 0.0 all-gather.2.cloned.1.call-start
  6.5 0.7 convert_element_type.15
  7.2 1.0 multiply_reduce_fusion
  8.2 0.1 copy.20
  8.3 0.7 copy.19
  9.0 0.8 broadcast_multiply_fusion
  9.9 1.6 concatenate.11
  11.5 0.0 all-gather.2.cloned.1.call-update
  11.5 1.0 pad_maximum_fusion.2
  12.5 1.4 broadcast_in_dim.14
  13.9 0.0 copy-start.2
  13.9 9.5 %all-to-all-start = ((f32[16,32,770]{2,1,0:T(8,128)}), f32[16,32,770]{2,1,0:T(8,128)S(1)}, u32[]{:S(2)}, u32[]{:S(2)}) async-start(f32[16,32,770]{2,1,0:T(8,128)} %broadcast_in_dim.14), calls=%async_computation | async-start | bytes 3670016 | tf_op jit(solution)/shard_map/all_to_all | solution.py:14
  23.4 0.0 copy-done.2
  23.4 0.1 reshape.35
  23.5 0.3 convert_reduce_fusion
  23.8 4.4 %broadcast_in_dim.15 = f32[16,32,32,32]{3,2,1,0:T(8,128)} broadcast(f32[16,32]{1,0:T(8,128)S(1)} %convert_reduce_fusion), dimensions={0,2} | broadcast | bytes 2099200 | tf_op jit(solution)/shard_map/broadcast_in_dim | solution.py:51
  28.2 7.8 %convert_element_type.18 = f32[512,1024]{1,0:T(8,128)} reshape(f32[16,32,32,32]{3,2,1,0:T(8,128)} %broadcast_in_dim.15) | data formatting | bytes 4194304 | tf_op jit(solution)/shard_map/convert_element_type | solution.py:52
  35.9 30.8 %all-to-all-done = f32[16,32,770]{2,1,0:T(8,128)S(1)} async-done(((f32[16,32,770]{2,1,0:T(8,128)}), f32[16,32,770]{2,1,0:T(8,128)S(1)}, u32[]{:S(2)}, u32[]{:S(2)}) %all-to-all-start) | async-done | bytes 1576992 | tf_op jit(solution)/shard_map/all_to_all | solution.py:14
  66.7 0.0 copy-start
  66.7 0.3 slice_reduce_fusion.3
  67.0 28.9 %all-gather.2.cloned.1.call-done = f32[1024,1026]{1,0:T(8,128)} async-done(((f32[32,1026]{1,0:T(8,128)}), f32[1024,1026]{1,0:T(8,128)}) %all-gather.2.cloned.1.call-update) | async-done | bytes 4202512 | tf_op jit(solution)/shard_map/all_gather | solution.py:42
  95.9 1.8 slice_reduce_fusion.1
  97.7 0.0 copy-done
  97.8 10.1 %fusion.9 = (f32[512]{0:T(512)S(1)}, f32[512,1024]{1,0:T(8,128)S(1)}) fusion(f32[512,1024]{1,0:T(8,128)} %convert_element_type.18, f32[1024]{0:T(1024)S(1)} %get-tuple-element.6, f32[512]{0:T(512)S(1)} %get-tuple-element.8, f32[1024,1026]{1,0:T(8,128)} %all-gather.2.cloned.1.call-done, f32[512,770]{1,0:T(8,128)} %bitcast.33, ...), kind=kOutput, calls=%fused_computation.28 | convolution fusion | flops 4836032000 | bytes 8927232 | tf_op jit(solution)/shard_map/dot_general | solution.py:53
  107.9 0.1 reshape.37
  107.9 3.3 %fusion.5 = f32[512,256]{1,0:T(8,128)S(1)} fusion(f32[512,1024]{1,0:T(8,128)S(1)} %get-tuple-element.14, f32[1024,1026]{1,0:T(8,128)} %all-gather.2.cloned.1.call-done), kind=kOutput, calls=%fused_computation.4 | convolution fusion | flops 1610612736 | bytes 3670016 | tf_op jit(solution)/shard_map/dot_general | solution.py:61
  111.3 0.0 copy-start.1
  111.4 26.8 %all_to_all.30 = f32[16,40,256]{2,1,0:T(8,128)S(1)} all-to-all(f32[16,40,256]{2,1,0:T(8,128)S(1)} %select_maximum_fusion), channel_id=1, replica_groups=mesh['zh'=4,'x'=4,'core'=2,'col'=16] {'col'}, dimensions={0} | all-to-all | bytes 1310720 | tf_op jit(solution)/shard_map/all_to_all | solution.py:29
  138.2 0.0 copy-done.1
  138.2 0.1 fusion.8
  138.3 21.1 %all_to_all.31 = f32[16,32,256]{2,1,0:T(8,128)S(1)} all-to-all(f32[16,32,256]{2,1,0:T(8,128)S(1)} %broadcast_in_dim.16), channel_id=1, replica_groups=mesh['zh'=4,'x'=4,'core'=2,'col'=16] {'zh','x'}, dimensions={0} | all-to-all | bytes 1048576 | tf_op jit(solution)/shard_map/all_to_all | solution.py:20
  159.5 2.1 collective-permute-start
  161.6 1.7 collective-permute-done
  163.2 0.1 select_bitcast_fusion.3
  163.3 0.1 pad_maximum_fusion
  163.4 1.8 fusion.10
  165.2 22.8 %all_to_all.32 = f32[16,32,256]{2,1,0:T(8,128)S(1)} all-to-all(f32[16,32,256]{2,1,0:T(8,128)S(1)} %fusion.10), channel_id=1, replica_groups=mesh['zh'=4,'x'=4,'core'=2,'col'=16] {'col'}, dimensions={0} | all-to-all | bytes 1048576 | tf_op jit(solution)/shard_map/all_to_all | solution.py:29
  188.1 0.1 divide_add_fusion.1
  188.2 18.3 %all_to_all.33 = f32[16,32,256]{2,1,0:T(8,128)S(1)} all-to-all(f32[16,32,256]{2,1,0:T(8,128)S(1)} %broadcast_in_dim.17), channel_id=1, replica_groups=mesh['zh'=4,'x'=4,'core'=2,'col'=16] {'zh','x'}, dimensions={0} | all-to-all | bytes 1048576 | tf_op jit(solution)/shard_map/all_to_all | solution.py:20
  206.5 1.9 collective-permute-start.1
  208.4 1.9 collective-permute-done.1
  210.3 0.1 select_bitcast_fusion.1
  210.4 0.1 pad_maximum_fusion.1
  210.5 0.1 copy.24
  210.6 1.8 fusion.11
  212.4 24.3 %all_to_all.34 = f32[16,32,256]{2,1,0:T(8,128)S(1)} all-to-all(f32[16,32,256]{2,1,0:T(8,128)S(1)} %fusion.11), channel_id=1, replica_groups=mesh['zh'=4,'x'=4,'core'=2,'col'=16] {'col'}, dimensions={0} | all-to-all | bytes 1048576 | tf_op jit(solution)/shard_map/all_to_all | solution.py:29
  236.8 0.7 divide_add_fusion
  (7 shorter events, 0.3 us)
Async XLA Ops:
  6.5 89.4 %all-gather.2.cloned.1.call-start = ((), (), s32[]{:S(2)}) async-start(), calls=%async_computation.6 | async-start | bytes 4866048 | tf_op jit(solution)/shard_map/all_gather | solution.py:42
  13.9 9.5 %copy-start.2 = (s32[16,512]{1,0:T(8,128)S(1)}, s32[16,512]{1,0:T(8,128)}, u32[]{:S(2)}) copy-start(s32[16,512]{1,0:T(8,128)} %param.9) | copy-start | bytes 98308
  13.9 52.8 %all-to-all-start = ((f32[16,32,770]{2,1,0:T(8,128)}), f32[16,32,770]{2,1,0:T(8,128)S(1)}, u32[]{:S(2)}, u32[]{:S(2)}) async-start(f32[16,32,770]{2,1,0:T(8,128)} %broadcast_in_dim.14), calls=%async_computation | async-start | bytes 3670016 | tf_op jit(solution)/shard_map/all_to_all | solution.py:14
  66.7 31.1 %copy-start = (f32[16,32,770]{2,1,0:T(8,128)}, f32[16,32,770]{2,1,0:T(8,128)S(1)}, u32[]{:S(2)}) copy-start(f32[16,32,770]{2,1,0:T(8,128)S(1)} %all-to-all-done) | copy-start | bytes 4730884
  111.3 26.9 %copy-start.1 = (f32[32,256]{1,0:T(8,128)S(1)}, f32[32,256]{1,0:T(8,128)}, u32[]{:S(2)}) copy-start(f32[32,256]{1,0:T(8,128)} %param.7) | copy-start | bytes 98308
  159.5 3.8 %collective-permute-start = (f32[16,32,256]{2,1,0:T(8,128)S(1)}, f32[16,32,256]{2,1,0:T(8,128)S(1)}, u32[]{:S(2)}, u32[]{:S(2)}) collective-permute-start(f32[16,32,256]{2,1,0:T(8,128)S(1)} %all_to_all.31), channel_id=1, source_target_pairs={{0,16},{16,0},{1,17},{17,1},{2,18},{18,2},{3,19},{19,3},{4,20},{20... | collective-permute-start | bytes 1572872 | tf_op jit(solution)/shard_map/ppermute | solution.py:21
  206.5 3.8 %collective-permute-start.1 = (f32[16,32,256]{2,1,0:T(8,128)S(1)}, f32[16,32,256]{2,1,0:T(8,128)S(1)}, u32[]{:S(2)}, u32[]{:S(2)}) collective-permute-start(f32[16,32,256]{2,1,0:T(8,128)S(1)} %all_to_all.33), channel_id=1, source_target_pairs={{0,16},{16,0},{1,17},{17,1},{2,18},{18,2},{3,19},{19,3},{4,20},{20... | collective-permute-start | bytes 1572872 | tf_op jit(solution)/shard_map/ppermute | solution.py:21
Sparse Core Ops, SparseCore 0:
  11.6 84.2 all-gather.1

commit v7 on v6

--- a/solution.py
+++ b/solution.py
@@ -59,7 +59,7 @@
         if iteration > 0:
             col_labels = gather_row_set(labels, n_chips)
         partial_value = jnp.dot(
-            weights, col_labels, precision=lax.Precision.HIGHEST, preferred_element_type=jnp.float32
+            weights, col_labels, precision=lax.Precision.HIGH, preferred_element_type=jnp.float32
         )
         if degree is None:
             row_sums = jnp.sum(weights, axis=1).reshape(n_col, 1, piece)

time: 245 us -> 243 us (level)
  no operation moved by 1% of the time
where the time goes in v7:
time: 243 us; the launch traced here: 242 us
  blocking collectives  113 us (47%)
  waiting for transfers between devices  63.4 us (26%)
  local copies, waits for them, and re-layouts  18.5 us (8%)
  matrix products  14.7 us (6%)
  between operations  13.6 us (6%)
  starting transfers between devices  13.3 us (5%)
  other arithmetic  5.11 us (2%)
    all_to_all x3, blocking collectives, scatter_sum(): lax.all_to_all(p.reshape((n, chunk) + p.shape[1:]), axis, 0, 0, tiled=False)  73.9 us
    all_to_all x2, blocking collectives, gather_row_set(): mine = lax.all_to_all(copies, CHIPS, 0, 0, tiled=False)  39.5 us
    all_to_all x1, waiting for transfers between devices, gather_rows(): got = lax.all_to_all(copies, axis, 0, 0, tiled=False)  30.8 us
    all_gather x1, waiting for transfers between devices, local(): lax.all_gather(jnp.concatenate([packed, seeded], axis=1), ('zh', 'x', 'co...  28.9 us
    dot_general x1, matrix products, local(): jnp.dot(row_emb, col_emb.T, precision=lax.Precision.HIGHEST, preferred_el...  10.1 us
    all_to_all x1, starting transfers between devices, gather_rows(): got = lax.all_to_all(copies, axis, 0, 0, tiled=False)  9.5 us
    convert_element_type x1, local copies, waits for them, and re-layouts, local(): col_mask = col_mask.reshape(block_rows, col_rows).astype(jnp.float32)  7.75 us
  transfers between devices with their start and end apart: 4, of which 4 were waited for; matrix products, arithmetic and copies ran while one was open for 6% of the time, Pallas kernels for 0%

profile of v7, /device:TPU:8, one launch (start us, length us, event | category | flops | bytes accessed | tf_op | source)
XLA Modules:
  0.0 242.0 jit_solution(14553740756757064827)
XLA Ops:
  6.5 0.0 all-gather.2.cloned.1.call-start
  6.5 0.7 convert_element_type.15
  7.2 1.0 multiply_reduce_fusion
  8.2 0.1 copy.20
  8.3 0.7 copy.19
  9.0 0.8 broadcast_multiply_fusion
  9.9 1.6 concatenate.11
  11.5 0.0 all-gather.2.cloned.1.call-update
  11.5 1.0 pad_maximum_fusion.2
  12.5 1.4 broadcast_in_dim.14
  13.9 0.0 copy-start.2
  13.9 9.5 %all-to-all-start = ((f32[16,32,770]{2,1,0:T(8,128)}), f32[16,32,770]{2,1,0:T(8,128)S(1)}, u32[]{:S(2)}, u32[]{:S(2)}) async-start(f32[16,32,770]{2,1,0:T(8,128)} %broadcast_in_dim.14), calls=%async_computation | async-start | bytes 3670016 | tf_op jit(solution)/shard_map/all_to_all | solution.py:14
  23.4 0.0 copy-done.2
  23.4 0.1 reshape.35
  23.5 0.3 convert_reduce_fusion
  23.8 4.4 %broadcast_in_dim.15 = f32[16,32,32,32]{3,2,1,0:T(8,128)} broadcast(f32[16,32]{1,0:T(8,128)S(1)} %convert_reduce_fusion), dimensions={0,2} | broadcast | bytes 2099200 | tf_op jit(solution)/shard_map/broadcast_in_dim | solution.py:51
  28.2 7.8 %convert_element_type.18 = f32[512,1024]{1,0:T(8,128)} reshape(f32[16,32,32,32]{3,2,1,0:T(8,128)} %broadcast_in_dim.15) | data formatting | bytes 4194304 | tf_op jit(solution)/shard_map/convert_element_type | solution.py:52
  35.9 30.8 %all-to-all-done = f32[16,32,770]{2,1,0:T(8,128)S(1)} async-done(((f32[16,32,770]{2,1,0:T(8,128)}), f32[16,32,770]{2,1,0:T(8,128)S(1)}, u32[]{:S(2)}, u32[]{:S(2)}) %all-to-all-start) | async-done | bytes 1576992 | tf_op jit(solution)/shard_map/all_to_all | solution.py:14
  66.7 0.0 copy-start
  66.7 0.3 slice_reduce_fusion.3
  67.0 28.9 %all-gather.2.cloned.1.call-done = f32[1024,1026]{1,0:T(8,128)} async-done(((f32[32,1026]{1,0:T(8,128)}), f32[1024,1026]{1,0:T(8,128)}) %all-gather.2.cloned.1.call-update) | async-done | bytes 4202512 | tf_op jit(solution)/shard_map/all_gather | solution.py:42
  95.9 1.8 slice_reduce_fusion.1
  97.7 0.0 copy-done
  97.8 10.1 %fusion.9 = (f32[512]{0:T(512)S(1)}, f32[512,1024]{1,0:T(8,128)S(1)}) fusion(f32[512,1024]{1,0:T(8,128)} %convert_element_type.18, f32[1024]{0:T(1024)S(1)} %get-tuple-element.6, f32[512]{0:T(512)S(1)} %get-tuple-element.8, f32[1024,1026]{1,0:T(8,128)} %all-gather.2.cloned.1.call-done, f32[512,770]{1,0:T(8,128)} %bitcast.33, ...), kind=kOutput, calls=%fused_computation.28 | convolution fusion | flops 4836032000 | bytes 8927232 | tf_op jit(solution)/shard_map/dot_general | solution.py:53
  107.9 0.1 reshape.37
  107.9 2.5 %fusion.5 = f32[512,256]{1,0:T(8,128)S(1)} fusion(f32[512,1024]{1,0:T(8,128)S(1)} %get-tuple-element.14, f32[1024,1026]{1,0:T(8,128)} %all-gather.2.cloned.1.call-done), kind=kOutput, calls=%fused_computation.4 | convolution fusion | flops 805306368 | bytes 3670016 | tf_op jit(solution)/shard_map/dot_general | solution.py:61
  110.5 0.0 copy-start.1
  110.6 26.8 %all_to_all.30 = f32[16,40,256]{2,1,0:T(8,128)S(1)} all-to-all(f32[16,40,256]{2,1,0:T(8,128)S(1)} %select_maximum_fusion), channel_id=1, replica_groups=mesh['zh'=4,'x'=4,'core'=2,'col'=16] {'col'}, dimensions={0} | all-to-all | bytes 1310720 | tf_op jit(solution)/shard_map/all_to_all | solution.py:29
  137.4 0.0 copy-done.1
  137.4 0.1 fusion.8
  137.5 21.2 %all_to_all.31 = f32[16,32,256]{2,1,0:T(8,128)S(1)} all-to-all(f32[16,32,256]{2,1,0:T(8,128)S(1)} %broadcast_in_dim.16), channel_id=1, replica_groups=mesh['zh'=4,'x'=4,'core'=2,'col'=16] {'zh','x'}, dimensions={0} | all-to-all | bytes 1048576 | tf_op jit(solution)/shard_map/all_to_all | solution.py:20
  158.7 1.9 collective-permute-start
  160.6 1.9 collective-permute-done
  162.5 0.1 select_bitcast_fusion.3
  162.6 0.1 pad_maximum_fusion
  162.7 1.0 fusion.10
  163.7 22.7 %all_to_all.32 = f32[16,32,256]{2,1,0:T(8,128)S(1)} all-to-all(f32[16,32,256]{2,1,0:T(8,128)S(1)} %fusion.10), channel_id=1, replica_groups=mesh['zh'=4,'x'=4,'core'=2,'col'=16] {'col'}, dimensions={0} | all-to-all | bytes 1048576 | tf_op jit(solution)/shard_map/all_to_all | solution.py:29
  186.5 0.1 divide_add_fusion.1
  186.6 18.3 %all_to_all.33 = f32[16,32,256]{2,1,0:T(8,128)S(1)} all-to-all(f32[16,32,256]{2,1,0:T(8,128)S(1)} %broadcast_in_dim.17), channel_id=1, replica_groups=mesh['zh'=4,'x'=4,'core'=2,'col'=16] {'zh','x'}, dimensions={0} | all-to-all | bytes 1048576 | tf_op jit(solution)/shard_map/all_to_all | solution.py:20
  204.9 1.9 collective-permute-start.1
  206.9 1.9 collective-permute-done.1
  208.7 0.1 select_bitcast_fusion.1
  208.8 0.1 pad_maximum_fusion.1
  209.0 0.1 copy.24
  209.0 1.0 fusion.11
  210.1 24.3 %all_to_all.34 = f32[16,32,256]{2,1,0:T(8,128)S(1)} all-to-all(f32[16,32,256]{2,1,0:T(8,128)S(1)} %fusion.11), channel_id=1, replica_groups=mesh['zh'=4,'x'=4,'core'=2,'col'=16] {'col'}, dimensions={0} | all-to-all | bytes 1048576 | tf_op jit(solution)/shard_map/all_to_all | solution.py:29
  234.5 0.7 divide_add_fusion
  (7 shorter events, 0.3 us)
Async XLA Ops:
  6.5 89.4 %all-gather.2.cloned.1.call-start = ((), (), s32[]{:S(2)}) async-start(), calls=%async_computation.6 | async-start | bytes 4866048 | tf_op jit(solution)/shard_map/all_gather | solution.py:42
  13.9 9.5 %copy-start.2 = (s32[16,512]{1,0:T(8,128)S(1)}, s32[16,512]{1,0:T(8,128)}, u32[]{:S(2)}) copy-start(s32[16,512]{1,0:T(8,128)} %param.9) | copy-start | bytes 98308
  13.9 52.8 %all-to-all-start = ((f32[16,32,770]{2,1,0:T(8,128)}), f32[16,32,770]{2,1,0:T(8,128)S(1)}, u32[]{:S(2)}, u32[]{:S(2)}) async-start(f32[16,32,770]{2,1,0:T(8,128)} %broadcast_in_dim.14), calls=%async_computation | async-start | bytes 3670016 | tf_op jit(solution)/shard_map/all_to_all | solution.py:14
  66.7 31.1 %copy-start = (f32[16,32,770]{2,1,0:T(8,128)}, f32[16,32,770]{2,1,0:T(8,128)S(1)}, u32[]{:S(2)}) copy-start(f32[16,32,770]{2,1,0:T(8,128)S(1)} %all-to-all-done) | copy-start | bytes 4730884
  110.5 26.9 %copy-start.1 = (f32[32,256]{1,0:T(8,128)S(1)}, f32[32,256]{1,0:T(8,128)}, u32[]{:S(2)}) copy-start(f32[32,256]{1,0:T(8,128)} %param.7) | copy-start | bytes 98308
  158.7 3.8 %collective-permute-start = (f32[16,32,256]{2,1,0:T(8,128)S(1)}, f32[16,32,256]{2,1,0:T(8,128)S(1)}, u32[]{:S(2)}, u32[]{:S(2)}) collective-permute-start(f32[16,32,256]{2,1,0:T(8,128)S(1)} %all_to_all.31), channel_id=1, source_target_pairs={{0,16},{16,0},{1,17},{17,1},{2,18},{18,2},{3,19},{19,3},{4,20},{20... | collective-permute-start | bytes 1572872 | tf_op jit(solution)/shard_map/ppermute | solution.py:21
  204.9 3.8 %collective-permute-start.1 = (f32[16,32,256]{2,1,0:T(8,128)S(1)}, f32[16,32,256]{2,1,0:T(8,128)S(1)}, u32[]{:S(2)}, u32[]{:S(2)}) collective-permute-start(f32[16,32,256]{2,1,0:T(8,128)S(1)} %all_to_all.33), channel_id=1, source_target_pairs={{0,16},{16,0},{1,17},{17,1},{2,18},{18,2},{3,19},{19,3},{4,20},{20... | collective-permute-start | bytes 1572872 | tf_op jit(solution)/shard_map/ppermute | solution.py:21
Sparse Core Ops, SparseCore 0:
  11.6 84.2 all-gather.1

commit v8 on v7

--- a/solution.py
+++ b/solution.py
@@ -39,11 +39,11 @@
     seeded = seed_mask.astype(jnp.float32)[:, None] * soft_labels
     squares = jnp.sum(embeddings * embeddings, axis=1)
     packed = jnp.concatenate([embeddings, sharpness[:, None], squares[:, None]], axis=1)
-    col_pack = lax.all_gather(jnp.concatenate([packed, seeded], axis=1), ("zh", "x", "core"), axis=0, tiled=True)
+    col_pack = lax.all_gather(packed, ("zh", "x", "core"), axis=0, tiled=True)
     row_pack = gather_rows(packed, "col", n_col)
+    col_labels = gather_row_set(seeded, n_chips)
     row_emb, row_width, row_squares = row_pack[:, :width], row_pack[:, width], row_pack[:, width + 1]
     col_emb, col_width, col_squares = col_pack[:, :width], col_pack[:, width], col_pack[:, width + 1]
-    col_labels = col_pack[:, width + 2:]
     block_rows = row_emb.shape[0]
     col_rows = col_emb.shape[0]
     grouped = tile_mask.reshape(n_col, 2 * n_chips, n_col)

time: 243 us -> 244 us (level)
  waiting for transfers between devices: 63.4 us -> 31.6 us
  blocking collectives: 113 us -> 142 us
  starting transfers between devices: 13.3 us -> 18.8 us
    all_gather x1, waiting for transfers between devices: 28.9 us -> 0.02 us  [local(): col_pack = lax.all_gather(packed, ('zh', 'x', 'core'), axis=0, tiled=True)]
    all_to_all x2 -> x3, blocking collectives: 39.5 us -> 64.6 us  [gather_row_set(): mine = lax.all_to_all(copies, CHIPS, 0, 0, tiled=False)]
    all_to_all x1, starting transfers between devices: 9.5 us -> 13 us  [gather_rows(): got = lax.all_to_all(copies, axis, 0, 0, tiled=False)]
    all_to_all x3, blocking collectives: 73.9 us -> 77.2 us  [scatter_sum(): lax.all_to_all(p.reshape((n, chunk) + p.shape[1:]), axis, 0, 0, tiled=False)]
    all_to_all x1, waiting for transfers between devices: 30.8 us -> 27.8 us  [gather_rows(): got = lax.all_to_all(copies, axis, 0, 0, tiled=False)]
    ppermute x2 -> x3, starting transfers between devices: 3.82 us -> 5.73 us  [gather_row_set(): other = lax.ppermute(mine, 'core', [(0, 1), (1, 0)])]
  transfers between devices with their start and end apart: 4 -> 5, of which waited for: 4 -> 3; matrix products, arithmetic and copies ran while one was open for 6% -> 7% of each run, Pallas kernels for 0% -> 0%
where the time goes in v8:
time: 244 us; the launch traced here: 243 us
  blocking collectives  142 us (58%)
  waiting for transfers between devices  31.6 us (13%)
  starting transfers between devices  18.8 us (8%)
  local copies, waits for them, and re-layouts  18 us (7%)
  between operations  13.6 us (6%)
  matrix products  13.2 us (5%)
  other arithmetic  5.97 us (2%)
    all_to_all x3, blocking collectives, scatter_sum(): lax.all_to_all(p.reshape((n, chunk) + p.shape[1:]), axis, 0, 0, tiled=False)  77.2 us
    all_to_all x3, blocking collectives, gather_row_set(): mine = lax.all_to_all(copies, CHIPS, 0, 0, tiled=False)  64.6 us
    all_to_all x1, waiting for transfers between devices, gather_rows(): got = lax.all_to_all(copies, axis, 0, 0, tiled=False)  27.8 us
    all_to_all x1, starting transfers between devices, gather_rows(): got = lax.all_to_all(copies, axis, 0, 0, tiled=False)  13 us
    dot_general x1, matrix products, local(): jnp.dot(row_emb, col_emb.T, precision=lax.Precision.HIGHEST, preferred_el...  10.1 us
    convert_element_type x1, local copies, waits for them, and re-layouts, local(): col_mask = col_mask.reshape(block_rows, col_rows).astype(jnp.float32)  7.68 us
    ppermute x3, starting transfers between devices, gather_row_set(): other = lax.ppermute(mine, 'core', [(0, 1), (1, 0)])  5.73 us
  transfers between devices with their start and end apart: 5, of which 3 were waited for; matrix products, arithmetic and copies ran while one was open for 7% of the time, Pallas kernels for 0%

profile of v8, /device:TPU:8, one launch (start us, length us, event | category | flops | bytes accessed | tf_op | source)
XLA Modules:
  0.0 242.9 jit_solution(10983406050684601438)
XLA Ops:
  6.5 0.0 all-gather.2.cloned.1.call-start
  6.5 1.0 multiply_reduce_fusion
  7.5 0.1 copy.18
  7.6 0.7 copy.17
  8.4 1.6 pad_maximum_fusion.3
  10.0 0.0 all-gather.2.cloned.1.call-update
  10.0 0.7 convert_element_type.18
  10.7 0.8 broadcast_multiply_fusion
  11.6 28.3 %all_to_all.35 = f32[16,32,256]{2,1,0:T(8,128)S(1)} all-to-all(f32[16,32,256]{2,1,0:T(8,128)S(1)} %broadcast_in_dim.18), channel_id=1, replica_groups=mesh['zh'=4,'x'=4,'core'=2,'col'=16] {'zh','x'}, dimensions={0} | all-to-all | bytes 1048576 | tf_op jit(solution)/shard_map/all_to_all | solution.py:20
  39.8 2.3 broadcast_in_dim.16
  42.2 13.0 %all-to-all-start = ((f32[16,32,770]{2,1,0:T(8,128)}), f32[16,32,770]{2,1,0:T(8,128)S(1)}, u32[]{:S(2)}, u32[]{:S(2)}) async-start(f32[16,32,770]{2,1,0:T(8,128)} %broadcast_in_dim.16), calls=%async_computation | async-start | bytes 3670016 | tf_op jit(solution)/shard_map/all_to_all | solution.py:14
  55.2 1.9 collective-permute-start
  57.1 0.0 copy-done.2
  57.1 0.1 reshape.38
  57.2 0.3 convert_reduce_fusion
  57.5 4.4 %broadcast_in_dim.17 = f32[16,32,32,32]{3,2,1,0:T(8,128)} broadcast(f32[16,32]{1,0:T(8,128)S(1)} %convert_reduce_fusion), dimensions={0,2} | broadcast | bytes 2099200 | tf_op jit(solution)/shard_map/broadcast_in_dim | solution.py:51
  61.9 7.7 %convert_element_type.17 = f32[512,1024]{1,0:T(8,128)} reshape(f32[16,32,32,32]{3,2,1,0:T(8,128)} %broadcast_in_dim.17) | data formatting | bytes 4194304 | tf_op jit(solution)/shard_map/convert_element_type | solution.py:52
  69.6 0.0 collective-permute-done
  69.6 0.1 select_bitcast_fusion.5
  69.7 0.1 pad_maximum_fusion
  69.7 27.8 %all-to-all-done = f32[16,32,770]{2,1,0:T(8,128)S(1)} async-done(((f32[16,32,770]{2,1,0:T(8,128)}), f32[16,32,770]{2,1,0:T(8,128)S(1)}, u32[]{:S(2)}, u32[]{:S(2)}) %all-to-all-start) | async-done | bytes 1576992 | tf_op jit(solution)/shard_map/all_to_all | solution.py:14
  97.5 0.3 slice_reduce_fusion.3
  97.8 0.0 all-gather.2.cloned.1.call-done
  97.9 2.0 slice_reduce_fusion.1
  99.9 10.1 %fusion.7 = (f32[512]{0:T(512)S(1)}, f32[512,1024]{1,0:T(8,128)S(1)}) fusion(f32[512,1024]{1,0:T(8,128)} %convert_element_type.17, f32[1024]{0:T(1024)S(1)} %get-tuple-element.6, f32[512]{0:T(512)S(1)} %get-tuple-element.8, f32[1024,770]{1,0:T(8,128)} %all-gather.2.cloned.1.call-done, f32[512,770]{1,0:T(8,128)} %bitcast.41, f32[1024]{0:T(1024)S(1)} %get-tuple-element.5, ...), kind=kOutput, calls=%fused_computation.29 | convolution fusion | flops 4836032000 | bytes 8927232 | tf_op jit(solution)/shard_map/dot_general | solution.py:53
  110.0 0.1 reshape.40
  110.1 1.0 fusion.8
  111.1 0.0 copy-start.1
  111.2 29.9 %all_to_all.36 = f32[16,40,256]{2,1,0:T(8,128)S(1)} all-to-all(f32[16,40,256]{2,1,0:T(8,128)S(1)} %select_maximum_fusion), channel_id=1, replica_groups=mesh['zh'=4,'x'=4,'core'=2,'col'=16] {'col'}, dimensions={0} | all-to-all | bytes 1310720 | tf_op jit(solution)/shard_map/all_to_all | solution.py:29
  141.1 0.1 fusion.6
  141.2 18.4 %all_to_all.37 = f32[16,32,256]{2,1,0:T(8,128)S(1)} all-to-all(f32[16,32,256]{2,1,0:T(8,128)S(1)} %broadcast_in_dim.19), channel_id=1, replica_groups=mesh['zh'=4,'x'=4,'core'=2,'col'=16] {'zh','x'}, dimensions={0} | all-to-all | bytes 1048576 | tf_op jit(solution)/shard_map/all_to_all | solution.py:20
  159.6 1.9 collective-permute-start.1
  161.5 1.9 collective-permute-done.1
  163.4 0.1 select_bitcast_fusion.3
  163.5 0.1 pad_maximum_fusion.1
  163.6 0.1 copy.20
  163.7 1.0 fusion.9
  164.7 22.9 %all_to_all.38 = f32[16,32,256]{2,1,0:T(8,128)S(1)} all-to-all(f32[16,32,256]{2,1,0:T(8,128)S(1)} %fusion.9), channel_id=1, replica_groups=mesh['zh'=4,'x'=4,'core'=2,'col'=16] {'col'}, dimensions={0} | all-to-all | bytes 1048576 | tf_op jit(solution)/shard_map/all_to_all | solution.py:29
  187.7 0.1 divide_add_fusion.1
  187.8 18.0 %all_to_all.39 = f32[16,32,256]{2,1,0:T(8,128)S(1)} all-to-all(f32[16,32,256]{2,1,0:T(8,128)S(1)} %broadcast_in_dim.20), channel_id=1, replica_groups=mesh['zh'=4,'x'=4,'core'=2,'col'=16] {'zh','x'}, dimensions={0} | all-to-all | bytes 1048576 | tf_op jit(solution)/shard_map/all_to_all | solution.py:20
  205.8 1.9 collective-permute-start.2
  207.8 1.9 collective-permute-done.2
  209.6 0.1 select_bitcast_fusion.1
  209.7 0.1 pad_maximum_fusion.2
  209.9 0.1 copy.21
  209.9 1.0 fusion.10
  211.0 24.4 %all_to_all.40 = f32[16,32,256]{2,1,0:T(8,128)S(1)} all-to-all(f32[16,32,256]{2,1,0:T(8,128)S(1)} %fusion.10), channel_id=1, replica_groups=mesh['zh'=4,'x'=4,'core'=2,'col'=16] {'col'}, dimensions={0} | all-to-all | bytes 1048576 | tf_op jit(solution)/shard_map/all_to_all | solution.py:29
  235.4 0.7 divide_add_fusion
  (12 shorter events, 0.3 us)
Async XLA Ops:
  6.5 91.3 %all-gather.2.cloned.1.call-start = ((), (), s32[]{:S(2)}) async-start(), calls=%async_computation.7 | async-start | bytes 3784704 | tf_op jit(solution)/shard_map/all_gather | solution.py:42
  42.2 15.0 %copy-start.2 = (s32[16,512]{1,0:T(8,128)S(1)}, s32[16,512]{1,0:T(8,128)}, u32[]{:S(2)}) copy-start(s32[16,512]{1,0:T(8,128)} %param.9) | copy-start | bytes 98308
  42.2 55.4 %all-to-all-start = ((f32[16,32,770]{2,1,0:T(8,128)}), f32[16,32,770]{2,1,0:T(8,128)S(1)}, u32[]{:S(2)}, u32[]{:S(2)}) async-start(f32[16,32,770]{2,1,0:T(8,128)} %broadcast_in_dim.16), calls=%async_computation | async-start | bytes 3670016 | tf_op jit(solution)/shard_map/all_to_all | solution.py:14
  55.2 14.4 %collective-permute-start = (f32[16,32,256]{2,1,0:T(8,128)S(1)}, f32[16,32,256]{2,1,0:T(8,128)S(1)}, u32[]{:S(2)}, u32[]{:S(2)}) collective-permute-start(f32[16,32,256]{2,1,0:T(8,128)S(1)} %all_to_all.35), channel_id=1, source_target_pairs={{0,16},{16,0},{1,17},{17,1},{2,18},{18,2},{3,19},{19,3},{4,20},{20... | collective-permute-start | bytes 1572872 | tf_op jit(solution)/shard_map/ppermute | solution.py:21
  97.5 2.4 copy-start
  111.1 30.0 %copy-start.1 = (f32[32,256]{1,0:T(8,128)S(1)}, f32[32,256]{1,0:T(8,128)}, u32[]{:S(2)}) copy-start(f32[32,256]{1,0:T(8,128)} %param.7) | copy-start | bytes 98308
  159.6 3.8 %collective-permute-start.1 = (f32[16,32,256]{2,1,0:T(8,128)S(1)}, f32[16,32,256]{2,1,0:T(8,128)S(1)}, u32[]{:S(2)}, u32[]{:S(2)}) collective-permute-start(f32[16,32,256]{2,1,0:T(8,128)S(1)} %all_to_all.37), channel_id=1, source_target_pairs={{0,16},{16,0},{1,17},{17,1},{2,18},{18,2},{3,19},{19,3},{4,20},{20... | collective-permute-start | bytes 1572872 | tf_op jit(solution)/shard_map/ppermute | solution.py:21
  205.8 3.8 %collective-permute-start.2 = (f32[16,32,256]{2,1,0:T(8,128)S(1)}, f32[16,32,256]{2,1,0:T(8,128)S(1)}, u32[]{:S(2)}, u32[]{:S(2)}) collective-permute-start(f32[16,32,256]{2,1,0:T(8,128)S(1)} %all_to_all.39), channel_id=1, source_target_pairs={{0,16},{16,0},{1,17},{17,1},{2,18},{18,2},{3,19},{19,3},{4,20},{20... | collective-permute-start | bytes 1572872 | tf_op jit(solution)/shard_map/ppermute | solution.py:21
Sparse Core Ops, SparseCore 0:
  10.5 86.1 all-gather.1

commit v9 on v4

--- a/solution.py
+++ b/solution.py
@@ -15,12 +15,15 @@
     return got.reshape((n * x.shape[0],) + x.shape[1:])
 
 
+def swap_halves(mine):
+    other = lax.ppermute(mine, "core", [(0, 1), (1, 0)])
+    return jnp.concatenate([mine, other], axis=0)
+
+
 def gather_row_set(x, n_chips):
     copies = jnp.broadcast_to(x[None], (n_chips,) + x.shape)
     mine = lax.all_to_all(copies, CHIPS, 0, 0, tiled=False)
-    other = lax.ppermute(mine, "core", [(0, 1), (1, 0)])
-    both = jnp.concatenate([mine, other], axis=0)
-    return both.reshape((2 * n_chips * x.shape[0],) + x.shape[1:])
+    return swap_halves(mine).reshape((2 * n_chips * x.shape[0],) + x.shape[1:])
 
 
 def scatter_sum(p, axis, n):
@@ -33,13 +36,13 @@
     n_chips = lax.axis_size(CHIPS)
     n_col = lax.axis_size("col")
     col_index = lax.axis_index("col")
-    core = lax.axis_index("core")
     piece, width = embeddings.shape
     n_labels = soft_labels.shape[1]
     seeded = seed_mask.astype(jnp.float32)[:, None] * soft_labels
     squares = jnp.sum(embeddings * embeddings, axis=1)
     packed = jnp.concatenate([embeddings, sharpness[:, None], squares[:, None]], axis=1)
-    col_pack = gather_row_set(jnp.concatenate([packed, seeded], axis=1), n_chips)
+    col_pack = lax.all_gather(jnp.concatenate([packed, seeded], axis=1), "x", axis=0, tiled=True)
+    col_pack = swap_halves(lax.all_gather(col_pack, "zh", axis=0, tiled=True))
     row_pack = gather_rows(packed, "col", n_col)
     row_emb, row_width, row_squares = row_pack[:, :width], row_pack[:, width], row_pack[:, width + 1]
     col_emb, col_width, col_squares = col_pack[:, :width], col_pack[:, width], col_pack[:, width + 1]
@@ -48,6 +51,7 @@
     col_rows = col_emb.shape[0]
     grouped = tile_mask.reshape(n_col, n_chips, 2, n_col)
     chosen = lax.dynamic_index_in_dim(grouped, col_index, axis=3, keepdims=False)
+    core = lax.axis_index("core")
     own_half = lax.dynamic_index_in_dim(chosen, core, axis=2, keepdims=False)
     other_half = lax.dynamic_index_in_dim(chosen, 1 - core, axis=2, keepdims=False)
     chosen = jnp.concatenate([own_half, other_half], axis=1)
@@ -62,7 +66,7 @@
         if iteration > 0:
             col_labels = gather_row_set(labels, n_chips)
         partial_value = jnp.dot(
-            weights, col_labels, precision=lax.Precision.HIGHEST, preferred_element_type=jnp.float32
+            weights, col_labels, precision=lax.Precision.HIGH, preferred_element_type=jnp.float32
         )
         if degree is None:
             row_sums = jnp.sum(weights, axis=1).reshape(n_col, 1, piece)

time: 268 us -> 283 us (1.056)
  starting transfers between devices: 43.5 us -> 15.1 us
  blocking collectives: 108 us -> 128 us
  between operations: 0.22 us -> 13.6 us
  local copies, waits for them, and re-layouts: 29.5 us -> 34.4 us
  waiting for transfers between devices: 67.2 us -> 71.2 us
    all_gather x0 -> x1, waiting for transfers between devices: none -> 67.5 us  [local(): col_pack = swap_halves(lax.all_gather(col_pack, 'zh', axis=0, tiled=True))]
    all_to_all x1 -> x0, waiting for transfers between devices: 45.3 us -> none  [gather_row_set(): mine = lax.all_to_all(copies, CHIPS, 0, 0, tiled=False)]
    all_to_all x1, waiting for transfers between devices: 18.4 us -> 0.01 us  [gather_rows(): got = lax.all_to_all(copies, axis, 0, 0, tiled=False)]
    all_to_all x1, starting transfers between devices: 24.6 us -> 9.37 us  [gather_rows(): got = lax.all_to_all(copies, axis, 0, 0, tiled=False)]
    all_gather x0 -> x1, blocking collectives: none -> 14 us  [local(): lax.all_gather(jnp.concatenate([packed, seeded], axis=1), 'x', axis=0, ti...]
    all_to_all x1 -> x0, starting transfers between devices: 13 us -> none  [gather_row_set(): mine = lax.all_to_all(copies, CHIPS, 0, 0, tiled=False)]
    ppermute x0 -> x1, local copies, waits for them, and re-layouts: none -> 3.19 us  [swap_halves(): other = lax.ppermute(mine, 'core', [(0, 1), (1, 0)])]
    all_to_all x3, blocking collectives: 71.5 us -> 74.7 us  [scatter_sum(): lax.all_to_all(p.reshape((n, chunk) + p.shape[1:]), axis, 0, 0, tiled=False)]
  transfers between devices with their start and end apart: 5 -> 5, of which waited for: 4 -> 3; matrix products, arithmetic and copies ran while one was open for 9% -> 10% of each run, Pallas kernels for 0% -> 0%
where the time goes in v9:
time: 283 us; the launch traced here: 282 us
  blocking collectives  128 us (45%)
  waiting for transfers between devices  71.2 us (25%)
  local copies, waits for them, and re-layouts  34.4 us (12%)
  starting transfers between devices  15.1 us (5%)
  matrix products  13.6 us (5%)
  between operations  13.6 us (5%)
  other arithmetic  6.38 us (2%)
    all_to_all x3, blocking collectives, scatter_sum(): lax.all_to_all(p.reshape((n, chunk) + p.shape[1:]), axis, 0, 0, tiled=False)  74.7 us
    all_gather x1, waiting for transfers between devices, local(): col_pack = swap_halves(lax.all_gather(col_pack, 'zh', axis=0, tiled=True))  67.5 us
    all_to_all x2, blocking collectives, gather_row_set(): mine = lax.all_to_all(copies, CHIPS, 0, 0, tiled=False)  38.9 us
    all_gather x1, blocking collectives, local(): lax.all_gather(jnp.concatenate([packed, seeded], axis=1), 'x', axis=0, ti...  14 us
    dynamic_slice x1, local copies, waits for them, and re-layouts, local(): own_half = lax.dynamic_index_in_dim(chosen, core, axis=2, keepdims=False)  10.1 us
    all_to_all x1, starting transfers between devices, gather_rows(): got = lax.all_to_all(copies, axis, 0, 0, tiled=False)  9.37 us
    dot_general x1, matrix products, local(): jnp.dot(row_emb, col_emb.T, precision=lax.Precision.HIGHEST, preferred_el...  8.62 us
    convert_element_type x1, local copies, waits for them, and re-layouts, local(): col_mask = col_mask.reshape(block_rows, col_rows).astype(jnp.float32)  7.71 us
  transfers between devices with their start and end apart: 5, of which 3 were waited for; matrix products, arithmetic and copies ran while one was open for 10% of the time, Pallas kernels for 0%

profile of v9, /device:TPU:8, one launch (start us, length us, event | category | flops | bytes accessed | tf_op | source)
XLA Modules:
  0.0 282.0 jit_solution(4201232136936695940)
XLA Ops:
  6.5 0.7 convert_element_type.12
  7.2 1.0 multiply_reduce_fusion
  8.2 0.1 copy.34
  8.3 0.7 copy.33
  9.0 0.8 broadcast_multiply_fusion
  9.9 1.0 concatenate.23
  10.8 14.0 %all_gather.6 = f32[128,1026]{1,0:T(8,128)} all-gather(f32[32,1026]{1,0:T(8,128)S(1)} %concatenate.23), channel_id=1, replica_groups=mesh['zh'=4,'x'=4,'core'=2,'col'=16] {'x'}, dimensions={0}, use_global_device_ids=true | all-gather | bytes 656640 | tf_op jit(solution)/shard_map/all_gather | solution.py:44
  24.8 0.0 all-gather.2.cloned.1.call-update
  24.9 1.0 pad_maximum_fusion.4
  25.8 1.5 broadcast_in_dim.14
  27.3 9.4 %all-to-all-start = ((f32[16,32,770]{2,1,0:T(8,128)}), f32[16,32,770]{2,1,0:T(8,128)S(1)}, u32[]{:S(2)}, u32[]{:S(2)}) async-start(f32[16,32,770]{2,1,0:T(8,128)} %broadcast_in_dim.14), calls=%async_computation | async-start | bytes 3670016 | tf_op jit(solution)/shard_map/all_to_all | solution.py:14
  36.7 67.5 %all-gather.2.cloned.1.call-done = f32[512,1026]{1,0:T(8,128)} async-done(((f32[128,1026]{1,0:T(8,128)}), f32[512,1026]{1,0:T(8,128)}) %all-gather.2.cloned.1.call-update) | async-done | bytes 2101264 | tf_op jit(solution)/shard_map/all_gather | solution.py:45
  104.1 3.0 %copy.37 = f32[512,1026]{0,1:T(8,128)} copy(f32[512,1026]{1,0:T(8,128)} %all-gather.2.cloned.1.call-done) | data formatting | bytes 4202496 | tf_op jit(solution)/shard_map/all_gather | solution.py:45
  107.1 1.9 collective-permute-start
  109.0 0.0 copy-done.6
  109.1 0.4 reshape.37
  109.5 10.1 %dynamic-slice_reduce_fusion.1 = (s32[16,16]{1,0:T(8,128)S(1)}, s32[16,16]{1,0:T(8,128)S(1)}) fusion(s32[16,16,2,16]{3,2,1,0:T(2,128)S(1)} %reshape.37, s32[]{:T(128)S(6)} %select_n.18, s32[]{:T(128)S(6)} %select_n.20, s32[]{:T(128)S(6)} %select_n.22), kind=kLoop, calls=%fused_computation.21 | loop fusion | bytes 4108 | tf_op jit(solution)/shard_map/jit(dynamic_index_in_dim)/dynamic_slice | solution.py:55
  119.6 0.1 add_convert_fusion
  119.7 4.4 %broadcast_in_dim.15 = f32[16,32,32,32]{3,2,1,0:T(8,128)} broadcast(f32[16,32]{1,0:T(8,128)S(1)} %add_convert_fusion), dimensions={0,2} | broadcast | bytes 2099200 | tf_op jit(solution)/shard_map/broadcast_in_dim | solution.py:58
  124.0 7.7 %convert_element_type.14 = f32[512,1024]{1,0:T(8,128)} reshape(f32[16,32,32,32]{3,2,1,0:T(8,128)} %broadcast_in_dim.15) | data formatting | bytes 4194304 | tf_op jit(solution)/shard_map/convert_element_type | solution.py:59
  131.7 0.0 all-to-all-done
  131.7 1.2 copy-done.3
  132.9 0.3 slice_reduce_fusion.1
  133.3 0.0 collective-permute-done
  133.3 3.2 %copy.38 = f32[512,1026]{1,0:T(8,128)} copy(f32[512,1026]{0,1:T(8,128)} %collective-permute-done) | data formatting | bytes 4202496 | tf_op jit(solution)/shard_map/ppermute | solution.py:19
  136.5 1.7 maximum_reduce_fusion
  138.1 0.1 copy-done.1
  138.3 0.5 copy-done.4
  138.8 8.6 %fusion.16 = (f32[512]{0:T(512)S(1)}, f32[512,1024]{1,0:T(8,128)}) fusion(f32[512,1024]{1,0:T(8,128)} %convert_element_type.14, f32[1024]{0:T(1024)S(1)} %get-tuple-element.6, f32[512]{0:T(512)S(1)} %get-tuple-element.8, f32[512,1026]{1,0:T(8,128)S(1)} %copy-done, f32[512,1026]{1,0:T(8,128)S(1)} %copy-done.1, f32[512,770]{1,0:T(8,128)S(1)} %bitcast.25, ...), kind=kOutput, calls=%fused_computation.34 | convolution fusion | flops 4836818432 | bytes 10500096 | tf_op jit(solution)/shard_map/dot_general | solution.py:60
  147.5 0.1 reshape.39
  147.5 2.9 %fusion.4 = f32[512,256]{1,0:T(8,128)S(1)} fusion(f32[512,1024]{1,0:T(8,128)} %get-tuple-element.12, f32[512,1026]{1,0:T(8,128)} %copy.38, f32[512,1026]{1,0:T(8,128)S(1)} %copy-done), kind=kOutput, calls=%fused_computation.9 | convolution fusion | flops 805568512 | bytes 6823936 | tf_op jit(solution)/shard_map/dot_general | solution.py:68
  150.5 0.0 copy-start.5
  150.5 27.2 %all_to_all.30 = f32[16,40,256]{2,1,0:T(8,128)S(1)} all-to-all(f32[16,40,256]{2,1,0:T(8,128)S(1)} %select_maximum_fusion), channel_id=1, replica_groups=mesh['zh'=4,'x'=4,'core'=2,'col'=16] {'col'}, dimensions={0} | all-to-all | bytes 1310720 | tf_op jit(solution)/shard_map/all_to_all | solution.py:31
  177.9 0.1 fusion.9
  178.0 20.5 %all_to_all.31 = f32[16,32,256]{2,1,0:T(8,128)S(1)} all-to-all(f32[16,32,256]{2,1,0:T(8,128)S(1)} %broadcast_in_dim.16), channel_id=1, replica_groups=mesh['zh'=4,'x'=4,'core'=2,'col'=16] {'zh','x'}, dimensions={0} | all-to-all | bytes 1048576 | tf_op jit(solution)/shard_map/all_to_all | solution.py:25
  198.5 1.9 collective-permute-start.1
  200.4 1.9 collective-permute-done.1
  202.3 0.1 pad_maximum_fusion.2
  202.4 1.0 fusion.17
  203.4 23.1 %all_to_all.32 = f32[16,32,256]{2,1,0:T(8,128)S(1)} all-to-all(f32[16,32,256]{2,1,0:T(8,128)S(1)} %fusion.17), channel_id=1, replica_groups=mesh['zh'=4,'x'=4,'core'=2,'col'=16] {'col'}, dimensions={0} | all-to-all | bytes 1048576 | tf_op jit(solution)/shard_map/all_to_all | solution.py:31
  226.6 0.1 divide_add_fusion.1
  226.7 18.4 %all_to_all.33 = f32[16,32,256]{2,1,0:T(8,128)S(1)} all-to-all(f32[16,32,256]{2,1,0:T(8,128)S(1)} %broadcast_in_dim.17), channel_id=1, replica_groups=mesh['zh'=4,'x'=4,'core'=2,'col'=16] {'zh','x'}, dimensions={0} | all-to-all | bytes 1048576 | tf_op jit(solution)/shard_map/all_to_all | solution.py:25
  245.2 1.9 collective-permute-start.2
  247.1 1.9 collective-permute-done.2
  249.0 0.1 pad_maximum_fusion.3
  249.0 1.0 fusion.18
  250.1 24.3 %all_to_all.34 = f32[16,32,256]{2,1,0:T(8,128)S(1)} all-to-all(f32[16,32,256]{2,1,0:T(8,128)S(1)} %fusion.18), channel_id=1, replica_groups=mesh['zh'=4,'x'=4,'core'=2,'col'=16] {'col'}, dimensions={0} | all-to-all | bytes 1048576 | tf_op jit(solution)/shard_map/all_to_all | solution.py:31
  274.4 0.7 divide_add_fusion
  (17 shorter events, 0.3 us)
Async XLA Ops:
  6.5 97.6 %all-gather.2.cloned.1.call-start = ((), (), s32[]{:S(2)}) async-start(), calls=%async_computation.6 | async-start | bytes 2949120 | tf_op jit(solution)/shard_map/all_gather | solution.py:45
  27.3 104.4 %all-to-all-start = ((f32[16,32,770]{2,1,0:T(8,128)}), f32[16,32,770]{2,1,0:T(8,128)S(1)}, u32[]{:S(2)}, u32[]{:S(2)}) async-start(f32[16,32,770]{2,1,0:T(8,128)} %broadcast_in_dim.14), calls=%async_computation | async-start | bytes 3670016 | tf_op jit(solution)/shard_map/all_to_all | solution.py:14
  36.7 72.4 %copy-start.6 = (s32[16,512]{1,0:T(8,128)S(1)}, s32[16,512]{1,0:T(8,128)}, u32[]{:S(2)}) copy-start(s32[16,512]{1,0:T(8,128)} %param.9) | copy-start | bytes 98308
  107.1 26.1 %collective-permute-start = (f32[512,1026]{0,1:T(8,128)}, f32[512,1026]{0,1:T(8,128)}, u32[]{:S(2)}, u32[]{:S(2)}) collective-permute-start(f32[512,1026]{0,1:T(8,128)} %copy.37), channel_id=1, source_target_pairs={{0,16},{16,0},{1,17},{17,1},{2,18},{18,2},{3,19},{19,3},{4,20},{20... | collective-permute-start | bytes 6303752 | tf_op jit(solution)/shard_map/ppermute | solution.py:19
  131.7 1.2 copy-start.3
  133.2 3.2 %copy-start = (f32[512,1026]{1,0:T(8,128)S(1)}, f32[512,1026]{1,0:T(8,128)}, u32[]{:S(2)}) copy-start(f32[512,1026]{1,0:T(8,128)} %all-gather.2.cloned.1.call-done) | copy-start | bytes 6303748
  136.5 1.8 copy-start.1
  136.5 2.4 copy-start.4
  150.5 27.4 %copy-start.5 = (f32[32,256]{1,0:T(8,128)S(1)}, f32[32,256]{1,0:T(8,128)}, u32[]{:S(2)}) copy-start(f32[32,256]{1,0:T(8,128)} %param.7) | copy-start | bytes 98308
  177.8 24.6 %copy-start.2 = (f32[512,1024]{1,0:T(8,128)S(1)}, f32[512,1024]{1,0:T(8,128)}, u32[]{:S(2)}) copy-start(f32[512,1024]{1,0:T(8,128)} %get-tuple-element.12) | copy-start | bytes 6291460
  198.5 3.8 %collective-permute-start.1 = (f32[16,32,256]{2,1,0:T(8,128)S(1)}, f32[16,32,256]{2,1,0:T(8,128)S(1)}, u32[]{:S(2)}, u32[]{:S(2)}) collective-permute-start(f32[16,32,256]{2,1,0:T(8,128)S(1)} %all_to_all.31), channel_id=1, source_target_pairs={{0,16},{16,0},{1,17},{17,1},{2,18},{18,2},{3,19},{19,3},{4,20},{20... | collective-permute-start | bytes 1572872 | tf_op jit(solution)/shard_map/ppermute | solution.py:19
  245.2 3.8 %collective-permute-start.2 = (f32[16,32,256]{2,1,0:T(8,128)S(1)}, f32[16,32,256]{2,1,0:T(8,128)S(1)}, u32[]{:S(2)}, u32[]{:S(2)}) collective-permute-start(f32[16,32,256]{2,1,0:T(8,128)S(1)} %all_to_all.33), channel_id=1, source_target_pairs={{0,16},{16,0},{1,17},{17,1},{2,18},{18,2},{3,19},{19,3},{4,20},{20... | collective-permute-start | bytes 1572872 | tf_op jit(solution)/shard_map/ppermute | solution.py:19
Sparse Core Ops, SparseCore 0:
  25.0 79.1 all-gather.1

commit v10 on v7

--- a/solution.py
+++ b/solution.py
@@ -37,13 +37,14 @@
     piece, width = embeddings.shape
     n_labels = soft_labels.shape[1]
     seeded = seed_mask.astype(jnp.float32)[:, None] * soft_labels
-    squares = jnp.sum(embeddings * embeddings, axis=1)
-    packed = jnp.concatenate([embeddings, sharpness[:, None], squares[:, None]], axis=1)
+    packed = jnp.concatenate([embeddings, sharpness[:, None]], axis=1)
     col_pack = lax.all_gather(jnp.concatenate([packed, seeded], axis=1), ("zh", "x", "core"), axis=0, tiled=True)
     row_pack = gather_rows(packed, "col", n_col)
-    row_emb, row_width, row_squares = row_pack[:, :width], row_pack[:, width], row_pack[:, width + 1]
-    col_emb, col_width, col_squares = col_pack[:, :width], col_pack[:, width], col_pack[:, width + 1]
-    col_labels = col_pack[:, width + 2:]
+    row_emb, row_width = row_pack[:, :width], row_pack[:, width]
+    col_emb, col_width = col_pack[:, :width], col_pack[:, width]
+    col_labels = col_pack[:, width + 1:]
+    row_squares = jnp.sum(row_emb * row_emb, axis=1)
+    col_squares = jnp.sum(col_emb * col_emb, axis=1)
     block_rows = row_emb.shape[0]
     col_rows = col_emb.shape[0]
     grouped = tile_mask.reshape(n_col, 2 * n_chips, n_col)

time: 243 us -> 242 us (level)
  no operation moved by 1% of the time
where the time goes in v10:
time: 242 us; the launch traced here: 241 us
  blocking collectives  113 us (47%)
  waiting for transfers between devices  63.6 us (26%)
  local copies, waits for them, and re-layouts  17.8 us (7%)
  between operations  13.6 us (6%)
  starting transfers between devices  13.5 us (6%)
  matrix products  12.6 us (5%)
  other arithmetic  6.38 us (3%)
    all_to_all x3, blocking collectives, scatter_sum(): lax.all_to_all(p.reshape((n, chunk) + p.shape[1:]), axis, 0, 0, tiled=False)  73.9 us
    all_to_all x2, blocking collectives, gather_row_set(): mine = lax.all_to_all(copies, CHIPS, 0, 0, tiled=False)  39.4 us
    all_to_all x1, waiting for transfers between devices, gather_rows(): got = lax.all_to_all(copies, axis, 0, 0, tiled=False)  30.8 us
    all_gather x1, waiting for transfers between devices, local(): lax.all_gather(jnp.concatenate([packed, seeded], axis=1), ('zh', 'x', 'co...  29.3 us
    all_to_all x1, starting transfers between devices, gather_rows(): got = lax.all_to_all(copies, axis, 0, 0, tiled=False)  9.5 us
    dot_general x1, matrix products, local(): jnp.dot(row_emb, col_emb.T, precision=lax.Precision.HIGHEST, preferred_el...  8.03 us
    convert_element_type x1, local copies, waits for them, and re-layouts, local(): col_mask = col_mask.reshape(block_rows, col_rows).astype(jnp.float32)  7.75 us
  transfers between devices with their start and end apart: 4, of which 4 were waited for; matrix products, arithmetic and copies ran while one was open for 6% of the time, Pallas kernels for 0%

profile of v10, /device:TPU:8, one launch (start us, length us, event | category | flops | bytes accessed | tf_op | source)
XLA Modules:
  0.0 240.9 jit_solution(10302086116522083841)
XLA Ops:
  6.5 0.0 all-gather.2.cloned.1.call-start
  6.5 0.7 copy.15
  7.3 0.7 convert_element_type.15
  7.9 0.8 broadcast_multiply_fusion
  8.8 1.6 concatenate.11
  10.4 0.0 all-gather.2.cloned.1.call-update
  10.4 0.9 pad_maximum_fusion.2
  11.3 1.4 broadcast_in_dim.11
  12.7 0.0 copy-start.3
  12.7 9.5 %all-to-all-start = ((f32[16,32,769]{2,1,0:T(8,128)}), f32[16,32,769]{2,1,0:T(8,128)S(1)}, u32[]{:S(2)}, u32[]{:S(2)}) async-start(f32[16,32,769]{2,1,0:T(8,128)} %broadcast_in_dim.11), calls=%async_computation | async-start | bytes 3670016 | tf_op jit(solution)/shard_map/all_to_all | solution.py:14
  22.2 0.0 copy-done.3
  22.2 0.1 reshape.36
  22.4 0.3 convert_reduce_fusion
  22.6 4.4 %broadcast_in_dim.12 = f32[16,32,32,32]{3,2,1,0:T(8,128)} broadcast(f32[16,32]{1,0:T(8,128)S(1)} %convert_reduce_fusion), dimensions={0,2} | broadcast | bytes 2099200 | tf_op jit(solution)/shard_map/broadcast_in_dim | solution.py:52
  27.0 7.7 %convert_element_type.18 = f32[512,1024]{1,0:T(8,128)} reshape(f32[16,32,32,32]{3,2,1,0:T(8,128)} %broadcast_in_dim.12) | data formatting | bytes 4194304 | tf_op jit(solution)/shard_map/convert_element_type | solution.py:53
  34.8 30.8 %all-to-all-done = f32[16,32,769]{2,1,0:T(8,128)S(1)} async-done(((f32[16,32,769]{2,1,0:T(8,128)}), f32[16,32,769]{2,1,0:T(8,128)S(1)}, u32[]{:S(2)}, u32[]{:S(2)}) %all-to-all-start) | async-done | bytes 1574944 | tf_op jit(solution)/shard_map/all_to_all | solution.py:14
  65.5 0.0 copy-start
  65.5 0.1 slice_reduce_fusion.1
  65.7 0.2 multiply_reduce_fusion.1
  65.8 29.3 %all-gather.2.cloned.1.call-done = f32[1024,1025]{1,0:T(8,128)} async-done(((f32[32,1025]{1,0:T(8,128)}), f32[1024,1025]{1,0:T(8,128)}) %all-gather.2.cloned.1.call-update) | async-done | bytes 4198416 | tf_op jit(solution)/shard_map/all_gather | solution.py:41
  95.1 1.4 slice_reduce_fusion
  96.5 0.0 copy-done
  96.5 2.2 multiply_reduce_fusion
  98.7 0.0 copy-done.1
  98.7 8.0 %fusion.9 = (f32[512]{0:T(512)S(1)}, f32[512,1024]{1,0:T(8,128)S(1)}) fusion(f32[512,1024]{1,0:T(8,128)S(1)} %copy-done.1, f32[1024]{0:T(1024)S(1)} %slice_reduce_fusion, f32[512]{0:T(512)S(1)} %slice_reduce_fusion.1, f32[1024,1025]{1,0:T(8,128)} %all-gather.2.cloned.1.call-done, f32[512,769]{1,0:T(8,128)} %bitcast.33, f32[1024]{0:T(1024)S(1)} %multiply_reduce_fusion, ...), kind=kOutput, calls=%fused_computation.27 | convolution fusion | flops 4836032000 | bytes 8927232 | tf_op jit(solution)/shard_map/dot_general | solution.py:54
  106.7 0.1 reshape.38
  106.8 2.5 %fusion.5 = f32[512,256]{1,0:T(8,128)S(1)} fusion(f32[512,1024]{1,0:T(8,128)S(1)} %get-tuple-element.10, f32[1024,1025]{1,0:T(8,128)} %all-gather.2.cloned.1.call-done), kind=kOutput, calls=%fused_computation.6 | convolution fusion | flops 805306368 | bytes 3670016 | tf_op jit(solution)/shard_map/dot_general | solution.py:62
  109.4 0.0 copy-start.2
  109.4 26.8 %all_to_all.30 = f32[16,40,256]{2,1,0:T(8,128)S(1)} all-to-all(f32[16,40,256]{2,1,0:T(8,128)S(1)} %select_maximum_fusion), channel_id=1, replica_groups=mesh['zh'=4,'x'=4,'core'=2,'col'=16] {'col'}, dimensions={0} | all-to-all | bytes 1310720 | tf_op jit(solution)/shard_map/all_to_all | solution.py:29
  136.3 0.0 copy-done.2
  136.3 0.1 fusion.8
  136.4 21.1 %all_to_all.31 = f32[16,32,256]{2,1,0:T(8,128)S(1)} all-to-all(f32[16,32,256]{2,1,0:T(8,128)S(1)} %broadcast_in_dim.13), channel_id=1, replica_groups=mesh['zh'=4,'x'=4,'core'=2,'col'=16] {'zh','x'}, dimensions={0} | all-to-all | bytes 1048576 | tf_op jit(solution)/shard_map/all_to_all | solution.py:20
  157.5 2.1 collective-permute-start
  159.6 1.7 collective-permute-done
  161.3 0.1 select_bitcast_fusion.3
  161.4 0.1 pad_maximum_fusion
  161.5 1.0 fusion.10
  162.5 22.8 %all_to_all.32 = f32[16,32,256]{2,1,0:T(8,128)S(1)} all-to-all(f32[16,32,256]{2,1,0:T(8,128)S(1)} %fusion.10), channel_id=1, replica_groups=mesh['zh'=4,'x'=4,'core'=2,'col'=16] {'col'}, dimensions={0} | all-to-all | bytes 1048576 | tf_op jit(solution)/shard_map/all_to_all | solution.py:29
  185.3 0.1 divide_add_fusion.1
  185.5 18.3 %all_to_all.33 = f32[16,32,256]{2,1,0:T(8,128)S(1)} all-to-all(f32[16,32,256]{2,1,0:T(8,128)S(1)} %broadcast_in_dim.14), channel_id=1, replica_groups=mesh['zh'=4,'x'=4,'core'=2,'col'=16] {'zh','x'}, dimensions={0} | all-to-all | bytes 1048576 | tf_op jit(solution)/shard_map/all_to_all | solution.py:20
  203.8 1.9 collective-permute-start.1
  205.7 1.9 collective-permute-done.1
  207.6 0.1 select_bitcast_fusion.1
  207.7 0.1 pad_maximum_fusion.1
  207.8 0.1 copy.18
  207.9 1.0 fusion.11
  209.0 24.3 %all_to_all.34 = f32[16,32,256]{2,1,0:T(8,128)S(1)} all-to-all(f32[16,32,256]{2,1,0:T(8,128)S(1)} %fusion.11), channel_id=1, replica_groups=mesh['zh'=4,'x'=4,'core'=2,'col'=16] {'col'}, dimensions={0} | all-to-all | bytes 1048576 | tf_op jit(solution)/shard_map/all_to_all | solution.py:29
  233.3 0.7 divide_add_fusion
  (8 shorter events, 0.3 us)
Async XLA Ops:
  6.5 88.6 %all-gather.2.cloned.1.call-start = ((), (), s32[]{:S(2)}) async-start(), calls=%async_computation.6 | async-start | bytes 4866048 | tf_op jit(solution)/shard_map/all_gather | solution.py:41
  12.7 9.5 %copy-start.3 = (s32[16,512]{1,0:T(8,128)S(1)}, s32[16,512]{1,0:T(8,128)}, u32[]{:S(2)}) copy-start(s32[16,512]{1,0:T(8,128)} %param.9) | copy-start | bytes 98308
  12.7 52.8 %all-to-all-start = ((f32[16,32,769]{2,1,0:T(8,128)}), f32[16,32,769]{2,1,0:T(8,128)S(1)}, u32[]{:S(2)}, u32[]{:S(2)}) async-start(f32[16,32,769]{2,1,0:T(8,128)} %broadcast_in_dim.11), calls=%async_computation | async-start | bytes 3670016 | tf_op jit(solution)/shard_map/all_to_all | solution.py:14
  65.5 31.0 %copy-start = (f32[16,32,769]{2,1,0:T(8,128)}, f32[16,32,769]{2,1,0:T(8,128)S(1)}, u32[]{:S(2)}) copy-start(f32[16,32,769]{2,1,0:T(8,128)S(1)} %all-to-all-done) | copy-start | bytes 4724740
  95.1 3.6 %copy-start.1 = (f32[512,1024]{1,0:T(8,128)S(1)}, f32[512,1024]{1,0:T(8,128)}, u32[]{:S(2)}) copy-start(f32[512,1024]{1,0:T(8,128)} %convert_element_type.18) | copy-start | bytes 6291460
  109.4 26.9 %copy-start.2 = (f32[32,256]{1,0:T(8,128)S(1)}, f32[32,256]{1,0:T(8,128)}, u32[]{:S(2)}) copy-start(f32[32,256]{1,0:T(8,128)} %param.7) | copy-start | bytes 98308
  157.5 3.8 %collective-permute-start = (f32[16,32,256]{2,1,0:T(8,128)S(1)}, f32[16,32,256]{2,1,0:T(8,128)S(1)}, u32[]{:S(2)}, u32[]{:S(2)}) collective-permute-start(f32[16,32,256]{2,1,0:T(8,128)S(1)} %all_to_all.31), channel_id=1, source_target_pairs={{0,16},{16,0},{1,17},{17,1},{2,18},{18,2},{3,19},{19,3},{4,20},{20... | collective-permute-start | bytes 1572872 | tf_op jit(solution)/shard_map/ppermute | solution.py:21
  203.8 3.8 %collective-permute-start.1 = (f32[16,32,256]{2,1,0:T(8,128)S(1)}, f32[16,32,256]{2,1,0:T(8,128)S(1)}, u32[]{:S(2)}, u32[]{:S(2)}) collective-permute-start(f32[16,32,256]{2,1,0:T(8,128)S(1)} %all_to_all.33), channel_id=1, source_target_pairs={{0,16},{16,0},{1,17},{17,1},{2,18},{18,2},{3,19},{19,3},{4,20},{20... | collective-permute-start | bytes 1572872 | tf_op jit(solution)/shard_map/ppermute | solution.py:21
Sparse Core Ops, SparseCore 0:
  10.5 84.5 all-gather.1

commit v11 on v10

--- a/solution.py
+++ b/solution.py
@@ -38,11 +38,14 @@
     n_labels = soft_labels.shape[1]
     seeded = seed_mask.astype(jnp.float32)[:, None] * soft_labels
     packed = jnp.concatenate([embeddings, sharpness[:, None]], axis=1)
-    col_pack = lax.all_gather(jnp.concatenate([packed, seeded], axis=1), ("zh", "x", "core"), axis=0, tiled=True)
+    seed_column = seed_mask.astype(jnp.float32)[:, None]
+    col_pack = lax.all_gather(
+        jnp.concatenate([packed, seed_column, soft_labels], axis=1), ("zh", "x", "core"), axis=0, tiled=True
+    )
     row_pack = gather_rows(packed, "col", n_col)
     row_emb, row_width = row_pack[:, :width], row_pack[:, width]
     col_emb, col_width = col_pack[:, :width], col_pack[:, width]
-    col_labels = col_pack[:, width + 1:]
+    col_labels = col_pack[:, width + 1:width + 2] * col_pack[:, width + 2:]
     row_squares = jnp.sum(row_emb * row_emb, axis=1)
     col_squares = jnp.sum(col_emb * col_emb, axis=1)
     block_rows = row_emb.shape[0]

time: 242 us -> 243 us (level)
  no operation moved by 1% of the time
where the time goes in v11:
time: 243 us; the launch traced here: 242 us
  blocking collectives  113 us (47%)
  waiting for transfers between devices  64.7 us (27%)
  local copies, waits for them, and re-layouts  18.4 us (8%)
  between operations  13.6 us (6%)
  starting transfers between devices  13.5 us (6%)
  matrix products  12.8 us (5%)
  other arithmetic  5.55 us (2%)
    all_to_all x3, blocking collectives, scatter_sum(): lax.all_to_all(p.reshape((n, chunk) + p.shape[1:]), axis, 0, 0, tiled=False)  73.9 us
    all_to_all x2, blocking collectives, gather_row_set(): mine = lax.all_to_all(copies, CHIPS, 0, 0, tiled=False)  39.4 us
    all_to_all x1, waiting for transfers between devices, gather_rows(): got = lax.all_to_all(copies, axis, 0, 0, tiled=False)  30.8 us
    all_gather x1, waiting for transfers between devices, local(): lax.all_gather(jnp.concatenate([packed, seed_column, soft_labels], axis=1...  30.3 us
    all_to_all x1, starting transfers between devices, gather_rows(): got = lax.all_to_all(copies, axis, 0, 0, tiled=False)  9.5 us
    dot_general x1, matrix products, local(): jnp.dot(row_emb, col_emb.T, precision=lax.Precision.HIGHEST, preferred_el...  8.03 us
    convert_element_type x1, local copies, waits for them, and re-layouts, local(): col_mask = col_mask.reshape(block_rows, col_rows).astype(jnp.float32)  7.75 us
  transfers between devices with their start and end apart: 4, of which 4 were waited for; matrix products, arithmetic and copies ran while one was open for 6% of the time, Pallas kernels for 0%

profile of v11, /device:TPU:8, one launch (start us, length us, event | category | flops | bytes accessed | tf_op | source)
XLA Modules:
  0.0 241.8 jit_solution(16674549918584235062)
XLA Ops:
  6.5 0.0 all-gather.2.cloned.1.call-start
  6.5 0.7 copy.17
  7.3 0.7 fusion.9
  7.9 0.1 copy.19
  8.0 1.6 concatenate.11
  9.7 0.0 all-gather.2.cloned.1.call-update
  9.7 0.9 pad_maximum_fusion.2
  10.6 1.4 broadcast_in_dim.13
  12.0 0.0 copy-start.3
  12.0 9.5 %all-to-all-start = ((f32[16,32,769]{2,1,0:T(8,128)}), f32[16,32,769]{2,1,0:T(8,128)S(1)}, u32[]{:S(2)}, u32[]{:S(2)}) async-start(f32[16,32,769]{2,1,0:T(8,128)} %broadcast_in_dim.13), calls=%async_computation | async-start | bytes 3670016 | tf_op jit(solution)/shard_map/all_to_all | solution.py:14
  21.5 0.0 copy-done.3
  21.5 0.1 reshape.36
  21.6 0.3 convert_reduce_fusion
  21.9 4.4 %broadcast_in_dim.15 = f32[16,32,32,32]{3,2,1,0:T(8,128)} broadcast(f32[16,32]{1,0:T(8,128)S(1)} %convert_reduce_fusion), dimensions={0,2} | broadcast | bytes 2099200 | tf_op jit(solution)/shard_map/broadcast_in_dim | solution.py:55
  26.3 7.7 %convert_element_type.19 = f32[512,1024]{1,0:T(8,128)} reshape(f32[16,32,32,32]{3,2,1,0:T(8,128)} %broadcast_in_dim.15) | data formatting | bytes 4194304 | tf_op jit(solution)/shard_map/convert_element_type | solution.py:56
  34.0 30.8 %all-to-all-done = f32[16,32,769]{2,1,0:T(8,128)S(1)} async-done(((f32[16,32,769]{2,1,0:T(8,128)}), f32[16,32,769]{2,1,0:T(8,128)S(1)}, u32[]{:S(2)}, u32[]{:S(2)}) %all-to-all-start) | async-done | bytes 1574944 | tf_op jit(solution)/shard_map/all_to_all | solution.py:14
  64.8 0.0 copy-start
  64.8 0.1 slice_reduce_fusion.2
  64.9 0.2 multiply_reduce_fusion.1
  65.1 30.3 %all-gather.2.cloned.1.call-done = f32[1024,1026]{1,0:T(8,128)} async-done(((f32[32,1026]{1,0:T(8,128)}), f32[1024,1026]{1,0:T(8,128)}) %all-gather.2.cloned.1.call-update) | async-done | bytes 4202512 | tf_op jit(solution)/shard_map/all_gather | solution.py:42
  95.4 1.9 slice_reduce_fusion
  97.3 2.2 multiply_reduce_fusion
  99.5 0.0 copy-done
  99.5 0.0 copy-done.1
  99.5 8.0 %fusion.10 = (f32[512]{0:T(512)S(1)}, f32[512,1024]{1,0:T(8,128)S(1)}) fusion(f32[512,1024]{1,0:T(8,128)S(1)} %copy-done.1, f32[1024]{0:T(1024)S(1)} %get-tuple-element.6, f32[512]{0:T(512)S(1)} %slice_reduce_fusion.2, f32[1024,1026]{1,0:T(8,128)} %all-gather.2.cloned.1.call-done, f32[512,769]{1,0:T(8,128)} %bitcast.35, f32[1024]{0:T(1024)S(1)} %multiply_reduce_fusion, ...), kind=kOutput, calls=%fused_computation.31 | convolution fusion | flops 4836032000 | bytes 8927232 | tf_op jit(solution)/shard_map/dot_general | solution.py:57
  107.5 0.1 reshape.38
  107.6 2.7 %fusion.5 = f32[512,256]{1,0:T(8,128)S(1)} fusion(f32[512,1024]{1,0:T(8,128)S(1)} %get-tuple-element.14, f32[1024,1026]{1,0:T(8,128)} %all-gather.2.cloned.1.call-done, f32[1024]{0:T(1024)S(1)} %get-tuple-element.5), kind=kOutput, calls=%fused_computation.7 | convolution fusion | flops 805568512 | bytes 3674112 | tf_op jit(solution)/shard_map/dot_general | solution.py:65
  110.3 0.0 copy-start.2
  110.4 26.8 %all_to_all.30 = f32[16,40,256]{2,1,0:T(8,128)S(1)} all-to-all(f32[16,40,256]{2,1,0:T(8,128)S(1)} %select_maximum_fusion), channel_id=1, replica_groups=mesh['zh'=4,'x'=4,'core'=2,'col'=16] {'col'}, dimensions={0} | all-to-all | bytes 1310720 | tf_op jit(solution)/shard_map/all_to_all | solution.py:29
  137.2 0.0 copy-done.2
  137.2 0.1 fusion.8
  137.4 21.1 %all_to_all.31 = f32[16,32,256]{2,1,0:T(8,128)S(1)} all-to-all(f32[16,32,256]{2,1,0:T(8,128)S(1)} %broadcast_in_dim.16), channel_id=1, replica_groups=mesh['zh'=4,'x'=4,'core'=2,'col'=16] {'zh','x'}, dimensions={0} | all-to-all | bytes 1048576 | tf_op jit(solution)/shard_map/all_to_all | solution.py:20
  158.5 2.1 collective-permute-start
  160.6 1.7 collective-permute-done
  162.3 0.1 select_bitcast_fusion.3
  162.4 0.1 pad_maximum_fusion
  162.4 1.0 fusion.11
  163.5 22.8 %all_to_all.32 = f32[16,32,256]{2,1,0:T(8,128)S(1)} all-to-all(f32[16,32,256]{2,1,0:T(8,128)S(1)} %fusion.11), channel_id=1, replica_groups=mesh['zh'=4,'x'=4,'core'=2,'col'=16] {'col'}, dimensions={0} | all-to-all | bytes 1048576 | tf_op jit(solution)/shard_map/all_to_all | solution.py:29
  186.3 0.1 divide_add_fusion.1
  186.4 18.3 %all_to_all.33 = f32[16,32,256]{2,1,0:T(8,128)S(1)} all-to-all(f32[16,32,256]{2,1,0:T(8,128)S(1)} %broadcast_in_dim.17), channel_id=1, replica_groups=mesh['zh'=4,'x'=4,'core'=2,'col'=16] {'zh','x'}, dimensions={0} | all-to-all | bytes 1048576 | tf_op jit(solution)/shard_map/all_to_all | solution.py:20
  204.7 1.9 collective-permute-start.1
  206.7 1.9 collective-permute-done.1
  208.5 0.1 select_bitcast_fusion.1
  208.7 0.1 pad_maximum_fusion.1
  208.8 0.1 copy.21
  208.8 1.0 fusion.12
  209.9 24.4 %all_to_all.34 = f32[16,32,256]{2,1,0:T(8,128)S(1)} all-to-all(f32[16,32,256]{2,1,0:T(8,128)S(1)} %fusion.12), channel_id=1, replica_groups=mesh['zh'=4,'x'=4,'core'=2,'col'=16] {'col'}, dimensions={0} | all-to-all | bytes 1048576 | tf_op jit(solution)/shard_map/all_to_all | solution.py:29
  234.3 0.7 divide_add_fusion
  (8 shorter events, 0.3 us)
Async XLA Ops:
  6.5 88.9 %all-gather.2.cloned.1.call-start = ((), (), s32[]{:S(2)}) async-start(), calls=%async_computation.6 | async-start | bytes 4866048 | tf_op jit(solution)/shard_map/all_gather | solution.py:42
  12.0 9.5 %copy-start.3 = (s32[16,512]{1,0:T(8,128)S(1)}, s32[16,512]{1,0:T(8,128)}, u32[]{:S(2)}) copy-start(s32[16,512]{1,0:T(8,128)} %param.9) | copy-start | bytes 98308
  12.0 52.8 %all-to-all-start = ((f32[16,32,769]{2,1,0:T(8,128)}), f32[16,32,769]{2,1,0:T(8,128)S(1)}, u32[]{:S(2)}, u32[]{:S(2)}) async-start(f32[16,32,769]{2,1,0:T(8,128)} %broadcast_in_dim.13), calls=%async_computation | async-start | bytes 3670016 | tf_op jit(solution)/shard_map/all_to_all | solution.py:14
  64.8 34.7 %copy-start = (f32[16,32,769]{2,1,0:T(8,128)}, f32[16,32,769]{2,1,0:T(8,128)S(1)}, u32[]{:S(2)}) copy-start(f32[16,32,769]{2,1,0:T(8,128)S(1)} %all-to-all-done) | copy-start | bytes 4724740
  95.4 4.0 %copy-start.1 = (f32[512,1024]{1,0:T(8,128)S(1)}, f32[512,1024]{1,0:T(8,128)}, u32[]{:S(2)}) copy-start(f32[512,1024]{1,0:T(8,128)} %convert_element_type.19) | copy-start | bytes 6291460
  110.3 26.9 %copy-start.2 = (f32[32,256]{1,0:T(8,128)S(1)}, f32[32,256]{1,0:T(8,128)}, u32[]{:S(2)}) copy-start(f32[32,256]{1,0:T(8,128)} %param.7) | copy-start | bytes 98308
  158.5 3.8 %collective-permute-start = (f32[16,32,256]{2,1,0:T(8,128)S(1)}, f32[16,32,256]{2,1,0:T(8,128)S(1)}, u32[]{:S(2)}, u32[]{:S(2)}) collective-permute-start(f32[16,32,256]{2,1,0:T(8,128)S(1)} %all_to_all.31), channel_id=1, source_target_pairs={{0,16},{16,0},{1,17},{17,1},{2,18},{18,2},{3,19},{19,3},{4,20},{20... | collective-permute-start | bytes 1572872 | tf_op jit(solution)/shard_map/ppermute | solution.py:21
  204.7 3.8 %collective-permute-start.1 = (f32[16,32,256]{2,1,0:T(8,128)S(1)}, f32[16,32,256]{2,1,0:T(8,128)S(1)}, u32[]{:S(2)}, u32[]{:S(2)}) collective-permute-start(f32[16,32,256]{2,1,0:T(8,128)S(1)} %all_to_all.33), channel_id=1, source_target_pairs={{0,16},{16,0},{1,17},{17,1},{2,18},{18,2},{3,19},{19,3},{4,20},{20... | collective-permute-start | bytes 1572872 | tf_op jit(solution)/shard_map/ppermute | solution.py:21
Sparse Core Ops, SparseCore 0:
  10.5 84.9 all-gather.1

commit v12 on v10

--- a/solution.py
+++ b/solution.py
@@ -38,13 +38,14 @@
     n_labels = soft_labels.shape[1]
     seeded = seed_mask.astype(jnp.float32)[:, None] * soft_labels
     packed = jnp.concatenate([embeddings, sharpness[:, None]], axis=1)
-    col_pack = lax.all_gather(jnp.concatenate([packed, seeded], axis=1), ("zh", "x", "core"), axis=0, tiled=True)
+    col_pack = lax.all_gather(jnp.concatenate([embeddings, seeded], axis=1), ("zh", "x", "core"), axis=0, tiled=True)
     row_pack = gather_rows(packed, "col", n_col)
+    squares = jnp.sum(embeddings * embeddings, axis=1)
+    col_scalars = gather_row_set(jnp.stack([sharpness, squares], axis=1), n_chips)
     row_emb, row_width = row_pack[:, :width], row_pack[:, width]
-    col_emb, col_width = col_pack[:, :width], col_pack[:, width]
-    col_labels = col_pack[:, width + 1:]
+    col_emb, col_labels = col_pack[:, :width], col_pack[:, width:]
+    col_width, col_squares = col_scalars[:, 0], col_scalars[:, 1]
     row_squares = jnp.sum(row_emb * row_emb, axis=1)
-    col_squares = jnp.sum(col_emb * col_emb, axis=1)
     block_rows = row_emb.shape[0]
     col_rows = col_emb.shape[0]
     grouped = tile_mask.reshape(n_col, 2 * n_chips, n_col)

time: 242 us -> 238 us (0.983)
  waiting for transfers between devices: 63.6 us -> 46.8 us
  starting transfers between devices: 13.5 us -> 27.2 us
    all_gather x1, waiting for transfers between devices: 29.3 us -> 7.78 us  [local(): lax.all_gather(jnp.concatenate([embeddings, seeded], axis=1), ('zh', 'x',...]
    all_to_all x0 -> x1, starting transfers between devices: none -> 12.9 us  [gather_row_set(): mine = lax.all_to_all(copies, CHIPS, 0, 0, tiled=False)]
    all_to_all x0 -> x1, waiting for transfers between devices: none -> 8.37 us  [gather_row_set(): mine = lax.all_to_all(copies, CHIPS, 0, 0, tiled=False)]
    all_to_all x1, waiting for transfers between devices: 30.8 us -> 26.8 us  [gather_rows(): got = lax.all_to_all(copies, axis, 0, 0, tiled=False)]
    ppermute x2 -> x3, starting transfers between devices: 4 us -> 5.73 us  [gather_row_set(): other = lax.ppermute(mine, 'core', [(0, 1), (1, 0)])]
  transfers between devices with their start and end apart: 4 -> 6, of which waited for: 4 -> 5; matrix products, arithmetic and copies ran while one was open for 6% -> 8% of each run, Pallas kernels for 0% -> 0%
where the time goes in v12:
time: 238 us; the launch traced here: 237 us
  blocking collectives  112 us (47%)
  waiting for transfers between devices  46.8 us (20%)
  starting transfers between devices  27.2 us (11%)
  local copies, waits for them, and re-layouts  15.5 us (7%)
  matrix products  14.4 us (6%)
  between operations  13.6 us (6%)
  other arithmetic  7.48 us (3%)
    all_to_all x3, blocking collectives, scatter_sum(): lax.all_to_all(p.reshape((n, chunk) + p.shape[1:]), axis, 0, 0, tiled=False)  72.4 us
    all_to_all x2, blocking collectives, gather_row_set(): mine = lax.all_to_all(copies, CHIPS, 0, 0, tiled=False)  39.6 us
    all_to_all x1, waiting for transfers between devices, gather_rows(): got = lax.all_to_all(copies, axis, 0, 0, tiled=False)  26.8 us
    all_to_all x1, starting transfers between devices, gather_row_set(): mine = lax.all_to_all(copies, CHIPS, 0, 0, tiled=False)  12.9 us
    dot_general x1, matrix products, local(): jnp.dot(row_emb, col_emb.T, precision=lax.Precision.HIGHEST, preferred_el...  10.1 us
    all_to_all x1, starting transfers between devices, gather_rows(): got = lax.all_to_all(copies, axis, 0, 0, tiled=False)  8.59 us
    all_to_all x1, waiting for transfers between devices, gather_row_set(): mine = lax.all_to_all(copies, CHIPS, 0, 0, tiled=False)  8.37 us
    all_gather x1, waiting for transfers between devices, local(): lax.all_gather(jnp.concatenate([embeddings, seeded], axis=1), ('zh', 'x',...  7.78 us
  transfers between devices with their start and end apart: 6, of which 5 were waited for; matrix products, arithmetic and copies ran while one was open for 8% of the time, Pallas kernels for 0%

profile of v12, /device:TPU:8, one launch (start us, length us, event | category | flops | bytes accessed | tf_op | source)
XLA Modules:
  0.0 236.9 jit_solution(2193267434082115020)
XLA Ops:
  6.5 0.0 all-gather.2.cloned.1.call-start
  6.5 0.7 convert_element_type.15
  7.2 0.8 broadcast_multiply_fusion
  8.0 1.5 pad_maximum_fusion.2
  9.6 0.0 all-gather.2.cloned.1.call-update
  9.6 1.0 multiply_reduce_fusion.1
  10.6 0.7 pad_maximum_fusion.5
  11.3 0.6 broadcast_in_dim.14
  11.9 12.9 %all-to-all-start.1 = ((f32[16,32,2]{1,2,0:T(2,128)}), f32[16,32,2]{1,2,0:T(2,128)S(1)}, u32[]{:S(2)}, u32[]{:S(2)}) async-start(f32[16,32,2]{1,2,0:T(2,128)} %broadcast_in_dim.14), calls=%async_computation.1 | async-start | bytes 32768 | tf_op jit(solution)/shard_map/all_to_all | solution.py:20
  24.8 0.7 copy.19
  25.5 0.9 pad_maximum_fusion.3
  26.4 8.4 %all-to-all-done.1 = f32[16,32,2]{1,2,0:T(2,128)S(1)} async-done(((f32[16,32,2]{1,2,0:T(2,128)}), f32[16,32,2]{1,2,0:T(2,128)S(1)}, u32[]{:S(2)}, u32[]{:S(2)}) %all-to-all-start.1) | async-done | bytes 4128 | tf_op jit(solution)/shard_map/all_to_all | solution.py:20
  34.8 1.4 broadcast_in_dim.13
  36.2 8.6 %all-to-all-start = ((f32[16,32,769]{2,1,0:T(8,128)}), f32[16,32,769]{2,1,0:T(8,128)S(1)}, u32[]{:S(2)}, u32[]{:S(2)}) async-start(f32[16,32,769]{2,1,0:T(8,128)} %broadcast_in_dim.13), calls=%async_computation | async-start | bytes 3670016 | tf_op jit(solution)/shard_map/all_to_all | solution.py:14
  44.8 1.9 collective-permute-start
  46.7 0.1 reshape.41
  46.9 0.3 convert_reduce_fusion
  47.1 4.4 %broadcast_in_dim.15 = f32[16,32,32,32]{3,2,1,0:T(8,128)} broadcast(f32[16,32]{1,0:T(8,128)S(1)} %convert_reduce_fusion), dimensions={0,2} | broadcast | bytes 2099200 | tf_op jit(solution)/shard_map/broadcast_in_dim | solution.py:53
  51.5 7.7 %convert_element_type.18 = f32[512,1024]{1,0:T(8,128)} reshape(f32[16,32,32,32]{3,2,1,0:T(8,128)} %broadcast_in_dim.15) | data formatting | bytes 4194304 | tf_op jit(solution)/shard_map/convert_element_type | solution.py:54
  59.2 0.0 collective-permute-done
  59.3 0.1 reshape.40
  59.4 26.8 %all-to-all-done = f32[16,32,769]{2,1,0:T(8,128)S(1)} async-done(((f32[16,32,769]{2,1,0:T(8,128)}), f32[16,32,769]{2,1,0:T(8,128)S(1)}, u32[]{:S(2)}, u32[]{:S(2)}) %all-to-all-start) | async-done | bytes 1574944 | tf_op jit(solution)/shard_map/all_to_all | solution.py:14
  86.2 0.1 slice_reduce_fusion
  86.4 0.2 multiply_reduce_fusion
  86.5 7.8 %all-gather.2.cloned.1.call-done = f32[1024,1024]{1,0:T(8,128)} async-done(((f32[32,1024]{1,0:T(8,128)}), f32[1024,1024]{1,0:T(8,128)}) %all-gather.2.cloned.1.call-update) | async-done | bytes 4194320 | tf_op jit(solution)/shard_map/all_gather | solution.py:41
  94.3 10.1 %fusion.10 = (f32[512]{0:T(512)S(1)}, f32[512,1024]{1,0:T(8,128)S(1)}) fusion(f32[512,1024]{1,0:T(8,128)} %convert_element_type.18, f32[1024]{0:T(1024)S(1)} %bitcast.47, f32[512]{0:T(512)S(1)} %slice_reduce_fusion, f32[1024,1024]{1,0:T(8,128)} %all-gather.2.cloned.1.call-done, f32[512,769]{1,0:T(8,128)} %bitcast.42, f32[1024]{0:T(1024)S(1)} %bitcast.46, ...), kind=kOutput, calls=%fused_computation.32 | convolution fusion | flops 4836032000 | bytes 8927232 | tf_op jit(solution)/shard_map/dot_general | solution.py:55
  104.4 0.1 reshape.43
  104.5 2.2 fusion.5
  106.7 0.0 copy-start.1
  106.8 25.3 %all_to_all.35 = f32[16,40,256]{2,1,0:T(8,128)S(1)} all-to-all(f32[16,40,256]{2,1,0:T(8,128)S(1)} %select_maximum_fusion), channel_id=1, replica_groups=mesh['zh'=4,'x'=4,'core'=2,'col'=16] {'col'}, dimensions={0} | all-to-all | bytes 1310720 | tf_op jit(solution)/shard_map/all_to_all | solution.py:29
  132.1 0.1 fusion.8
  132.3 21.3 %all_to_all.36 = f32[16,32,256]{2,1,0:T(8,128)S(1)} all-to-all(f32[16,32,256]{2,1,0:T(8,128)S(1)} %broadcast_in_dim.16), channel_id=1, replica_groups=mesh['zh'=4,'x'=4,'core'=2,'col'=16] {'zh','x'}, dimensions={0} | all-to-all | bytes 1048576 | tf_op jit(solution)/shard_map/all_to_all | solution.py:20
  153.6 1.9 collective-permute-start.1
  155.5 1.9 collective-permute-done.1
  157.3 0.1 select_bitcast_fusion.3
  157.5 0.1 pad_maximum_fusion
  157.5 1.0 fusion.11
  158.6 22.8 %all_to_all.37 = f32[16,32,256]{2,1,0:T(8,128)S(1)} all-to-all(f32[16,32,256]{2,1,0:T(8,128)S(1)} %fusion.11), channel_id=1, replica_groups=mesh['zh'=4,'x'=4,'core'=2,'col'=16] {'col'}, dimensions={0} | all-to-all | bytes 1048576 | tf_op jit(solution)/shard_map/all_to_all | solution.py:29
  181.4 0.1 divide_add_fusion.1
  181.5 18.3 %all_to_all.38 = f32[16,32,256]{2,1,0:T(8,128)S(1)} all-to-all(f32[16,32,256]{2,1,0:T(8,128)S(1)} %broadcast_in_dim.17), channel_id=1, replica_groups=mesh['zh'=4,'x'=4,'core'=2,'col'=16] {'zh','x'}, dimensions={0} | all-to-all | bytes 1048576 | tf_op jit(solution)/shard_map/all_to_all | solution.py:20
  199.8 1.9 collective-permute-start.2
  201.8 1.9 collective-permute-done.2
  203.6 0.1 select_bitcast_fusion.1
  203.8 0.1 pad_maximum_fusion.1
  203.9 0.1 copy.22
  203.9 1.0 fusion.12
  205.0 24.4 %all_to_all.39 = f32[16,32,256]{2,1,0:T(8,128)S(1)} all-to-all(f32[16,32,256]{2,1,0:T(8,128)S(1)} %fusion.12), channel_id=1, replica_groups=mesh['zh'=4,'x'=4,'core'=2,'col'=16] {'col'}, dimensions={0} | all-to-all | bytes 1048576 | tf_op jit(solution)/shard_map/all_to_all | solution.py:29
  229.4 0.7 divide_add_fusion
  (16 shorter events, 0.3 us)
Async XLA Ops:
  6.5 87.8 %all-gather.2.cloned.1.call-start = ((), (), s32[]{:S(2)}) async-start(), calls=%async_computation.7 | async-start | bytes 4325376 | tf_op jit(solution)/shard_map/all_gather | solution.py:41
  11.9 22.9 %all-to-all-start.1 = ((f32[16,32,2]{1,2,0:T(2,128)}), f32[16,32,2]{1,2,0:T(2,128)S(1)}, u32[]{:S(2)}, u32[]{:S(2)}) async-start(f32[16,32,2]{1,2,0:T(2,128)} %broadcast_in_dim.14), calls=%async_computation.1 | async-start | bytes 32768 | tf_op jit(solution)/shard_map/all_to_all | solution.py:20
  36.2 10.5 %copy-start.2 = (s32[16,512]{1,0:T(8,128)S(1)}, s32[16,512]{1,0:T(8,128)}, u32[]{:S(2)}) copy-start(s32[16,512]{1,0:T(8,128)} %param.9) | copy-start | bytes 98308
  36.2 50.0 %all-to-all-start = ((f32[16,32,769]{2,1,0:T(8,128)}), f32[16,32,769]{2,1,0:T(8,128)S(1)}, u32[]{:S(2)}, u32[]{:S(2)}) async-start(f32[16,32,769]{2,1,0:T(8,128)} %broadcast_in_dim.13), calls=%async_computation | async-start | bytes 3670016 | tf_op jit(solution)/shard_map/all_to_all | solution.py:14
  44.8 14.4 %collective-permute-start = (f32[16,32,2]{1,2,0:T(2,128)S(1)}, f32[16,32,2]{1,2,0:T(2,128)S(1)}, u32[]{:S(2)}, u32[]{:S(2)}) collective-permute-start(f32[16,32,2]{1,2,0:T(2,128)S(1)} %all-to-all-done.1), channel_id=1, source_target_pairs={{0,16},{16,0},{1,17},{17,1},{2,18},{18,2},{3,19},{19,3},{4,20},{20... | collective-permute-start | bytes 12296 | tf_op jit(solution)/shard_map/ppermute | solution.py:21
  86.2 8.1 %copy-start = (f32[16,32,769]{2,1,0:T(8,128)}, f32[16,32,769]{2,1,0:T(8,128)S(1)}, u32[]{:S(2)}) copy-start(f32[16,32,769]{2,1,0:T(8,128)S(1)} %all-to-all-done) | copy-start | bytes 4724740
  106.7 25.4 %copy-start.1 = (f32[32,256]{1,0:T(8,128)S(1)}, f32[32,256]{1,0:T(8,128)}, u32[]{:S(2)}) copy-start(f32[32,256]{1,0:T(8,128)} %param.7) | copy-start | bytes 98308
  153.6 3.8 %collective-permute-start.1 = (f32[16,32,256]{2,1,0:T(8,128)S(1)}, f32[16,32,256]{2,1,0:T(8,128)S(1)}, u32[]{:S(2)}, u32[]{:S(2)}) collective-permute-start(f32[16,32,256]{2,1,0:T(8,128)S(1)} %all_to_all.36), channel_id=1, source_target_pairs={{0,16},{16,0},{1,17},{17,1},{2,18},{18,2},{3,19},{19,3},{4,20},{20... | collective-permute-start | bytes 1572872 | tf_op jit(solution)/shard_map/ppermute | solution.py:21
  199.8 3.8 %collective-permute-start.2 = (f32[16,32,256]{2,1,0:T(8,128)S(1)}, f32[16,32,256]{2,1,0:T(8,128)S(1)}, u32[]{:S(2)}, u32[]{:S(2)}) collective-permute-start(f32[16,32,256]{2,1,0:T(8,128)S(1)} %all_to_all.38), channel_id=1, source_target_pairs={{0,16},{16,0},{1,17},{17,1},{2,18},{18,2},{3,19},{19,3},{4,20},{20... | collective-permute-start | bytes 1572872 | tf_op jit(solution)/shard_map/ppermute | solution.py:21
Sparse Core Ops, SparseCore 0:
  10.5 83.8 all-gather.1

commit v13 on v12

--- a/solution.py
+++ b/solution.py
@@ -38,13 +38,16 @@
     n_labels = soft_labels.shape[1]
     seeded = seed_mask.astype(jnp.float32)[:, None] * soft_labels
     packed = jnp.concatenate([embeddings, sharpness[:, None]], axis=1)
-    col_pack = lax.all_gather(jnp.concatenate([embeddings, seeded], axis=1), ("zh", "x", "core"), axis=0, tiled=True)
+    col_pack = lax.all_gather(jnp.concatenate([embeddings, soft_labels], axis=1), ("zh", "x", "core"), axis=0, tiled=True)
     row_pack = gather_rows(packed, "col", n_col)
     squares = jnp.sum(embeddings * embeddings, axis=1)
-    col_scalars = gather_row_set(jnp.stack([sharpness, squares], axis=1), n_chips)
+    col_scalars = gather_row_set(
+        jnp.stack([sharpness, squares, seed_mask.astype(jnp.float32)], axis=1), n_chips
+    )
     row_emb, row_width = row_pack[:, :width], row_pack[:, width]
-    col_emb, col_labels = col_pack[:, :width], col_pack[:, width:]
+    col_emb = col_pack[:, :width]
     col_width, col_squares = col_scalars[:, 0], col_scalars[:, 1]
+    col_labels = col_scalars[:, 2:3] * col_pack[:, width:]
     row_squares = jnp.sum(row_emb * row_emb, axis=1)
     block_rows = row_emb.shape[0]
     col_rows = col_emb.shape[0]

time: 238 us -> 239 us (level)
  no operation moved by 1% of the time
where the time goes in v13:
time: 239 us; the launch traced here: 238 us
  blocking collectives  113 us (47%)
  waiting for transfers between devices  47.3 us (20%)
  starting transfers between devices  27.2 us (11%)
  local copies, waits for them, and re-layouts  15.5 us (6%)
  matrix products  14.5 us (6%)
  between operations  13.6 us (6%)
  other arithmetic  6.68 us (3%)
    all_to_all x3, blocking collectives, scatter_sum(): lax.all_to_all(p.reshape((n, chunk) + p.shape[1:]), axis, 0, 0, tiled=False)  74.4 us
    all_to_all x2, blocking collectives, gather_row_set(): mine = lax.all_to_all(copies, CHIPS, 0, 0, tiled=False)  38.7 us
    all_to_all x1, waiting for transfers between devices, gather_rows(): got = lax.all_to_all(copies, axis, 0, 0, tiled=False)  26.9 us
    all_to_all x1, starting transfers between devices, gather_row_set(): mine = lax.all_to_all(copies, CHIPS, 0, 0, tiled=False)  12.9 us
    dot_general x1, matrix products, local(): jnp.dot(row_emb, col_emb.T, precision=lax.Precision.HIGHEST, preferred_el...  10.1 us
    all_to_all x1, starting transfers between devices, gather_rows(): got = lax.all_to_all(copies, axis, 0, 0, tiled=False)  8.57 us
    all_to_all x1, waiting for transfers between devices, gather_row_set(): mine = lax.all_to_all(copies, CHIPS, 0, 0, tiled=False)  8.39 us
    all_gather x1, waiting for transfers between devices, local(): lax.all_gather(jnp.concatenate([embeddings, soft_labels], axis=1), ('zh',...  8.29 us
  transfers between devices with their start and end apart: 6, of which 5 were waited for; matrix products, arithmetic and copies ran while one was open for 8% of the time, Pallas kernels for 0%

profile of v13, /device:TPU:8, one launch (start us, length us, event | category | flops | bytes accessed | tf_op | source)
XLA Modules:
  0.0 237.9 jit_solution(12330984435800314041)
XLA Ops:
  6.5 0.0 all-gather.2.cloned.1.call-start
  6.5 1.6 pad_maximum_fusion.2
  8.1 0.0 all-gather.2.cloned.1.call-update
  8.1 1.0 multiply_reduce_fusion.1
  9.1 0.7 fusion.10
  9.8 0.7 pad_maximum_fusion.5
  10.5 0.6 broadcast_in_dim.14
  11.1 12.9 %all-to-all-start.1 = ((f32[16,32,3]{1,2,0:T(4,128)}), f32[16,32,3]{1,2,0:T(4,128)S(1)}, u32[]{:S(2)}, u32[]{:S(2)}) async-start(f32[16,32,3]{1,2,0:T(4,128)} %broadcast_in_dim.14), calls=%async_computation.1 | async-start | bytes 65536 | tf_op jit(solution)/shard_map/all_to_all | solution.py:20
  24.0 0.7 copy.19
  24.7 0.9 pad_maximum_fusion.3
  25.6 8.4 %all-to-all-done.1 = f32[16,32,3]{1,2,0:T(4,128)S(1)} async-done(((f32[16,32,3]{1,2,0:T(4,128)}), f32[16,32,3]{1,2,0:T(4,128)S(1)}, u32[]{:S(2)}, u32[]{:S(2)}) %all-to-all-start.1) | async-done | bytes 6176 | tf_op jit(solution)/shard_map/all_to_all | solution.py:20
  34.0 1.4 broadcast_in_dim.13
  35.4 8.6 %all-to-all-start = ((f32[16,32,769]{2,1,0:T(8,128)}), f32[16,32,769]{2,1,0:T(8,128)S(1)}, u32[]{:S(2)}, u32[]{:S(2)}) async-start(f32[16,32,769]{2,1,0:T(8,128)} %broadcast_in_dim.13), calls=%async_computation | async-start | bytes 3670016 | tf_op jit(solution)/shard_map/all_to_all | solution.py:14
  44.0 1.9 collective-permute-start
  45.9 0.0 copy-done.2
  45.9 0.1 reshape.41
  46.1 0.3 convert_reduce_fusion
  46.3 4.4 %broadcast_in_dim.15 = f32[16,32,32,32]{3,2,1,0:T(8,128)} broadcast(f32[16,32]{1,0:T(8,128)S(1)} %convert_reduce_fusion), dimensions={0,2} | broadcast | bytes 2099200 | tf_op jit(solution)/shard_map/broadcast_in_dim | solution.py:56
  50.7 7.7 %convert_element_type.19 = f32[512,1024]{1,0:T(8,128)} reshape(f32[16,32,32,32]{3,2,1,0:T(8,128)} %broadcast_in_dim.15) | data formatting | bytes 4194304 | tf_op jit(solution)/shard_map/convert_element_type | solution.py:57
  58.4 0.0 collective-permute-done
  58.5 0.1 reshape.40
  58.6 26.9 %all-to-all-done = f32[16,32,769]{2,1,0:T(8,128)S(1)} async-done(((f32[16,32,769]{2,1,0:T(8,128)}), f32[16,32,769]{2,1,0:T(8,128)S(1)}, u32[]{:S(2)}, u32[]{:S(2)}) %all-to-all-start) | async-done | bytes 1574944 | tf_op jit(solution)/shard_map/all_to_all | solution.py:14
  85.5 0.1 slice_reduce_fusion
  85.6 0.2 multiply_reduce_fusion
  85.8 8.3 %all-gather.2.cloned.1.call-done = f32[1024,1024]{1,0:T(8,128)} async-done(((f32[32,1024]{1,0:T(8,128)}), f32[1024,1024]{1,0:T(8,128)}) %all-gather.2.cloned.1.call-update) | async-done | bytes 4194320 | tf_op jit(solution)/shard_map/all_gather | solution.py:41
  94.1 10.1 %fusion.11 = (f32[512]{0:T(512)S(1)}, f32[512,1024]{1,0:T(8,128)S(1)}) fusion(f32[512,1024]{1,0:T(8,128)} %convert_element_type.19, f32[1024]{0:T(1024)S(1)} %bitcast.49, f32[512]{0:T(512)S(1)} %slice_reduce_fusion, f32[1024,1024]{1,0:T(8,128)} %all-gather.2.cloned.1.call-done, f32[512,769]{1,0:T(8,128)} %bitcast.45, f32[1024]{0:T(1024)S(1)} %bitcast.50, ...), kind=kOutput, calls=%fused_computation.35 | convolution fusion | flops 4836032000 | bytes 8927232 | tf_op jit(solution)/shard_map/dot_general | solution.py:58
  104.2 0.1 reshape.43
  104.3 2.3 fusion.5
  106.6 0.0 copy-start.1
  106.7 27.3 %all_to_all.35 = f32[16,40,256]{2,1,0:T(8,128)S(1)} all-to-all(f32[16,40,256]{2,1,0:T(8,128)S(1)} %select_maximum_fusion), channel_id=1, replica_groups=mesh['zh'=4,'x'=4,'core'=2,'col'=16] {'col'}, dimensions={0} | all-to-all | bytes 1310720 | tf_op jit(solution)/shard_map/all_to_all | solution.py:29
  134.0 0.1 fusion.8
  134.2 20.4 %all_to_all.36 = f32[16,32,256]{2,1,0:T(8,128)S(1)} all-to-all(f32[16,32,256]{2,1,0:T(8,128)S(1)} %broadcast_in_dim.16), channel_id=1, replica_groups=mesh['zh'=4,'x'=4,'core'=2,'col'=16] {'zh','x'}, dimensions={0} | all-to-all | bytes 1048576 | tf_op jit(solution)/shard_map/all_to_all | solution.py:20
  154.6 1.9 collective-permute-start.1
  156.5 1.9 collective-permute-done.1
  158.4 0.1 select_bitcast_fusion.3
  158.5 0.1 pad_maximum_fusion
  158.5 1.0 fusion.12
  159.6 22.8 %all_to_all.37 = f32[16,32,256]{2,1,0:T(8,128)S(1)} all-to-all(f32[16,32,256]{2,1,0:T(8,128)S(1)} %fusion.12), channel_id=1, replica_groups=mesh['zh'=4,'x'=4,'core'=2,'col'=16] {'col'}, dimensions={0} | all-to-all | bytes 1048576 | tf_op jit(solution)/shard_map/all_to_all | solution.py:29
  182.4 0.1 divide_add_fusion.1
  182.5 18.4 %all_to_all.38 = f32[16,32,256]{2,1,0:T(8,128)S(1)} all-to-all(f32[16,32,256]{2,1,0:T(8,128)S(1)} %broadcast_in_dim.17), channel_id=1, replica_groups=mesh['zh'=4,'x'=4,'core'=2,'col'=16] {'zh','x'}, dimensions={0} | all-to-all | bytes 1048576 | tf_op jit(solution)/shard_map/all_to_all | solution.py:20
  200.9 1.9 collective-permute-start.2
  202.8 1.9 collective-permute-done.2
  204.7 0.1 select_bitcast_fusion.1
  204.8 0.1 pad_maximum_fusion.1
  204.9 0.1 copy.22
  205.0 1.0 fusion.13
  206.0 24.3 %all_to_all.39 = f32[16,32,256]{2,1,0:T(8,128)S(1)} all-to-all(f32[16,32,256]{2,1,0:T(8,128)S(1)} %fusion.13), channel_id=1, replica_groups=mesh['zh'=4,'x'=4,'core'=2,'col'=16] {'col'}, dimensions={0} | all-to-all | bytes 1048576 | tf_op jit(solution)/shard_map/all_to_all | solution.py:29
  230.4 0.7 divide_add_fusion
  (15 shorter events, 0.3 us)
Async XLA Ops:
  6.5 87.6 %all-gather.2.cloned.1.call-start = ((), (), s32[]{:S(2)}) async-start(), calls=%async_computation.7 | async-start | bytes 4325376 | tf_op jit(solution)/shard_map/all_gather | solution.py:41
  11.1 22.9 %all-to-all-start.1 = ((f32[16,32,3]{1,2,0:T(4,128)}), f32[16,32,3]{1,2,0:T(4,128)S(1)}, u32[]{:S(2)}, u32[]{:S(2)}) async-start(f32[16,32,3]{1,2,0:T(4,128)} %broadcast_in_dim.14), calls=%async_computation.1 | async-start | bytes 65536 | tf_op jit(solution)/shard_map/all_to_all | solution.py:20
  35.4 10.5 %copy-start.2 = (s32[16,512]{1,0:T(8,128)S(1)}, s32[16,512]{1,0:T(8,128)}, u32[]{:S(2)}) copy-start(s32[16,512]{1,0:T(8,128)} %param.9) | copy-start | bytes 98308
  35.4 50.1 %all-to-all-start = ((f32[16,32,769]{2,1,0:T(8,128)}), f32[16,32,769]{2,1,0:T(8,128)S(1)}, u32[]{:S(2)}, u32[]{:S(2)}) async-start(f32[16,32,769]{2,1,0:T(8,128)} %broadcast_in_dim.13), calls=%async_computation | async-start | bytes 3670016 | tf_op jit(solution)/shard_map/all_to_all | solution.py:14
  44.0 14.4 %collective-permute-start = (f32[16,32,3]{1,2,0:T(4,128)S(1)}, f32[16,32,3]{1,2,0:T(4,128)S(1)}, u32[]{:S(2)}, u32[]{:S(2)}) collective-permute-start(f32[16,32,3]{1,2,0:T(4,128)S(1)} %all-to-all-done.1), channel_id=1, source_target_pairs={{0,16},{16,0},{1,17},{17,1},{2,18},{18,2},{3,19},{19,3},{4,20},{20... | collective-permute-start | bytes 18440 | tf_op jit(solution)/shard_map/ppermute | solution.py:21
  85.5 8.6 %copy-start = (f32[16,32,769]{2,1,0:T(8,128)}, f32[16,32,769]{2,1,0:T(8,128)S(1)}, u32[]{:S(2)}) copy-start(f32[16,32,769]{2,1,0:T(8,128)S(1)} %all-to-all-done) | copy-start | bytes 4724740
  106.6 27.4 %copy-start.1 = (f32[32,256]{1,0:T(8,128)S(1)}, f32[32,256]{1,0:T(8,128)}, u32[]{:S(2)}) copy-start(f32[32,256]{1,0:T(8,128)} %param.7) | copy-start | bytes 98308
  154.6 3.8 %collective-permute-start.1 = (f32[16,32,256]{2,1,0:T(8,128)S(1)}, f32[16,32,256]{2,1,0:T(8,128)S(1)}, u32[]{:S(2)}, u32[]{:S(2)}) collective-permute-start(f32[16,32,256]{2,1,0:T(8,128)S(1)} %all_to_all.36), channel_id=1, source_target_pairs={{0,16},{16,0},{1,17},{17,1},{2,18},{18,2},{3,19},{19,3},{4,20},{20... | collective-permute-start | bytes 1572872 | tf_op jit(solution)/shard_map/ppermute | solution.py:21
  200.9 3.8 %collective-permute-start.2 = (f32[16,32,256]{2,1,0:T(8,128)S(1)}, f32[16,32,256]{2,1,0:T(8,128)S(1)}, u32[]{:S(2)}, u32[]{:S(2)}) collective-permute-start(f32[16,32,256]{2,1,0:T(8,128)S(1)} %all_to_all.38), channel_id=1, source_target_pairs={{0,16},{16,0},{1,17},{17,1},{2,18},{18,2},{3,19},{19,3},{4,20},{20... | collective-permute-start | bytes 1572872 | tf_op jit(solution)/shard_map/ppermute | solution.py:21
Sparse Core Ops, SparseCore 0:
  10.5 83.5 all-gather.1
